TPU v7x, 32 devices: a whole 2x2x4 slice. The times are simulated.
32 devices in a mesh: grp: 2 (over y), cell: 8 (over z, x), gene: 2 (over core).
Axes of the slice: x: 2, y: 2, z: 4, core: 2. Of those that a mesh axis runs over, the one named last changes fastest.
Arguments:
- expression: bfloat16 [2048, 16384], P(('grp', 'cell'), 'gene'), parts along dimension 0, may hold values from -6 to 6
- design: bfloat16 [2048, 128], P(('grp', 'cell')), parts along dimension 0, may hold values from -24 to 24
- quantile_level: float32 [16384], P('gene'), may hold values from 0.1 to 0.9
Outputs:
- quantile_slack: bfloat16 [2048, 16384], P(('grp', 'cell'), 'gene'), parts along dimension 0
- low_rank_coef: float32 [32768, 128], P(('grp', 'gene', 'cell')), parts along dimension 0
There are 2 independent parts, one for each index of `grp`. A program takes and returns all parts, laid end to end along the dimension named above; an argument that names none is the same for every part. Nothing has to cross between parts.
All inputs are finite; a program needn't handle non-finite values.
Results may differ from a plain program's by a relative error of at most 0.0025.
The roundings to bfloat16 on the way count: a program that leaves them out, or rounds other values in their place, can miss the bound.
Values may be sent and summed in bfloat16 or wider, within the bound.
No kernel may reach another device: no remote copies, remote signals or barrier semaphores. Data moves between devices by JAX's collectives and lax.ppermute only.
A program may use at most 64 MiB of HBM per device.

v0:
```python
import math

import jax
import jax.numpy as jnp
from jax import lax
from jax.sharding import PartitionSpec as P

NS_STEPS = 8


shrink_rate = 0.25


def matmul(left, right):
    return jnp.dot(left, right, precision=lax.Precision.HIGHEST)


def invert(matrix):
    identity = jnp.eye(matrix.shape[0], dtype=jnp.float32)
    factor = jnp.linalg.cholesky(matrix)
    lower_inv = lax.linalg.triangular_solve(factor, identity, left_side=True, lower=True)
    return matmul(lower_inv.T, lower_inv)


def newton(moment):
    identity = jnp.eye(moment.shape[0], dtype=jnp.float32)
    current = moment / jnp.trace(moment)
    root_inv = identity
    for sweep in range(NS_STEPS):
        middle = 1.5 * identity - 0.5 * matmul(root_inv, current)
        current = matmul(current, middle)
        root_inv = matmul(middle, root_inv)
    return root_inv


def per_device(expression, design, quantile_level):
    width = design.shape[1]
    identity = jnp.eye(width, dtype=jnp.float32)
    local_gram = lax.dot_general(
        design, design, (((0,), (0,)), ((), ())), preferred_element_type=jnp.float32
    )
    crossed = lax.psum_scatter(
        lax.dot_general(
            expression, design, (((0,), (0,)), ((), ())), preferred_element_type=jnp.float32
        ),
        "cell",
        scatter_dimension=0,
        tiled=True,
    )
    gram_total = lax.psum(local_gram, "cell")
    inverse = invert(gram_total + identity)
    coef = matmul(crossed, inverse)
    local_moment = lax.dot_general(
        coef, coef, (((0,), (0,)), ((), ())), precision=lax.Precision.HIGHEST
    )
    moment = lax.psum(local_moment, ("cell", "gene"))
    root_inv = newton(moment)
    low_rank_coef = coef - shrink_rate / math.sqrt(width) * matmul(coef, root_inv)
    coef_low = coef.astype(jnp.bfloat16)
    fitted = lax.dot_general(
        design,
        lax.all_gather(coef_low, "cell", axis=0, tiled=True),
        (((1,), (1,)), ((), ())),
        preferred_element_type=jnp.float32,
    )
    slack = expression.astype(jnp.float32) - fitted
    level = quantile_level[None, :]
    quantile_slack = (slack - jnp.clip(slack, level - 1.0, level)).astype(jnp.bfloat16)
    return (quantile_slack, low_rank_coef)


def solution(mesh):
    placed = (P(("grp", "cell"), "gene"), P(("grp", "cell"), None), P("gene"))
    return jax.shard_map(
        per_device,
        mesh=mesh,
        in_specs=placed,
        out_specs=(P(("grp", "cell"), "gene"), P(("grp", "gene", "cell"), None)),
        check_vma=False,
    )
```

profile of v0, /device:TPU:0, one launch (start us, length us, event | category | flops | bytes accessed | tf_op | source)
XLA Modules:
  0.0 335.5 jit_solution(2231902465308282045)
XLA Ops:
  7.2 0.0 copy-start
  7.2 0.0 all-reduce.3.cloned.1.call-start
  7.2 0.7 copy-done
  7.9 0.8 fusion.18
  8.8 0.0 all-reduce.3.cloned.1.call-update
  8.8 0.0 reduce-scatter.2.cloned.1.call-start
  8.8 4.3 %fusion.17 = f32[8192,128]{1,0:T(8,128)} fusion(bf16[128,8192]{1,0:T(8,128)(2,1)} %param.3, bf16[128,128]{1,0:T(8,128)(2,1)S(1)} %copy-done), kind=kOutput, calls=%fused_computation.38 | convolution fusion | flops 268435456 | bytes 6324224 | tf_op jit(solution)/shard_map/dot_general | solution.py:43
  13.1 0.0 reduce-scatter.2.cloned.1.call-update
  13.1 0.0 copy-start.3
  13.2 0.0 copy-start.1
  13.2 0.0 all-reduce.5.cloned.1.call-start
  13.2 0.1 copy.7
  13.4 70.6 %all-reduce.3.cloned.1.call-done = f32[128,128]{0,1:T(8,128)} async-done(((f32[128,128]{0,1:T(8,128)}), f32[128,128]{0,1:T(8,128)}) %all-reduce.3.cloned.1.call-update) | async-done | bytes 65552 | tf_op jit(solution)/shard_map/psum | solution.py:50
  84.0 0.8 convert_add_fusion
  84.8 0.1 copy.8
  84.9 11.7 %cholesky.29 = f32[128,128]{1,0:T(8,128)S(1)} custom-call(f32[128,128]{1,0:T(8,128)S(1)} %fusion.13), custom_call_target="Cholesky" | custom-call | tf_op jit(solution)/shard_map/jit(cholesky)/cholesky | solution.py:20
  96.7 0.6 compare_reduce_fusion
  97.3 0.7 fusion.10
  98.0 9.8 %custom-call.6 = f32[1,128,128]{1,2,0:T(8,128)S(1)} custom-call(f32[1,128,128]{2,1,0:T(8,128)S(1)} %fusion.10), custom_call_target="InvertDiagBlocksLowerTriangular" | custom-call | tf_op jit(solution)/shard_map/triangular_solve | solution.py:21
  107.8 0.2 fusion.11
  108.0 0.3 fusion.19
  108.3 67.6 %reduce-scatter.2.cloned.1.call-done = f32[1024,128]{1,0:T(8,128)} async-done(((f32[8192,128]{1,0:T(8,128)}), f32[1024,128]{1,0:T(8,128)}) %reduce-scatter.2.cloned.1.call-update) | async-done | bytes 524304 | tf_op jit(solution)/shard_map/reduce_scatter | solution.py:42
  176.0 2.3 fusion.16
  178.3 1.6 fusion.20
  179.9 0.0 all-reduce.5.cloned.1.call-update
  180.0 0.2 all-gather.2.cloned.1.call-start
  180.2 0.0 copy-done.3
  180.2 0.0 copy-done.1
  180.2 2.4 copy.5
  182.7 0.0 all-gather.2.cloned.1.call-update
  182.7 83.3 %all-reduce.5.cloned.1.call-done = f32[128,128]{1,0:T(8,128)} async-done(((f32[128,128]{1,0:T(8,128)}), f32[128,128]{1,0:T(8,128)}) %all-reduce.5.cloned.1.call-update) | async-done | bytes 65552 | tf_op jit(solution)/shard_map/psum | solution.py:56
  266.0 1.5 select_reduce_fusion
  267.5 1.7 fusion.9
  269.1 0.2 fusion.14
  269.3 1.7 fusion.15
  271.0 0.2 fusion.8
  271.2 0.2 fusion.21
  271.5 0.2 fusion.22
  271.7 0.2 fusion.7
  271.9 0.0 copy-start.2
  271.9 0.2 fusion.23
  272.1 0.2 fusion.24
  272.3 0.2 fusion.6
  272.5 0.2 fusion.25
  272.7 0.2 fusion.26
  273.0 0.2 fusion.5
  273.2 0.2 fusion.27
  273.4 0.2 fusion.28
  273.6 0.2 fusion.4
  273.8 0.2 fusion.29
  274.0 0.2 fusion.30
  274.2 0.2 fusion.3
  274.4 0.2 fusion.31
  274.6 0.2 fusion.32
  274.9 0.2 fusion.2
  275.1 0.2 fusion.33
  275.3 1.4 fusion.1
  276.6 42.0 %all-gather.2.cloned.1.call-done = bf16[8192,128]{1,0:T(8,128)(2,1)} async-done(((bf16[1024,128]{1,0:T(8,128)(2,1)}), bf16[8192,128]{1,0:T(8,128)(2,1)}) %all-gather.2.cloned.1.call-update) | async-done | bytes 2097168 | tf_op jit(solution)/shard_map/all_gather | solution.py:62
  318.7 0.0 copy-done.2
  318.7 6.2 %subtract_convert_fusion = bf16[128,8192]{0,1:T(8,128)(2,1)} fusion(bf16[8192,128]{1,0:T(8,128)(2,1)} %all-gather.2.cloned.1.call-done, bf16[128,128]{1,0:T(8,128)(2,1)S(1)} %copy-done, bf16[128,8192]{0,1:T(8,128)(2,1)S(1)} %copy-done.2, f32[8192]{0:T(1024)S(1)} %broadcast_add_fusion, f32[8192]{0:T(1024)S(1)} %copy-done.3), kind=kOutput, calls=%fused_computation.2 | convolution fusion | flops 274726912 | bytes 6389760 | tf_op jit(solution)/shard_map/dot_general | solution.py:60
  324.9 4.1 %copy.9 = bf16[128,8192]{1,0:T(8,128)(2,1)} copy(bf16[128,8192]{0,1:T(8,128)(2,1)} %subtract_convert_fusion) | data formatting | bytes 4194304
  (4 shorter events, 0.1 us)
Async XLA Ops:
  7.2 0.8 copy-start
  7.2 76.8 %all-reduce.3.cloned.1.call-start = ((), (), s32[]{:S(2)}) async-start(), calls=%async_computation.2 | async-start | bytes 131072 | tf_op jit(solution)/shard_map/psum | solution.py:50
  8.8 167.2 %reduce-scatter.2.cloned.1.call-start = ((), (), s32[]{:S(2)}) async-start(), calls=%async_computation.1 | async-start | bytes 4718592 | tf_op jit(solution)/shard_map/reduce_scatter | solution.py:42
  13.1 167.0 %copy-start.3 = (f32[8192]{0:T(1024)S(1)}, f32[8192]{0:T(1024)}, u32[]{:S(2)}) copy-start(f32[8192]{0:T(1024)} %param.5) | copy-start | bytes 98308
  13.2 167.1 %copy-start.1 = (bf16[128,8192]{1,0:T(8,128)(2,1)S(1)}, bf16[128,8192]{1,0:T(8,128)(2,1)}, u32[]{:S(2)}) copy-start(bf16[128,8192]{1,0:T(8,128)(2,1)} %param.3) | copy-start | bytes 6291460
  13.2 252.8 %all-reduce.5.cloned.1.call-start = ((), (), s32[]{:S(2)}) async-start(), calls=%async_computation.4 | async-start | bytes 131072 | tf_op jit(solution)/shard_map/psum | solution.py:56
  180.0 138.7 %all-gather.2.cloned.1.call-start = ((), (), s32[]{:S(2)}) async-start(), calls=%async_computation.3 | async-start | bytes 2359296 | tf_op jit(solution)/shard_map/all_gather | solution.py:62
  271.9 46.8 %copy-start.2 = (bf16[128,8192]{0,1:T(8,128)(2,1)S(1)}, bf16[128,8192]{0,1:T(8,128)(2,1)}, u32[]{:S(2)}) copy-start(bf16[128,8192]{0,1:T(8,128)(2,1)} %copy.5) | copy-start | bytes 6291460
Sparse Core Ops, SparseCore 0:
  12.0 71.9 all-reduce.2
  87.6 88.3 reduce-scatter.1
  180.1 85.8 all-reduce.4
  268.0 50.6 all-gather.1
where the time goes:
time: 336 us; the launch traced here: 335 us
  waiting for transfers between devices  264 us (79%)
  other arithmetic  25.2 us (8%)
  matrix products  24.8 us (7%)
  between operations  14 us (4%)
  local copies, waits for them, and re-layouts  7.44 us (2%)
    psum x1, waiting for transfers between devices, per_device(): moment = lax.psum(local_moment, ('cell', 'gene'))  83.3 us
    psum x1, waiting for transfers between devices, per_device(): gram_total = lax.psum(local_gram, 'cell')  70.6 us
    reduce_scatter x1, waiting for transfers between devices, per_device(): lax.psum_scatter(lax.dot_general(expression, design, (((0,), (0,)), ((),...  67.6 us
    all_gather x1, waiting for transfers between devices, per_device(): lax.all_gather(coef_low, 'cell', axis=0, tiled=True)  42 us
    another operation x4, other arithmetic, invert(): factor = jnp.linalg.cholesky(matrix)  12.4 us
    dot_general x26, matrix products, matmul(): return jnp.dot(left, right, precision=lax.Precision.HIGHEST)  11.6 us
    another operation x2, other arithmetic, invert(): lax.linalg.triangular_solve(factor, identity, left_side=True, lower=True)  10.5 us
    unnamed x10, local copies, waits for them, and re-layouts  7.23 us
  transfers between devices with their start and end apart: 4, of which 4 were waited for; matrix products, arithmetic and copies ran while one was open for 12% of the time, Pallas kernels for 0%

commit v1 on v0

--- a/solution.py
+++ b/solution.py
@@ -33,33 +33,47 @@
     return root_inv
 
 
+def gather_rows(block, axis):
+    n = lax.axis_size(axis)
+    tiled = jnp.concatenate([block] * n, axis=0)
+    return lax.all_to_all(tiled, axis, 0, 0, tiled=True)
+
+
+def butterfly_sum(value, axis):
+    n = lax.axis_size(axis)
+    if n & (n - 1):
+        return lax.psum(value, axis)
+    bit = 1
+    while bit < n:
+        pairs = [(i, i ^ bit) for i in range(n)]
+        value = value + lax.ppermute(value, axis, pairs)
+        bit *= 2
+    return value
+
+
 def per_device(expression, design, quantile_level):
     width = design.shape[1]
     identity = jnp.eye(width, dtype=jnp.float32)
-    local_gram = lax.dot_general(
-        design, design, (((0,), (0,)), ((), ())), preferred_element_type=jnp.float32
+    design_all = gather_rows(design, "cell")
+    gram_total = lax.dot_general(
+        design_all, design_all, (((0,), (0,)), ((), ())), preferred_element_type=jnp.float32
     )
-    crossed = lax.psum_scatter(
-        lax.dot_general(
-            expression, design, (((0,), (0,)), ((), ())), preferred_element_type=jnp.float32
-        ),
-        "cell",
-        scatter_dimension=0,
-        tiled=True,
+    inverse = invert(gram_total + identity)
+    expression_genes = lax.all_to_all(expression, "cell", 1, 0, tiled=True)
+    crossed = lax.dot_general(
+        expression_genes, design_all, (((0,), (0,)), ((), ())), preferred_element_type=jnp.float32
     )
-    gram_total = lax.psum(local_gram, "cell")
-    inverse = invert(gram_total + identity)
     coef = matmul(crossed, inverse)
     local_moment = lax.dot_general(
         coef, coef, (((0,), (0,)), ((), ())), precision=lax.Precision.HIGHEST
     )
-    moment = lax.psum(local_moment, ("cell", "gene"))
+    moment = butterfly_sum(butterfly_sum(local_moment, "gene"), "cell")
     root_inv = newton(moment)
     low_rank_coef = coef - shrink_rate / math.sqrt(width) * matmul(coef, root_inv)
     coef_low = coef.astype(jnp.bfloat16)
     fitted = lax.dot_general(
         design,
-        lax.all_gather(coef_low, "cell", axis=0, tiled=True),
+        gather_rows(coef_low, "cell"),
         (((1,), (1,)), ((), ())),
         preferred_element_type=jnp.float32,
     )

time: 336 us -> 154 us (0.46)
  waiting for transfers between devices: 264 us -> 72.7 us
  starting transfers between devices: 0.34 us -> 18.5 us
  between operations: 14 us -> 1.01 us
  local copies, waits for them, and re-layouts: 7.44 us -> 18.5 us
  matrix products: 24.8 us -> 18.3 us
    psum x2 -> x0, waiting for transfers between devices: 154 us -> none  [the longest x1 83.3 us: per_device(): moment = lax.psum(local_moment, ('cell', 'gene'))]
    reduce_scatter x1 -> x0, waiting for transfers between devices: 67.6 us -> none  [per_device(): lax.psum_scatter(lax.dot_general(expression, design, (((0,), (0,)), ((),...]
    all_to_all x0 -> x3, waiting for transfers between devices: none -> 64.7 us  [the longest x2 41.3 us: gather_rows(): return lax.all_to_all(tiled, axis, 0, 0, tiled=True)]
    all_gather x1 -> x0, waiting for transfers between devices: 42 us -> none  [per_device(): lax.all_gather(coef_low, 'cell', axis=0, tiled=True)]
    all_to_all x0 -> x3, starting transfers between devices: none -> 16.6 us  [the longest x2 12.3 us: gather_rows(): return lax.all_to_all(tiled, axis, 0, 0, tiled=True)]
    ppermute x0 -> x4, waiting for transfers between devices: none -> 8.04 us  [butterfly_sum(): value = value + lax.ppermute(value, axis, pairs)]
    unnamed x10 -> x21, local copies, waits for them, and re-layouts: 7.23 us -> 14.2 us
    all_to_all x0 -> x2, local copies, waits for them, and re-layouts: none -> 3.45 us  [the longest x1 2.6 us: per_device(): expression_genes = lax.all_to_all(expression, 'cell', 1, 0, tiled=True)]
  transfers between devices with their start and end apart: 4 -> 7, of which waited for: 4 -> 6; matrix products, arithmetic and copies ran while one was open for 12% -> 25% of each run, Pallas kernels for 0% -> 0%
where the time goes in v1:
time: 154 us; the launch traced here: 153 us
  waiting for transfers between devices  72.7 us (47%)
  other arithmetic  23.5 us (15%)
  local copies, waits for them, and re-layouts  18.5 us (12%)
  starting transfers between devices  18.5 us (12%)
  matrix products  18.3 us (12%)
    all_to_all x2, waiting for transfers between devices, gather_rows(): return lax.all_to_all(tiled, axis, 0, 0, tiled=True)  41.3 us
    all_to_all x1, waiting for transfers between devices, per_device(): expression_genes = lax.all_to_all(expression, 'cell', 1, 0, tiled=True)  23.4 us
    unnamed x21, local copies, waits for them, and re-layouts  14.2 us
    another operation x3, other arithmetic, invert(): factor = jnp.linalg.cholesky(matrix)  12.4 us
    all_to_all x2, starting transfers between devices, gather_rows(): return lax.all_to_all(tiled, axis, 0, 0, tiled=True)  12.3 us
    another operation x2, other arithmetic, invert(): lax.linalg.triangular_solve(factor, identity, left_side=True, lower=True)  10.5 us
    dot_general x26, matrix products, matmul(): return jnp.dot(left, right, precision=lax.Precision.HIGHEST)  8.58 us
    ppermute x4, waiting for transfers between devices, butterfly_sum(): value = value + lax.ppermute(value, axis, pairs)  8.04 us
  transfers between devices with their start and end apart: 7, of which 6 were waited for; matrix products, arithmetic and copies ran while one was open for 25% of the time, Pallas kernels for 0%

profile of v1, /device:TPU:0, one launch (start us, length us, event | category | flops | bytes accessed | tf_op | source)
XLA Modules:
  0.0 152.5 jit_solution(18045542996240944857)
XLA Ops:
  0.6 0.8 constant_dynamic-update-slice_fusion.7
  1.4 0.8 constant_dynamic-update-slice_fusion.6
  2.2 0.8 constant_dynamic-update-slice_fusion.5
  2.9 0.8 constant_dynamic-update-slice_fusion.4
  3.7 0.8 constant_dynamic-update-slice_fusion.3
  4.5 0.8 constant_dynamic-update-slice_fusion.2
  5.2 0.8 constant_dynamic-update-slice_fusion.1
  6.0 0.8 constant_dynamic-update-slice_fusion
  6.8 0.8 copy.20
  7.6 7.3 %all-to-all-start = ((bf16[8,128,128]{1,2,0:T(8,128)(2,1)}), bf16[8,128,128]{1,2,0:T(8,128)(2,1)S(1)}, u32[]{:S(2)}, u32[]{:S(2)}) async-start(bf16[8,128,128]{1,2,0:T(8,128)(2,1)} %copy.20), calls=%async_computation | async-start | bytes 524288 | tf_op jit(solution)/shard_map/all_to_all | solution.py:39
  14.9 3.2 %copy.19 = bf16[128,8192]{0,1:T(8,128)(2,1)S(1)} copy(bf16[128,8192]{1,0:T(8,128)(2,1)} %param.3) | data formatting | bytes 4194304 | tf_op args[0]
  18.1 2.6 %copy.22 = bf16[128,8,1024]{2,0,1:T(8,128)(2,1)} copy(bf16[128,8,1024]{0,2,1:T(8,128)(2,1)S(1)} %bitcast.85) | data formatting | bytes 4194304 | tf_op jit(solution)/shard_map/all_to_all | solution.py:62
  20.7 3.1 %all-to-all-done = bf16[8,128,128]{1,2,0:T(8,128)(2,1)S(1)} async-done(((bf16[8,128,128]{1,2,0:T(8,128)(2,1)}), bf16[8,128,128]{1,2,0:T(8,128)(2,1)S(1)}, u32[]{:S(2)}, u32[]{:S(2)}) %all-to-all-start) | async-done | bytes 262176 | tf_op jit(solution)/shard_map/all_to_all | solution.py:39
  23.8 4.4 %all-to-all-start.1 = ((bf16[128,8,1024]{2,0,1:T(8,128)(2,1)}), bf16[128,8,1024]{2,0,1:T(8,128)(2,1)}, u32[]{:S(2)}, u32[]{:S(2)}) async-start(bf16[128,8,1024]{2,0,1:T(8,128)(2,1)} %copy.22), calls=%async_computation.1 | async-start | bytes 4194304 | tf_op jit(solution)/shard_map/all_to_all | solution.py:62
  28.2 0.2 convolution_bitcast_fusion.1
  28.4 0.1 copy.24
  28.6 11.7 %cholesky.29 = f32[128,128]{1,0:T(8,128)S(1)} custom-call(f32[128,128]{1,0:T(8,128)S(1)} %fusion.19), custom_call_target="Cholesky" | custom-call | tf_op jit(solution)/shard_map/jit(cholesky)/cholesky | solution.py:20
  40.3 0.6 compare_reduce_fusion
  40.9 0.7 fusion.15
  41.6 9.8 %custom-call.6 = f32[1,128,128]{1,2,0:T(8,128)S(1)} custom-call(f32[1,128,128]{2,1,0:T(8,128)S(1)} %fusion.15), custom_call_target="InvertDiagBlocksLowerTriangular" | custom-call | tf_op jit(solution)/shard_map/triangular_solve | solution.py:21
  51.4 0.2 fusion.16
  51.7 0.3 fusion.22
  52.0 23.4 %all-to-all-done.1 = bf16[128,8,1024]{2,0,1:T(8,128)(2,1)} async-done(((bf16[128,8,1024]{2,0,1:T(8,128)(2,1)}), bf16[128,8,1024]{2,0,1:T(8,128)(2,1)}, u32[]{:S(2)}, u32[]{:S(2)}) %all-to-all-start.1) | async-done | bytes 2097184 | tf_op jit(solution)/shard_map/all_to_all | solution.py:62
  75.4 2.0 %fusion.3 = f32[128,1024]{1,0:T(8,128)S(1)} fusion(bf16[8,128,128]{1,2,0:T(8,128)(2,1)S(1)} %all-to-all-done, bf16[128,8,1024]{2,0,1:T(8,128)(2,1)} %all-to-all-done.1), kind=kOutput, calls=%fused_computation.5 | convolution fusion | flops 268435456 | bytes 2883584 | tf_op jit(solution)/shard_map/dot_general | solution.py:63
  77.4 1.0 constant_dynamic-update-slice_fusion.15
  78.4 1.0 fusion.23
  79.4 0.1 collective-permute-start
  79.7 1.1 collective-permute-done
  80.8 1.5 collective-permute-start.1
  82.3 2.8 %collective-permute-done.1 = f32[128,128]{1,0:T(8,128)S(1)} collective-permute-done((f32[128,128]{1,0:T(8,128)S(1)}, f32[128,128]{1,0:T(8,128)S(1)}, u32[]{:S(2)}, u32[]{:S(2)}) %collective-permute-start.1) | collective-permute-done | bytes 65568 | tf_op jit(solution)/shard_map/ppermute | solution.py:49
  85.1 0.1 collective-permute-start.2
  85.2 4.2 %collective-permute-done.2 = f32[128,128]{1,0:T(8,128)S(1)} collective-permute-done((f32[128,128]{1,0:T(8,128)S(1)}, f32[128,128]{1,0:T(8,128)S(1)}, u32[]{:S(2)}, u32[]{:S(2)}) %collective-permute-start.2) | collective-permute-done | bytes 65568 | tf_op jit(solution)/shard_map/ppermute | solution.py:49
  89.5 0.2 collective-permute-start.3
  89.7 1.3 copy-done
  91.0 5.0 %all-to-all-start.2 = ((bf16[8,1024,128]{2,1,0:T(8,128)(2,1)}), bf16[8,1024,128]{2,1,0:T(8,128)(2,1)}, u32[]{:S(2)}, u32[]{:S(2)}) async-start(bf16[8,1024,128]{2,1,0:T(8,128)(2,1)} %bitcast.86), calls=%async_computation.2 | async-start | bytes 4194304 | tf_op jit(solution)/shard_map/all_to_all | solution.py:39
  96.0 0.6 select_reduce_fusion
  96.6 0.8 fusion.14
  97.5 0.8 fusion.21
  98.3 0.2 fusion.20
  98.5 0.2 fusion.13
  98.7 0.2 fusion.25
  98.9 0.2 fusion.24
  99.1 0.2 fusion.12
  99.3 0.0 copy-start.1
  99.4 0.2 fusion.27
  99.6 0.2 fusion.26
  99.8 0.2 fusion.11
  100.0 0.2 fusion.29
  100.2 0.2 fusion.28
  100.4 0.2 fusion.10
  100.6 0.2 fusion.31
  100.8 0.2 fusion.30
  101.0 0.2 fusion.9
  101.3 0.2 fusion.33
  101.5 0.2 fusion.32
  101.7 0.2 fusion.8
  101.9 0.2 fusion.35
  102.1 0.2 fusion.34
  102.3 0.2 fusion.7
  102.5 0.2 fusion.36
  102.7 1.4 fusion.6
  104.1 38.2 %all-to-all-done.2 = bf16[8,1024,128]{2,1,0:T(8,128)(2,1)} async-done(((bf16[8,1024,128]{2,1,0:T(8,128)(2,1)}), bf16[8,1024,128]{2,1,0:T(8,128)(2,1)}, u32[]{:S(2)}, u32[]{:S(2)}) %all-to-all-start.2) | async-done | bytes 2097184 | tf_op jit(solution)/shard_map/all_to_all | solution.py:39
  142.3 6.2 %subtract_convert_fusion = bf16[128,8192]{0,1:T(8,128)(2,1)} fusion(bf16[8192,128]{1,0:T(8,128)(2,1)} %bitcast.9, bf16[128,128]{1,0:T(8,128)(2,1)S(1)} %copy-done.1, bf16[128,8192]{0,1:T(8,128)(2,1)S(1)} %copy.19, f32[8192]{0:T(1024)S(1)} %broadcast_add_fusion, f32[8192]{0:T(1024)S(1)} %copy-done.2), kind=kOutput, calls=%fused_computation.2 | convolution fusion | flops 274726912 | bytes 6389760 | tf_op jit(solution)/shard_map/dot_general | solution.py:74
  148.5 4.1 %copy.25 = bf16[128,8192]{1,0:T(8,128)(2,1)} copy(bf16[128,8192]{0,1:T(8,128)(2,1)} %subtract_convert_fusion) | data formatting | bytes 4194304
  (18 shorter events, 0.4 us)
Async XLA Ops:
  7.6 16.2 %all-to-all-start = ((bf16[8,128,128]{1,2,0:T(8,128)(2,1)}), bf16[8,128,128]{1,2,0:T(8,128)(2,1)S(1)}, u32[]{:S(2)}, u32[]{:S(2)}) async-start(bf16[8,128,128]{1,2,0:T(8,128)(2,1)} %copy.20), calls=%async_computation | async-start | bytes 524288 | tf_op jit(solution)/shard_map/all_to_all | solution.py:39
  20.7 7.5 %copy-start.2 = (f32[8192]{0:T(1024)S(1)}, f32[8192]{0:T(1024)}, u32[]{:S(2)}) copy-start(f32[8192]{0:T(1024)} %param.5) | copy-start | bytes 98308
  23.8 51.6 %all-to-all-start.1 = ((bf16[128,8,1024]{2,0,1:T(8,128)(2,1)}), bf16[128,8,1024]{2,0,1:T(8,128)(2,1)}, u32[]{:S(2)}, u32[]{:S(2)}) async-start(bf16[128,8,1024]{2,0,1:T(8,128)(2,1)} %copy.22), calls=%async_computation.1 | async-start | bytes 4194304 | tf_op jit(solution)/shard_map/all_to_all | solution.py:62
  79.4 1.3 collective-permute-start
  80.8 4.3 %collective-permute-start.1 = (f32[128,128]{1,0:T(8,128)S(1)}, f32[128,128]{1,0:T(8,128)S(1)}, u32[]{:S(2)}, u32[]{:S(2)}) collective-permute-start(f32[128,128]{1,0:T(8,128)S(1)} %add.34), channel_id=1, source_target_pairs={{0,2},{2,0},{4,6},{6,4},{8,10},{10,8},{12,14},{14,12},{1,3},{3,1},... | collective-permute-start | bytes 196616 | tf_op jit(solution)/shard_map/ppermute | solution.py:49
  85.1 4.3 %collective-permute-start.2 = (f32[128,128]{1,0:T(8,128)S(1)}, f32[128,128]{1,0:T(8,128)S(1)}, u32[]{:S(2)}, u32[]{:S(2)}) collective-permute-start(f32[128,128]{1,0:T(8,128)S(1)} %add.35), channel_id=1, source_target_pairs={{0,4},{2,6},{4,0},{6,2},{8,12},{10,14},{12,8},{14,10},{1,5},{3,7},... | collective-permute-start | bytes 196616 | tf_op jit(solution)/shard_map/ppermute | solution.py:49
  89.5 6.5 %collective-permute-start.3 = (f32[128,128]{1,0:T(8,128)S(1)}, f32[128,128]{1,0:T(8,128)S(1)}, u32[]{:S(2)}, u32[]{:S(2)}) collective-permute-start(f32[128,128]{1,0:T(8,128)S(1)} %add.36), channel_id=1, source_target_pairs={{0,8},{2,10},{4,12},{6,14},{8,0},{10,2},{12,4},{14,6},{1,9},{3,11}... | collective-permute-start | bytes 196616 | tf_op jit(solution)/shard_map/ppermute | solution.py:49
  89.7 1.3 copy-start
  91.0 51.3 %all-to-all-start.2 = ((bf16[8,1024,128]{2,1,0:T(8,128)(2,1)}), bf16[8,1024,128]{2,1,0:T(8,128)(2,1)}, u32[]{:S(2)}, u32[]{:S(2)}) async-start(bf16[8,1024,128]{2,1,0:T(8,128)(2,1)} %bitcast.86), calls=%async_computation.2 | async-start | bytes 4194304 | tf_op jit(solution)/shard_map/all_to_all | solution.py:39
  99.3 42.9 %copy-start.1 = (bf16[128,128]{1,0:T(8,128)(2,1)S(1)}, bf16[128,128]{1,0:T(8,128)(2,1)}, u32[]{:S(2)}) copy-start(bf16[128,128]{1,0:T(8,128)(2,1)} %param.4) | copy-start | bytes 98308

commit v2 on v1

--- a/solution.py
+++ b/solution.py
@@ -1,3 +1,4 @@
+import functools
 import math
 
 import jax
@@ -33,10 +34,58 @@
     return root_inv
 
 
+def cell_ring(mesh):
+    devices = mesh.devices
+    names = list(mesh.axis_names)
+    index = [0] * len(names)
+    index[names.index("cell")] = slice(None)
+    line = list(devices[tuple(index)].reshape(-1))
+    n = len(line)
+    try:
+        coords = [tuple(d.coords) for d in line]
+    except (AttributeError, TypeError):
+        return list(range(n))
+    varying = [a for a in range(len(coords[0])) if len({c[a] for c in coords}) > 1]
+    where = {c: i for i, c in enumerate(coords)}
+    if len(varying) == 1:
+        return sorted(range(n), key=lambda i: coords[i][varying[0]])
+    if len(varying) != 2:
+        return list(range(n))
+    sizes = [len({c[a] for c in coords}) for a in varying]
+    if sizes[0] * sizes[1] != n:
+        return list(range(n))
+    if sizes[0] % 2:
+        varying, sizes = varying[::-1], sizes[::-1]
+        if sizes[0] % 2:
+            return list(range(n))
+    lows = [min(c[a] for c in coords) for a in varying]
+    path = []
+    for u in range(sizes[0]):
+        span = range(1, sizes[1]) if u % 2 == 0 else range(sizes[1] - 1, 0, -1)
+        path += [(u, v) for v in span]
+    path += [(u, 0) for u in range(sizes[0] - 1, -1, -1)]
+    order = []
+    for u, v in path:
+        key = list(coords[0])
+        key[varying[0]] = lows[0] + u
+        key[varying[1]] = lows[1] + v
+        order.append(where[tuple(key)])
+    return order
+
+
 def gather_rows(block, axis):
     n = lax.axis_size(axis)
-    tiled = jnp.concatenate([block] * n, axis=0)
-    return lax.all_to_all(tiled, axis, 0, 0, tiled=True)
+    if n & (n - 1):
+        return lax.all_gather(block, axis, axis=0, tiled=True)
+    me = lax.axis_index(axis)
+    bit = 1
+    while bit < n:
+        pairs = [(i, i ^ bit) for i in range(n)]
+        other = lax.ppermute(block, axis, pairs)
+        low = (me & bit) == 0
+        block = jnp.where(low, jnp.concatenate([block, other]), jnp.concatenate([other, block]))
+        bit *= 2
+    return block
 
 
 def butterfly_sum(value, axis):
@@ -51,15 +100,17 @@
     return value
 
 
-def per_device(expression, design, quantile_level):
+def per_device(ring, expression, design, quantile_level):
+    n = len(ring)
     width = design.shape[1]
+    span = expression.shape[1] // n
     identity = jnp.eye(width, dtype=jnp.float32)
+    expression_genes = lax.all_to_all(expression, "cell", 1, 0, tiled=True)
     design_all = gather_rows(design, "cell")
     gram_total = lax.dot_general(
         design_all, design_all, (((0,), (0,)), ((), ())), preferred_element_type=jnp.float32
     )
     inverse = invert(gram_total + identity)
-    expression_genes = lax.all_to_all(expression, "cell", 1, 0, tiled=True)
     crossed = lax.dot_general(
         expression_genes, design_all, (((0,), (0,)), ((), ())), preferred_element_type=jnp.float32
     )
@@ -70,23 +121,42 @@
     moment = butterfly_sum(butterfly_sum(local_moment, "gene"), "cell")
     root_inv = newton(moment)
     low_rank_coef = coef - shrink_rate / math.sqrt(width) * matmul(coef, root_inv)
-    coef_low = coef.astype(jnp.bfloat16)
-    fitted = lax.dot_general(
-        design,
-        gather_rows(coef_low, "cell"),
-        (((1,), (1,)), ((), ())),
-        preferred_element_type=jnp.float32,
-    )
-    slack = expression.astype(jnp.float32) - fitted
-    level = quantile_level[None, :]
-    quantile_slack = (slack - jnp.clip(slack, level - 1.0, level)).astype(jnp.bfloat16)
-    return (quantile_slack, low_rank_coef)
+    coef_low_t = coef.astype(jnp.bfloat16).T
+
+    ring_arr = jnp.array(ring, dtype=jnp.int32)
+    pos_arr = jnp.array([ring.index(i) for i in range(n)], dtype=jnp.int32)
+    me = lax.axis_index("cell")
+    pos = pos_arr[me]
+    forward = [(ring[q], ring[(q + 1) % n]) for q in range(n)]
+    backward = [(ring[(q + 1) % n], ring[q]) for q in range(n)]
+
+    out = jnp.zeros(expression.shape, jnp.bfloat16)
+
+    def place(out, block, owner):
+        start = owner * span
+        fitted = jnp.dot(design, block, preferred_element_type=jnp.float32)
+        local = lax.dynamic_slice_in_dim(expression, start, span, axis=1).astype(jnp.float32)
+        level = lax.dynamic_slice_in_dim(quantile_level, start, span)[None, :]
+        slack = local - fitted
+        piece = (slack - jnp.clip(slack, level - 1.0, level)).astype(jnp.bfloat16)
+        return lax.dynamic_update_slice_in_dim(out, piece, start, axis=1)
+
+    out = place(out, coef_low_t, me)
+    ahead, behind = coef_low_t, coef_low_t
+    for step in range(1, n // 2 + 1):
+        ahead = lax.ppermute(ahead, "cell", forward)
+        out = place(out, ahead, ring_arr[(pos - step) % n])
+        if step <= (n - 1) // 2:
+            behind = lax.ppermute(behind, "cell", backward)
+            out = place(out, behind, ring_arr[(pos + step) % n])
+    return (out, low_rank_coef)
 
 
 def solution(mesh):
     placed = (P(("grp", "cell"), "gene"), P(("grp", "cell"), None), P("gene"))
+    ring = cell_ring(mesh)
     return jax.shard_map(
-        per_device,
+        functools.partial(per_device, ring),
         mesh=mesh,
         in_specs=placed,
         out_specs=(P(("grp", "cell"), "gene"), P(("grp", "gene", "cell"), None)),

time: 154 us -> 147 us (0.955)
  waiting for transfers between devices: 72.7 us -> 50.9 us
  between operations: 1.01 us -> 10.2 us
  starting transfers between devices: 18.5 us -> 24.9 us
  matrix products: 18.3 us -> 22.6 us
  local copies, waits for them, and re-layouts: 18.5 us -> 14.5 us
    all_to_all x2 -> x0, waiting for transfers between devices: 41.3 us -> none  [gather_rows(): return lax.all_to_all(tiled, axis, 0, 0, tiled=True)]
    ppermute x0 -> x10, waiting for transfers between devices: none -> 39.2 us  [the longest x3 36 us: gather_rows(): other = lax.ppermute(block, axis, pairs)]
    all_to_all x1, waiting for transfers between devices: 23.4 us -> 0.01 us  [per_device(): expression_genes = lax.all_to_all(expression, 'cell', 1, 0, tiled=True)]
    ppermute x0 -> x10, starting transfers between devices: none -> 15.5 us  [the longest x3 7.46 us: gather_rows(): other = lax.ppermute(block, axis, pairs)]
    all_to_all x2 -> x0, starting transfers between devices: 12.3 us -> none  [gather_rows(): return lax.all_to_all(tiled, axis, 0, 0, tiled=True)]
    unnamed x21 -> x11, local copies, waits for them, and re-layouts: 14.2 us -> 4.11 us
    dynamic_update_slice x0 -> x8, local copies, waits for them, and re-layouts: none -> 5.07 us  [place(): return lax.dynamic_update_slice_in_dim(out, piece, start, axis=1)]
    dot_general x1 -> x8, matrix products: 6.18 us -> 10.5 us  [place(): fitted = jnp.dot(design, block, preferred_element_type=jnp.float32)]
  transfers between devices with their start and end apart: 7 -> 15, of which waited for: 6 -> 9; matrix products, arithmetic and copies ran while one was open for 25% -> 33% of each run, Pallas kernels for 0% -> 0%
where the time goes in v2:
time: 147 us
  waiting for transfers between devices  50.9 us (35%)
  starting transfers between devices  24.9 us (17%)
  other arithmetic  23.6 us (16%)
  matrix products  22.6 us (15%)
  local copies, waits for them, and re-layouts  14.5 us (10%)
  between operations  10.2 us (7%)
    ppermute x3, waiting for transfers between devices, gather_rows(): other = lax.ppermute(block, axis, pairs)  36 us
    another operation x3, other arithmetic, invert(): factor = jnp.linalg.cholesky(matrix)  12.4 us
    ppermute x4, waiting for transfers between devices, butterfly_sum(): value = value + lax.ppermute(value, axis, pairs)  11.7 us
    another operation x2, other arithmetic, invert(): lax.linalg.triangular_solve(factor, identity, left_side=True, lower=True)  10.5 us
    dot_general x8, matrix products, place(): fitted = jnp.dot(design, block, preferred_element_type=jnp.float32)  10.5 us
    dot_general x26, matrix products, matmul(): return jnp.dot(left, right, precision=lax.Precision.HIGHEST)  8.58 us
    ppermute x3, starting transfers between devices, gather_rows(): other = lax.ppermute(block, axis, pairs)  7.46 us
    all_to_all x1, starting transfers between devices, per_device(): expression_genes = lax.all_to_all(expression, 'cell', 1, 0, tiled=True)  7.42 us
  transfers between devices with their start and end apart: 15, of which 9 were waited for; matrix products, arithmetic and copies ran while one was open for 33% of the time, Pallas kernels for 0%

profile of v2, /device:TPU:0, one launch (start us, length us, event | category | flops | bytes accessed | tf_op | source)
XLA Modules:
  0.0 146.8 jit_solution(16357872054067453236)
XLA Ops:
  0.6 4.1 %copy.41 = bf16[128,8192]{0,1:T(8,128)(2,1)} copy(bf16[128,8192]{1,0:T(8,128)(2,1)} %param.5) | data formatting | bytes 4194304 | tf_op args[0]
  4.7 7.4 %all-to-all-start = ((bf16[128,8,1024]{0,2,1:T(8,128)(2,1)}), bf16[128,8,1024]{0,2,1:T(8,128)(2,1)S(1)}, u32[]{:S(2)}, u32[]{:S(2)}) async-start(bf16[128,8,1024]{0,2,1:T(8,128)(2,1)} %bitcast), calls=%async_computation | async-start | bytes 4194304 | tf_op jit(solution)/shard_map/all_to_all | solution.py:108
  12.1 2.0 %collective-permute-start = (bf16[128,128]{1,0:T(8,128)(2,1)S(1)}, bf16[128,128]{1,0:T(8,128)(2,1)S(1)}, u32[]{:S(2)}, u32[]{:S(2)}) collective-permute-start(bf16[128,128]{1,0:T(8,128)(2,1)S(1)} %copy-done.1), channel_id=1, source_target_pairs={{0,2},{2,0},{4,6},{6,4},{8,10},{10,8},{12,14},{14,12},{1,3},{3,1},... | collective-permute-start | bytes 98312 | tf_op jit(solution)/shard_map/ppermute | solution.py:84
  14.2 15.7 %collective-permute-done = bf16[128,128]{1,0:T(8,128)(2,1)S(1)} collective-permute-done((bf16[128,128]{1,0:T(8,128)(2,1)S(1)}, bf16[128,128]{1,0:T(8,128)(2,1)S(1)}, u32[]{:S(2)}, u32[]{:S(2)}) %collective-permute-start) | collective-permute-done | bytes 32800 | tf_op jit(solution)/shard_map/ppermute | solution.py:84
  29.9 1.8 %collective-permute-start.1 = (bf16[256,128]{1,0:T(8,128)(2,1)S(1)}, bf16[256,128]{1,0:T(8,128)(2,1)S(1)}, u32[]{:S(2)}, u32[]{:S(2)}) collective-permute-start(bf16[256,128]{1,0:T(8,128)(2,1)S(1)} %maximum_select_fusion.2), channel_id=1, source_target_pairs={{0,4},{2,6},{4,0},{6,2},{8,12},{10,14},{12,8},{14,10},{1,5},{3,7},... | collective-permute-start | bytes 196616 | tf_op jit(solution)/shard_map/ppermute | solution.py:84
  31.7 16.9 %collective-permute-done.1 = bf16[256,128]{1,0:T(8,128)(2,1)S(1)} collective-permute-done((bf16[256,128]{1,0:T(8,128)(2,1)S(1)}, bf16[256,128]{1,0:T(8,128)(2,1)S(1)}, u32[]{:S(2)}, u32[]{:S(2)}) %collective-permute-start.1) | collective-permute-done | bytes 65568 | tf_op jit(solution)/shard_map/ppermute | solution.py:84
  48.6 3.6 %collective-permute-start.2 = (bf16[512,128]{1,0:T(8,128)(2,1)S(1)}, bf16[512,128]{1,0:T(8,128)(2,1)S(1)}, u32[]{:S(2)}, u32[]{:S(2)}) collective-permute-start(bf16[512,128]{1,0:T(8,128)(2,1)S(1)} %maximum_select_fusion.1), channel_id=1, source_target_pairs={{0,8},{2,10},{4,12},{6,14},{8,0},{10,2},{12,4},{14,6},{1,9},{3,11}... | collective-permute-start | bytes 393224 | tf_op jit(solution)/shard_map/ppermute | solution.py:84
  52.2 0.6 dynamic_slice.74
  57.5 0.7 fusion.29
  62.6 3.4 %collective-permute-done.2 = bf16[512,128]{1,0:T(8,128)(2,1)S(1)} collective-permute-done((bf16[512,128]{1,0:T(8,128)(2,1)S(1)}, bf16[512,128]{1,0:T(8,128)(2,1)S(1)}, u32[]{:S(2)}, u32[]{:S(2)}) %collective-permute-start.2) | collective-permute-done | bytes 131104 | tf_op jit(solution)/shard_map/ppermute | solution.py:84
  66.0 0.3 fusion.24
  66.4 11.7 %cholesky.29 = f32[128,128]{1,0:T(8,128)S(1)} custom-call(f32[128,128]{1,0:T(8,128)S(1)} %fusion.22), custom_call_target="Cholesky" | custom-call | tf_op jit(solution)/shard_map/jit(cholesky)/cholesky | solution.py:21
  78.1 0.6 compare_reduce_fusion
  78.8 0.7 fusion.18
  79.5 9.8 %custom-call.6 = f32[1,128,128]{1,2,0:T(8,128)S(1)} custom-call(f32[1,128,128]{2,1,0:T(8,128)S(1)} %fusion.18), custom_call_target="InvertDiagBlocksLowerTriangular" | custom-call | tf_op jit(solution)/shard_map/triangular_solve | solution.py:22
  89.3 0.2 fusion.19
  89.5 0.3 fusion.30
  89.8 2.6 %copy.43 = bf16[8,128,1024]{2,1,0:T(8,128)(2,1)} copy(bf16[8,128,1024]{1,2,0:T(8,128)(2,1)S(1)} %bitcast.144) | data formatting | bytes 4194304 | tf_op jit(solution)/shard_map/all_to_all | solution.py:108
  92.4 2.1 %fusion.25 = f32[128,1024]{1,0:T(8,128)S(1)} fusion(bf16[1024,1024]{1,0:T(8,128)(2,1)} %bitcast.145, bf16[512,128]{1,0:T(8,128)(2,1)S(1)} %collective-permute-done.2, bf16[512,128]{1,0:T(8,128)(2,1)S(1)} %maximum_select_fusion.1, pred[]{:T(512)S(6)} %eq.25), kind=kOutput, calls=%fused_computation.61 | convolution fusion | flops 269615104 | bytes 2883585 | tf_op jit(solution)/shard_map/dot_general | solution.py:114
  94.5 1.0 fusion.31
  95.5 1.0 fusion.32
  96.6 1.2 collective-permute-done.10
  97.8 1.5 %collective-permute-start.11 = (f32[128,128]{1,0:T(8,128)S(1)}, f32[128,128]{1,0:T(8,128)S(1)}, u32[]{:S(2)}, u32[]{:S(2)}) collective-permute-start(f32[128,128]{1,0:T(8,128)S(1)} %add.189), channel_id=1, source_target_pairs={{0,2},{2,0},{4,6},{6,4},{8,10},{10,8},{12,14},{14,12},{1,3},{3,1},... | collective-permute-start | bytes 196616 | tf_op jit(solution)/shard_map/ppermute | solution.py:98
  99.4 0.6 collective-permute-start.4
  100.0 1.5 collective-permute-start.3
  101.5 0.7 collective-permute-done.11
  102.3 1.3 subtract_convert_fusion.7
  103.7 5.2 %collective-permute-done.12 = f32[128,128]{1,0:T(8,128)S(1)} collective-permute-done((f32[128,128]{1,0:T(8,128)S(1)}, f32[128,128]{1,0:T(8,128)S(1)}, u32[]{:S(2)}, u32[]{:S(2)}) %collective-permute-start.12) | collective-permute-done | bytes 65568 | tf_op jit(solution)/shard_map/ppermute | solution.py:98
  109.0 0.4 collective-permute-start.13
  109.6 4.6 %collective-permute-done.13 = f32[128,128]{1,0:T(8,128)S(1)} collective-permute-done((f32[128,128]{1,0:T(8,128)S(1)}, f32[128,128]{1,0:T(8,128)S(1)}, u32[]{:S(2)}, u32[]{:S(2)}) %collective-permute-start.13) | collective-permute-done | bytes 65568 | tf_op jit(solution)/shard_map/ppermute | solution.py:98
  114.2 0.6 select_reduce_fusion
  114.8 0.8 fusion.16
  115.6 0.8 fusion.26
  116.7 0.2 fusion.15
  117.1 0.2 fusion.33
  117.3 0.2 fusion.14
  118.0 0.2 fusion.13
  118.6 0.2 fusion.12
  119.2 0.2 fusion.11
  119.9 0.2 fusion.10
  120.1 0.2 fusion.43
  120.5 0.2 fusion.9
  120.7 1.8 %collective-permute-start.5 = (bf16[128,1024]{0,1:T(8,128)(2,1)S(1)}, bf16[128,1024]{0,1:T(8,128)(2,1)S(1)}, u32[]{:S(2)}, u32[]{:S(2)}) collective-permute-start(bf16[128,1024]{0,1:T(8,128)(2,1)S(1)} %collective-permute-done.3), channel_id=1, source_target_pairs={{4,8},{8,12},{12,14},{14,10},{10,6},{6,2},{2,0},{0,4},{5,9},{9,13}... | collective-permute-start | bytes 786440 | tf_op jit(solution)/shard_map/ppermute | solution.py:147
  122.5 1.3 subtract_convert_fusion.6
  124.0 1.4 fusion.8
  125.4 1.3 subtract_convert_fusion.5
  127.0 0.3 collective-permute-start.6
  127.4 0.7 constant_dynamic-update-slice_fusion.6
  128.1 0.7 constant_dynamic-update-slice_fusion.5
  128.8 1.8 %collective-permute-start.7 = (bf16[128,1024]{0,1:T(8,128)(2,1)S(1)}, bf16[128,1024]{0,1:T(8,128)(2,1)S(1)}, u32[]{:S(2)}, u32[]{:S(2)}) collective-permute-start(bf16[128,1024]{0,1:T(8,128)(2,1)S(1)} %collective-permute-done.5), channel_id=1, source_target_pairs={{4,8},{8,12},{12,14},{14,10},{10,6},{6,2},{2,0},{0,4},{5,9},{9,13}... | collective-permute-start | bytes 786440 | tf_op jit(solution)/shard_map/ppermute | solution.py:147
  130.6 1.3 subtract_convert_fusion.4
  131.9 1.6 %collective-permute-done.6 = bf16[128,1024]{0,1:T(8,128)(2,1)S(1)} collective-permute-done((bf16[128,1024]{0,1:T(8,128)(2,1)S(1)}, bf16[128,1024]{0,1:T(8,128)(2,1)S(1)}, u32[]{:S(2)}, u32[]{:S(2)}) %collective-permute-start.6) | collective-permute-done | bytes 262176 | tf_op jit(solution)/shard_map/ppermute | solution.py:150
  133.5 1.3 subtract_convert_fusion.3
  135.1 0.3 collective-permute-start.8
  135.4 0.7 constant_dynamic-update-slice_fusion.4
  136.1 0.7 constant_dynamic-update-slice_fusion.3
  136.8 1.8 %collective-permute-start.9 = (bf16[128,1024]{0,1:T(8,128)(2,1)S(1)}, bf16[128,1024]{0,1:T(8,128)(2,1)S(1)}, u32[]{:S(2)}, u32[]{:S(2)}) collective-permute-start(bf16[128,1024]{0,1:T(8,128)(2,1)S(1)} %collective-permute-done.7), channel_id=1, source_target_pairs={{4,8},{8,12},{12,14},{14,10},{10,6},{6,2},{2,0},{0,4},{5,9},{9,13}... | collective-permute-start | bytes 786440 | tf_op jit(solution)/shard_map/ppermute | solution.py:147
  138.6 1.3 subtract_convert_fusion.2
  139.9 1.6 %collective-permute-done.8 = bf16[128,1024]{0,1:T(8,128)(2,1)S(1)} collective-permute-done((bf16[128,1024]{0,1:T(8,128)(2,1)S(1)}, bf16[128,1024]{0,1:T(8,128)(2,1)S(1)}, u32[]{:S(2)}, u32[]{:S(2)}) %collective-permute-start.8) | collective-permute-done | bytes 262176 | tf_op jit(solution)/shard_map/ppermute | solution.py:150
  141.5 1.3 subtract_convert_fusion.1
  143.1 0.7 constant_dynamic-update-slice_fusion.2
  143.8 0.7 constant_dynamic-update-slice_fusion.1
  144.6 1.3 subtract_convert_fusion
  146.0 0.7 constant_dynamic-update-slice_fusion
  (50 shorter events, 4.3 us)
Async XLA Ops:
  4.7 7.4 %copy-start.1 = (bf16[128,128]{1,0:T(8,128)(2,1)S(1)}, bf16[128,128]{1,0:T(8,128)(2,1)}, u32[]{:S(2)}) copy-start(bf16[128,128]{1,0:T(8,128)(2,1)} %param.6) | copy-start | bytes 98308
  4.7 47.5 %copy-start.4 = (s32[8]{0:T(128)S(1)}, s32[8]{0:T(128)}, u32[]{:S(2)}) copy-start(s32[8]{0:T(128)} %constant.149.clone) | copy-start | bytes 100
  4.7 52.8 %copy-start.3 = (s32[8]{0:T(128)S(1)}, s32[8]{0:T(128)}, u32[]{:S(2)}) copy-start(s32[8]{0:T(128)} %constant.148.clone) | copy-start | bytes 100
  4.7 85.1 %all-to-all-start = ((bf16[128,8,1024]{0,2,1:T(8,128)(2,1)}), bf16[128,8,1024]{0,2,1:T(8,128)(2,1)S(1)}, u32[]{:S(2)}, u32[]{:S(2)}) async-start(bf16[128,8,1024]{0,2,1:T(8,128)(2,1)} %bitcast), calls=%async_computation | async-start | bytes 4194304 | tf_op jit(solution)/shard_map/all_to_all | solution.py:108
  12.1 17.7 %collective-permute-start = (bf16[128,128]{1,0:T(8,128)(2,1)S(1)}, bf16[128,128]{1,0:T(8,128)(2,1)S(1)}, u32[]{:S(2)}, u32[]{:S(2)}) collective-permute-start(bf16[128,128]{1,0:T(8,128)(2,1)S(1)} %copy-done.1), channel_id=1, source_target_pairs={{0,2},{2,0},{4,6},{6,4},{8,10},{10,8},{12,14},{14,12},{1,3},{3,1},... | collective-permute-start | bytes 98312 | tf_op jit(solution)/shard_map/ppermute | solution.py:84
  29.9 18.7 %collective-permute-start.1 = (bf16[256,128]{1,0:T(8,128)(2,1)S(1)}, bf16[256,128]{1,0:T(8,128)(2,1)S(1)}, u32[]{:S(2)}, u32[]{:S(2)}) collective-permute-start(bf16[256,128]{1,0:T(8,128)(2,1)S(1)} %maximum_select_fusion.2), channel_id=1, source_target_pairs={{0,4},{2,6},{4,0},{6,2},{8,12},{10,14},{12,8},{14,10},{1,5},{3,7},... | collective-permute-start | bytes 196616 | tf_op jit(solution)/shard_map/ppermute | solution.py:84
  48.6 17.4 %collective-permute-start.2 = (bf16[512,128]{1,0:T(8,128)(2,1)S(1)}, bf16[512,128]{1,0:T(8,128)(2,1)S(1)}, u32[]{:S(2)}, u32[]{:S(2)}) collective-permute-start(bf16[512,128]{1,0:T(8,128)(2,1)S(1)} %maximum_select_fusion.1), channel_id=1, source_target_pairs={{0,8},{2,10},{4,12},{6,14},{8,0},{10,2},{12,4},{14,6},{1,9},{3,11}... | collective-permute-start | bytes 393224 | tf_op jit(solution)/shard_map/ppermute | solution.py:84
  92.4 4.2 %copy-start.2 = (f32[8192]{0:T(1024)S(1)}, f32[8192]{0:T(1024)}, u32[]{:S(2)}) copy-start(f32[8192]{0:T(1024)} %param.7) | copy-start | bytes 98308
  96.5 1.3 collective-permute-start.10
  97.8 4.3 %collective-permute-start.11 = (f32[128,128]{1,0:T(8,128)S(1)}, f32[128,128]{1,0:T(8,128)S(1)}, u32[]{:S(2)}, u32[]{:S(2)}) collective-permute-start(f32[128,128]{1,0:T(8,128)S(1)} %add.189), channel_id=1, source_target_pairs={{0,2},{2,0},{4,6},{6,4},{8,10},{10,8},{12,14},{14,12},{1,3},{3,1},... | collective-permute-start | bytes 196616 | tf_op jit(solution)/shard_map/ppermute | solution.py:98
  99.4 26.0 %collective-permute-start.4 = (bf16[128,1024]{0,1:T(8,128)(2,1)S(1)}, bf16[128,1024]{0,1:T(8,128)(2,1)S(1)}, u32[]{:S(2)}, u32[]{:S(2)}) collective-permute-start(bf16[128,1024]{0,1:T(8,128)(2,1)S(1)} %convert_bitcast_fusion), channel_id=1, source_target_pairs={{8,4},{12,8},{14,12},{10,14},{6,10},{2,6},{0,2},{4,0},{9,5},{13,9}... | collective-permute-start | bytes 786440 | tf_op jit(solution)/shard_map/ppermute | solution.py:150
  100.0 20.7 %collective-permute-start.3 = (bf16[128,1024]{0,1:T(8,128)(2,1)S(1)}, bf16[128,1024]{0,1:T(8,128)(2,1)S(1)}, u32[]{:S(2)}, u32[]{:S(2)}) collective-permute-start(bf16[128,1024]{0,1:T(8,128)(2,1)S(1)} %convert_bitcast_fusion), channel_id=1, source_target_pairs={{4,8},{8,12},{12,14},{14,10},{10,6},{6,2},{2,0},{0,4},{5,9},{9,13}... | collective-permute-start | bytes 786440 | tf_op jit(solution)/shard_map/ppermute | solution.py:147
  102.2 6.8 %collective-permute-start.12 = (f32[128,128]{1,0:T(8,128)S(1)}, f32[128,128]{1,0:T(8,128)S(1)}, u32[]{:S(2)}, u32[]{:S(2)}) collective-permute-start(f32[128,128]{1,0:T(8,128)S(1)} %add.190), channel_id=1, source_target_pairs={{0,4},{2,6},{4,0},{6,2},{8,12},{10,14},{12,8},{14,10},{1,5},{3,7},... | collective-permute-start | bytes 196616 | tf_op jit(solution)/shard_map/ppermute | solution.py:98
  109.0 5.2 %collective-permute-start.13 = (f32[128,128]{1,0:T(8,128)S(1)}, f32[128,128]{1,0:T(8,128)S(1)}, u32[]{:S(2)}, u32[]{:S(2)}) collective-permute-start(f32[128,128]{1,0:T(8,128)S(1)} %add.191), channel_id=1, source_target_pairs={{0,8},{2,10},{4,12},{6,14},{8,0},{10,2},{12,4},{14,6},{1,9},{3,11}... | collective-permute-start | bytes 196616 | tf_op jit(solution)/shard_map/ppermute | solution.py:98
  109.6 15.9 %copy-start = (bf16[128,8192]{1,0:T(8,128)(2,1)}, bf16[128,8192]{1,0:T(8,128)(2,1)S(1)}, u32[]{:S(2)}) copy-start(bf16[128,8192]{1,0:T(8,128)(2,1)S(1)} %constant_dynamic-update-slice_fusion.7) | copy-start | bytes 6291460
  120.7 8.1 %collective-permute-start.5 = (bf16[128,1024]{0,1:T(8,128)(2,1)S(1)}, bf16[128,1024]{0,1:T(8,128)(2,1)S(1)}, u32[]{:S(2)}, u32[]{:S(2)}) collective-permute-start(bf16[128,1024]{0,1:T(8,128)(2,1)S(1)} %collective-permute-done.3), channel_id=1, source_target_pairs={{4,8},{8,12},{12,14},{14,10},{10,6},{6,2},{2,0},{0,4},{5,9},{9,13}... | collective-permute-start | bytes 786440 | tf_op jit(solution)/shard_map/ppermute | solution.py:147
  127.0 6.4 %collective-permute-start.6 = (bf16[128,1024]{0,1:T(8,128)(2,1)S(1)}, bf16[128,1024]{0,1:T(8,128)(2,1)S(1)}, u32[]{:S(2)}, u32[]{:S(2)}) collective-permute-start(bf16[128,1024]{0,1:T(8,128)(2,1)S(1)} %collective-permute-done.4), channel_id=1, source_target_pairs={{8,4},{12,8},{14,12},{10,14},{6,10},{2,6},{0,2},{4,0},{9,5},{13,9}... | collective-permute-start | bytes 786440 | tf_op jit(solution)/shard_map/ppermute | solution.py:150
  128.8 8.0 %collective-permute-start.7 = (bf16[128,1024]{0,1:T(8,128)(2,1)S(1)}, bf16[128,1024]{0,1:T(8,128)(2,1)S(1)}, u32[]{:S(2)}, u32[]{:S(2)}) collective-permute-start(bf16[128,1024]{0,1:T(8,128)(2,1)S(1)} %collective-permute-done.5), channel_id=1, source_target_pairs={{4,8},{8,12},{12,14},{14,10},{10,6},{6,2},{2,0},{0,4},{5,9},{9,13}... | collective-permute-start | bytes 786440 | tf_op jit(solution)/shard_map/ppermute | solution.py:147
  135.1 6.4 %collective-permute-start.8 = (bf16[128,1024]{0,1:T(8,128)(2,1)S(1)}, bf16[128,1024]{0,1:T(8,128)(2,1)S(1)}, u32[]{:S(2)}, u32[]{:S(2)}) collective-permute-start(bf16[128,1024]{0,1:T(8,128)(2,1)S(1)} %collective-permute-done.6), channel_id=1, source_target_pairs={{8,4},{12,8},{14,12},{10,14},{6,10},{2,6},{0,2},{4,0},{9,5},{13,9}... | collective-permute-start | bytes 786440 | tf_op jit(solution)/shard_map/ppermute | solution.py:150
  136.8 7.7 %collective-permute-start.9 = (bf16[128,1024]{0,1:T(8,128)(2,1)S(1)}, bf16[128,1024]{0,1:T(8,128)(2,1)S(1)}, u32[]{:S(2)}, u32[]{:S(2)}) collective-permute-start(bf16[128,1024]{0,1:T(8,128)(2,1)S(1)} %collective-permute-done.7), channel_id=1, source_target_pairs={{4,8},{8,12},{12,14},{14,10},{10,6},{6,2},{2,0},{0,4},{5,9},{9,13}... | collective-permute-start | bytes 786440 | tf_op jit(solution)/shard_map/ppermute | solution.py:147

commit v3 on v2

--- a/solution.py
+++ b/solution.py
@@ -105,8 +105,9 @@
     width = design.shape[1]
     span = expression.shape[1] // n
     identity = jnp.eye(width, dtype=jnp.float32)
-    expression_genes = lax.all_to_all(expression, "cell", 1, 0, tiled=True)
     design_all = gather_rows(design, "cell")
+    sent = expression + (design_all[0, 0] * 0).astype(expression.dtype)
+    expression_genes = lax.all_to_all(sent, "cell", 1, 0, tiled=True)
     gram_total = lax.dot_general(
         design_all, design_all, (((0,), (0,)), ((), ())), preferred_element_type=jnp.float32
     )

time: 147 us -> 130 us (0.88)
  waiting for transfers between devices: 50.9 us -> 32.2 us
  matrix products: 22.6 us -> 17.1 us
  other arithmetic: 23.6 us -> 27.5 us
    ppermute x3, waiting for transfers between devices: 36 us -> 4.35 us  [gather_rows(): other = lax.ppermute(block, axis, pairs)]
    all_to_all x1, waiting for transfers between devices: 0.01 us -> 10.8 us  [per_device(): expression_genes = lax.all_to_all(sent, 'cell', 1, 0, tiled=True)]
    dot_general x8, matrix products: 10.5 us -> 6.72 us  [place(): fitted = jnp.dot(design, block, preferred_element_type=jnp.float32)]
    ppermute x3, waiting for transfers between devices: 3.18 us -> 4.83 us  [per_device(): behind = lax.ppermute(behind, 'cell', backward)]
    add x0 -> x1, other arithmetic: none -> 1.48 us  [per_device(): sent = expression + (design_all[0, 0] * 0).astype(expression.dtype)]
    unnamed x11 -> x21, local copies, waits for them, and re-layouts: 4.11 us -> 4.6 us
  transfers between devices with their start and end apart: 15 -> 15, of which waited for: 9 -> 9; matrix products, arithmetic and copies ran while one was open for 33% -> 38% of each run, Pallas kernels for 0% -> 0%
where the time goes in v3:
time: 130 us; the launch traced here: 129 us
  waiting for transfers between devices  32.2 us (25%)
  other arithmetic  27.5 us (21%)
  starting transfers between devices  25.2 us (19%)
  matrix products  17.1 us (13%)
  local copies, waits for them, and re-layouts  15.9 us (12%)
  between operations  11 us (8%)
    another operation x3, other arithmetic, invert(): factor = jnp.linalg.cholesky(matrix)  12.4 us
    ppermute x4, waiting for transfers between devices, butterfly_sum(): value = value + lax.ppermute(value, axis, pairs)  12.2 us
    all_to_all x1, waiting for transfers between devices, per_device(): expression_genes = lax.all_to_all(sent, 'cell', 1, 0, tiled=True)  10.8 us
    another operation x2, other arithmetic, invert(): lax.linalg.triangular_solve(factor, identity, left_side=True, lower=True)  10.5 us
    ppermute x3, starting transfers between devices, gather_rows(): other = lax.ppermute(block, axis, pairs)  8.3 us
    dot_general x26, matrix products, matmul(): return jnp.dot(left, right, precision=lax.Precision.HIGHEST)  8.1 us
    all_to_all x1, starting transfers between devices, per_device(): expression_genes = lax.all_to_all(sent, 'cell', 1, 0, tiled=True)  7.14 us
    ppermute x4, starting transfers between devices, per_device(): ahead = lax.ppermute(ahead, 'cell', forward)  6.82 us
  transfers between devices with their start and end apart: 15, of which 9 were waited for; matrix products, arithmetic and copies ran while one was open for 38% of the time, Pallas kernels for 0%

profile of v3, /device:TPU:0, one launch (start us, length us, event | category | flops | bytes accessed | tf_op | source)
XLA Modules:
  0.0 128.9 jit_solution(9972320449463768809)
XLA Ops:
  0.6 3.0 %collective-permute-start = (bf16[128,128]{1,0:T(8,128)(2,1)}, bf16[128,128]{1,0:T(8,128)(2,1)S(1)}, u32[]{:S(2)}, u32[]{:S(2)}) collective-permute-start(bf16[128,128]{1,0:T(8,128)(2,1)} %param.6), channel_id=1, source_target_pairs={{0,2},{2,0},{4,6},{6,4},{8,10},{10,8},{12,14},{14,12},{1,3},{3,1},... | collective-permute-start | bytes 98312 | tf_op jit(solution)/shard_map/ppermute | solution.py:84
  3.7 2.1 %collective-permute-done = bf16[128,128]{1,0:T(8,128)(2,1)S(1)} collective-permute-done((bf16[128,128]{1,0:T(8,128)(2,1)}, bf16[128,128]{1,0:T(8,128)(2,1)S(1)}, u32[]{:S(2)}, u32[]{:S(2)}) %collective-permute-start) | collective-permute-done | bytes 32800 | tf_op jit(solution)/shard_map/ppermute | solution.py:84
  5.8 0.9 maximum_select_fusion.2
  6.6 2.2 %collective-permute-start.1 = (bf16[256,128]{1,0:T(8,128)(2,1)S(1)}, bf16[256,128]{1,0:T(8,128)(2,1)S(1)}, u32[]{:S(2)}, u32[]{:S(2)}) collective-permute-start(bf16[256,128]{1,0:T(8,128)(2,1)S(1)} %maximum_select_fusion.2), channel_id=1, source_target_pairs={{0,4},{2,6},{4,0},{6,2},{8,12},{10,14},{12,8},{14,10},{1,5},{3,7},... | collective-permute-start | bytes 196616 | tf_op jit(solution)/shard_map/ppermute | solution.py:84
  8.8 2.2 %collective-permute-done.1 = bf16[256,128]{1,0:T(8,128)(2,1)S(1)} collective-permute-done((bf16[256,128]{1,0:T(8,128)(2,1)S(1)}, bf16[256,128]{1,0:T(8,128)(2,1)S(1)}, u32[]{:S(2)}, u32[]{:S(2)}) %collective-permute-start.1) | collective-permute-done | bytes 65568 | tf_op jit(solution)/shard_map/ppermute | solution.py:84
  11.1 3.1 %collective-permute-start.2 = (bf16[512,128]{1,0:T(8,128)(2,1)S(1)}, bf16[512,128]{1,0:T(8,128)(2,1)S(1)}, u32[]{:S(2)}, u32[]{:S(2)}) collective-permute-start(bf16[512,128]{1,0:T(8,128)(2,1)S(1)} %maximum_select_fusion.1), channel_id=1, source_target_pairs={{0,8},{2,10},{4,12},{6,14},{8,0},{10,2},{12,4},{14,6},{1,9},{3,11}... | collective-permute-start | bytes 393224 | tf_op jit(solution)/shard_map/ppermute | solution.py:84
  14.2 3.2 %copy.41 = bf16[128,8192]{0,1:T(8,128)(2,1)S(1)} copy(bf16[128,8192]{1,0:T(8,128)(2,1)} %param.5) | data formatting | bytes 4194304 | tf_op args[0]
  17.5 0.6 slice.14
  18.8 1.5 %broadcast_add_fusion = bf16[128,8192]{0,1:T(8,128)(2,1)} fusion(bf16[128,8192]{0,1:T(8,128)(2,1)S(1)} %copy.41, bf16[]{:T(256)} %bitcast), kind=kLoop, calls=%fused_computation.34 | loop fusion | flops 1048576 | bytes 4194306 | tf_op jit(solution)/shard_map/add | solution.py:109
  20.3 7.1 %all-to-all-start = ((bf16[128,8,1024]{0,2,1:T(8,128)(2,1)}), bf16[128,8,1024]{0,2,1:T(8,128)(2,1)S(1)}, u32[]{:S(2)}, u32[]{:S(2)}) async-start(bf16[128,8,1024]{0,2,1:T(8,128)(2,1)} %bitcast.150), calls=%async_computation | async-start | bytes 4194304 | tf_op jit(solution)/shard_map/all_to_all | solution.py:110
  27.4 0.6 dynamic_slice.74
  32.7 0.7 fusion.25
  37.8 0.3 fusion.27
  38.2 11.7 %cholesky.29 = f32[128,128]{1,0:T(8,128)S(1)} custom-call(f32[128,128]{1,0:T(8,128)S(1)} %fusion.22), custom_call_target="Cholesky" | custom-call | tf_op jit(solution)/shard_map/jit(cholesky)/cholesky | solution.py:21
  50.0 0.6 compare_reduce_fusion
  50.6 0.7 fusion.18
  51.3 9.8 %custom-call.6 = f32[1,128,128]{1,2,0:T(8,128)S(1)} custom-call(f32[1,128,128]{2,1,0:T(8,128)S(1)} %fusion.18), custom_call_target="InvertDiagBlocksLowerTriangular" | custom-call | tf_op jit(solution)/shard_map/triangular_solve | solution.py:22
  61.1 0.2 fusion.19
  61.4 0.3 fusion.28
  61.7 10.8 %all-to-all-done = bf16[128,8,1024]{0,2,1:T(8,128)(2,1)S(1)} async-done(((bf16[128,8,1024]{0,2,1:T(8,128)(2,1)}), bf16[128,8,1024]{0,2,1:T(8,128)(2,1)S(1)}, u32[]{:S(2)}, u32[]{:S(2)}) %all-to-all-start) | async-done | bytes 2097184 | tf_op jit(solution)/shard_map/all_to_all | solution.py:110
  72.4 1.3 %copy-done.2 = bf16[128,8,1024]{0,2,1:T(8,128)(2,1)} copy-done((bf16[128,8,1024]{0,2,1:T(8,128)(2,1)}, bf16[128,8,1024]{0,2,1:T(8,128)(2,1)S(1)}, u32[]{:S(2)}) %copy-start.2) | copy-done | bytes 2097176
  73.8 2.9 %copy.43 = bf16[8,128,1024]{2,1,0:T(8,128)(2,1)S(1)} copy(bf16[8,128,1024]{1,2,0:T(8,128)(2,1)} %bitcast.149) | data formatting | bytes 4194304 | tf_op jit(solution)/shard_map/all_to_all | solution.py:110
  76.6 0.7 fusion.26
  77.4 0.6 fusion.29
  78.0 1.0 fusion.30
  79.1 0.6 broadcast_add_fusion.1
  79.7 0.6 collective-permute-done.10
  80.3 1.3 %collective-permute-start.11 = (f32[128,128]{1,0:T(8,128)S(1)}, f32[128,128]{1,0:T(8,128)S(1)}, u32[]{:S(2)}, u32[]{:S(2)}) collective-permute-start(f32[128,128]{1,0:T(8,128)S(1)} %add.197), channel_id=1, source_target_pairs={{0,2},{2,0},{4,6},{6,4},{8,10},{10,8},{12,14},{14,12},{1,3},{3,1},... | collective-permute-start | bytes 196616 | tf_op jit(solution)/shard_map/ppermute | solution.py:98
  81.7 0.8 collective-permute-start.4
  82.5 1.3 collective-permute-start.3
  83.8 0.9 collective-permute-done.11
  84.8 0.4 subtract_convert_fusion.7
  85.3 6.1 %collective-permute-done.12 = f32[128,128]{1,0:T(8,128)} collective-permute-done((f32[128,128]{1,0:T(8,128)S(1)}, f32[128,128]{1,0:T(8,128)}, u32[]{:S(2)}, u32[]{:S(2)}) %collective-permute-start.12) | collective-permute-done | bytes 65568 | tf_op jit(solution)/shard_map/ppermute | solution.py:98
  91.3 0.8 add.199
  92.2 0.3 collective-permute-start.13
  92.8 4.7 %collective-permute-done.13 = f32[128,128]{1,0:T(8,128)S(1)} collective-permute-done((f32[128,128]{1,0:T(8,128)S(1)}, f32[128,128]{1,0:T(8,128)S(1)}, u32[]{:S(2)}, u32[]{:S(2)}) %collective-permute-start.13) | collective-permute-done | bytes 65568 | tf_op jit(solution)/shard_map/ppermute | solution.py:98
  97.4 0.7 select_reduce_fusion
  98.1 0.8 fusion.16
  98.9 0.8 fusion.24
  99.9 0.2 fusion.15
  101.8 0.2 fusion.12
  103.1 0.2 fusion.10
  103.8 0.2 fusion.9
  104.0 1.8 %collective-permute-start.5 = (bf16[128,1024]{0,1:T(8,128)(2,1)}, bf16[128,1024]{0,1:T(8,128)(2,1)}, u32[]{:S(2)}, u32[]{:S(2)}) collective-permute-start(bf16[128,1024]{0,1:T(8,128)(2,1)} %collective-permute-done.3), channel_id=1, source_target_pairs={{4,8},{8,12},{12,14},{14,10},{10,6},{6,2},{2,0},{0,4},{5,9},{9,13}... | collective-permute-start | bytes 786440 | tf_op jit(solution)/shard_map/ppermute | solution.py:148
  105.8 1.3 %subtract_convert_fusion.6 = bf16[128,1024]{0,1:T(8,128)(2,1)S(1)} fusion(bf16[128,1024]{0,1:T(8,128)(2,1)} %collective-permute-done.3, bf16[128,128]{1,0:T(8,128)(2,1)S(1)} %copy-done.4, f32[1024]{0:T(1024)S(1)} %copy-done.7, f32[1024]{0:T(1024)S(1)} %copy-done.8, bf16[128,8192]{0,1:T(8,128)(2,1)S(1)} %copy-done.1, s32[]{:T(128)S(6)} %select_n.139), kind=kOutput, calls=%fused_computation.41 | convolution fusion | flops 34340864 | bytes 827396 | tf_op jit(solution)/shard_map/dot_general | solution.py:138
  107.3 1.4 %fusion.8 = f32[1024,128]{1,0:T(8,128)} fusion(f32[1024,128]{1,0:T(8,128)S(1)} %fusion.29, f32[128,128]{1,0:T(8,128)S(1)} %fusion.43), kind=kOutput, calls=%fused_computation.17 | convolution fusion | flops 201588736 | bytes 1114112 | tf_op jit(solution)/shard_map/dot_general | solution.py:16
  108.7 1.3 %subtract_convert_fusion.5 = bf16[128,1024]{0,1:T(8,128)(2,1)S(1)} fusion(bf16[128,1024]{0,1:T(8,128)(2,1)} %collective-permute-done.4, bf16[128,128]{1,0:T(8,128)(2,1)S(1)} %copy-done.4, f32[1024]{0:T(1024)S(1)} %get-tuple-element.26, f32[1024]{0:T(1024)S(1)} %get-tuple-element.27, bf16[128,8192]{0,1:T(8,128)(2,1)S(1)} %copy-done.1, s32[]{:T(128)S(6)} %select_n.142), kind=kOutput, calls=%fused_computation.40 | convolution fusion | flops 34340864 | bytes 827396 | tf_op jit(solution)/shard_map/dot_general | solution.py:138
  110.3 0.3 collective-permute-start.6
  110.7 0.7 constant_dynamic-update-slice_fusion.6
  111.4 0.7 constant_dynamic-update-slice_fusion.5
  112.1 1.8 %collective-permute-start.7 = (bf16[128,1024]{0,1:T(8,128)(2,1)}, bf16[128,1024]{0,1:T(8,128)(2,1)S(1)}, u32[]{:S(2)}, u32[]{:S(2)}) collective-permute-start(bf16[128,1024]{0,1:T(8,128)(2,1)} %collective-permute-done.5), channel_id=1, source_target_pairs={{4,8},{8,12},{12,14},{14,10},{10,6},{6,2},{2,0},{0,4},{5,9},{9,13}... | collective-permute-start | bytes 786440 | tf_op jit(solution)/shard_map/ppermute | solution.py:148
  113.9 1.3 %subtract_convert_fusion.4 = bf16[128,1024]{0,1:T(8,128)(2,1)S(1)} fusion(bf16[128,1024]{0,1:T(8,128)(2,1)} %collective-permute-done.5, bf16[128,128]{1,0:T(8,128)(2,1)S(1)} %copy-done.4, f32[1024]{0:T(1024)S(1)} %get-tuple-element.24, f32[1024]{0:T(1024)S(1)} %get-tuple-element.25, bf16[128,8192]{0,1:T(8,128)(2,1)S(1)} %copy-done.1, s32[]{:T(128)S(6)} %select_n.145), kind=kOutput, calls=%fused_computation.39 | convolution fusion | flops 34340864 | bytes 827396 | tf_op jit(solution)/shard_map/dot_general | solution.py:138
  115.2 2.3 %collective-permute-done.6 = bf16[128,1024]{0,1:T(8,128)(2,1)S(1)} collective-permute-done((bf16[128,1024]{0,1:T(8,128)(2,1)}, bf16[128,1024]{0,1:T(8,128)(2,1)S(1)}, u32[]{:S(2)}, u32[]{:S(2)}) %collective-permute-start.6) | collective-permute-done | bytes 262176 | tf_op jit(solution)/shard_map/ppermute | solution.py:151
  117.5 0.4 subtract_convert_fusion.3
  118.2 0.7 constant_dynamic-update-slice_fusion.4
  119.0 0.7 constant_dynamic-update-slice_fusion.3
  119.7 2.0 %collective-permute-start.9 = (bf16[128,1024]{0,1:T(8,128)(2,1)S(1)}, bf16[128,1024]{0,1:T(8,128)(2,1)}, u32[]{:S(2)}, u32[]{:S(2)}) collective-permute-start(bf16[128,1024]{0,1:T(8,128)(2,1)S(1)} %collective-permute-done.7), channel_id=1, source_target_pairs={{4,8},{8,12},{12,14},{14,10},{10,6},{6,2},{2,0},{0,4},{5,9},{9,13}... | collective-permute-start | bytes 786440 | tf_op jit(solution)/shard_map/ppermute | solution.py:148
  121.7 0.4 subtract_convert_fusion.2
  122.1 2.5 %collective-permute-done.8 = bf16[128,1024]{0,1:T(8,128)(2,1)S(1)} collective-permute-done((bf16[128,1024]{0,1:T(8,128)(2,1)S(1)}, bf16[128,1024]{0,1:T(8,128)(2,1)S(1)}, u32[]{:S(2)}, u32[]{:S(2)}) %collective-permute-start.8) | collective-permute-done | bytes 262176 | tf_op jit(solution)/shard_map/ppermute | solution.py:151
  124.6 0.4 subtract_convert_fusion.1
  125.3 0.7 constant_dynamic-update-slice_fusion.2
  126.0 0.7 constant_dynamic-update-slice_fusion.1
  126.7 1.3 %subtract_convert_fusion = bf16[128,1024]{0,1:T(8,128)(2,1)S(1)} fusion(bf16[128,1024]{0,1:T(8,128)(2,1)} %collective-permute-done.9, bf16[128,128]{1,0:T(8,128)(2,1)S(1)} %copy-done.4, f32[1024]{0:T(1024)S(1)} %get-tuple-element.4, f32[1024]{0:T(1024)S(1)} %get-tuple-element.5, bf16[128,8192]{0,1:T(8,128)(2,1)S(1)} %copy-done.1, s32[]{:T(128)S(6)} %select_n.157), kind=kOutput, calls=%fused_computation.35 | convolution fusion | flops 34340864 | bytes 827396 | tf_op jit(solution)/shard_map/dot_general | solution.py:138
  128.2 0.7 constant_dynamic-update-slice_fusion
  (63 shorter events, 5.4 us)
Async XLA Ops:
  0.6 5.1 %collective-permute-start = (bf16[128,128]{1,0:T(8,128)(2,1)}, bf16[128,128]{1,0:T(8,128)(2,1)S(1)}, u32[]{:S(2)}, u32[]{:S(2)}) collective-permute-start(bf16[128,128]{1,0:T(8,128)(2,1)} %param.6), channel_id=1, source_target_pairs={{0,2},{2,0},{4,6},{6,4},{8,10},{10,8},{12,14},{14,12},{1,3},{3,1},... | collective-permute-start | bytes 98312 | tf_op jit(solution)/shard_map/ppermute | solution.py:84
  6.6 4.4 %collective-permute-start.1 = (bf16[256,128]{1,0:T(8,128)(2,1)S(1)}, bf16[256,128]{1,0:T(8,128)(2,1)S(1)}, u32[]{:S(2)}, u32[]{:S(2)}) collective-permute-start(bf16[256,128]{1,0:T(8,128)(2,1)S(1)} %maximum_select_fusion.2), channel_id=1, source_target_pairs={{0,4},{2,6},{4,0},{6,2},{8,12},{10,14},{12,8},{14,10},{1,5},{3,7},... | collective-permute-start | bytes 196616 | tf_op jit(solution)/shard_map/ppermute | solution.py:84
  11.1 6.3 %collective-permute-start.2 = (bf16[512,128]{1,0:T(8,128)(2,1)S(1)}, bf16[512,128]{1,0:T(8,128)(2,1)S(1)}, u32[]{:S(2)}, u32[]{:S(2)}) collective-permute-start(bf16[512,128]{1,0:T(8,128)(2,1)S(1)} %maximum_select_fusion.1), channel_id=1, source_target_pairs={{0,8},{2,10},{4,12},{6,14},{8,0},{10,2},{12,4},{14,6},{1,9},{3,11}... | collective-permute-start | bytes 393224 | tf_op jit(solution)/shard_map/ppermute | solution.py:84
  17.4 2.9 %copy-start = (bf16[128,8192]{0,1:T(8,128)(2,1)}, bf16[128,8192]{0,1:T(8,128)(2,1)S(1)}, u32[]{:S(2)}) copy-start(bf16[128,8192]{0,1:T(8,128)(2,1)S(1)} %copy.41) | copy-start | bytes 6291460
  20.3 7.1 %copy-start.9 = (s32[8]{0:T(128)S(1)}, s32[8]{0:T(128)}, u32[]{:S(2)}) copy-start(s32[8]{0:T(128)} %constant.152.clone) | copy-start | bytes 100
  20.3 12.4 %copy-start.6 = (s32[8]{0:T(128)S(1)}, s32[8]{0:T(128)}, u32[]{:S(2)}) copy-start(s32[8]{0:T(128)} %constant.151.clone) | copy-start | bytes 100
  20.3 52.2 %all-to-all-start = ((bf16[128,8,1024]{0,2,1:T(8,128)(2,1)}), bf16[128,8,1024]{0,2,1:T(8,128)(2,1)S(1)}, u32[]{:S(2)}, u32[]{:S(2)}) async-start(bf16[128,8,1024]{0,2,1:T(8,128)(2,1)} %bitcast.150), calls=%async_computation | async-start | bytes 4194304 | tf_op jit(solution)/shard_map/all_to_all | solution.py:110
  72.4 1.3 %copy-start.2 = (bf16[128,8,1024]{0,2,1:T(8,128)(2,1)}, bf16[128,8,1024]{0,2,1:T(8,128)(2,1)S(1)}, u32[]{:S(2)}) copy-start(bf16[128,8,1024]{0,2,1:T(8,128)(2,1)S(1)} %all-to-all-done) | copy-start | bytes 6291460
  77.4 1.7 %copy-start.5 = (f32[8192]{0:T(1024)S(1)}, f32[8192]{0:T(1024)}, u32[]{:S(2)}) copy-start(f32[8192]{0:T(1024)} %param.7) | copy-start | bytes 98308
  77.4 7.4 %copy-start.1 = (bf16[128,8192]{0,1:T(8,128)(2,1)S(1)}, bf16[128,8192]{0,1:T(8,128)(2,1)}, u32[]{:S(2)}) copy-start(bf16[128,8192]{0,1:T(8,128)(2,1)} %copy-done) | copy-start | bytes 6291460
  77.4 7.4 %copy-start.4 = (bf16[128,128]{1,0:T(8,128)(2,1)S(1)}, bf16[128,128]{1,0:T(8,128)(2,1)}, u32[]{:S(2)}) copy-start(bf16[128,128]{1,0:T(8,128)(2,1)} %param.6) | copy-start | bytes 98308
  79.0 1.3 %collective-permute-start.10 = (f32[128,128]{1,0:T(8,128)S(1)}, f32[128,128]{1,0:T(8,128)S(1)}, u32[]{:S(2)}, u32[]{:S(2)}) collective-permute-start(f32[128,128]{1,0:T(8,128)S(1)} %fusion.30), channel_id=1, source_target_pairs={{0,1},{1,0},{2,3},{3,2},{4,5},{5,4},{6,7},{7,6},{8,9},{9,8},{10,11... | collective-permute-start | bytes 196616 | tf_op jit(solution)/shard_map/ppermute | solution.py:98
  80.3 4.3 %collective-permute-start.11 = (f32[128,128]{1,0:T(8,128)S(1)}, f32[128,128]{1,0:T(8,128)S(1)}, u32[]{:S(2)}, u32[]{:S(2)}) collective-permute-start(f32[128,128]{1,0:T(8,128)S(1)} %add.197), channel_id=1, source_target_pairs={{0,2},{2,0},{4,6},{6,4},{8,10},{10,8},{12,14},{14,12},{1,3},{3,1},... | collective-permute-start | bytes 196616 | tf_op jit(solution)/shard_map/ppermute | solution.py:98
  81.7 27.0 %collective-permute-start.4 = (bf16[128,1024]{0,1:T(8,128)(2,1)S(1)}, bf16[128,1024]{0,1:T(8,128)(2,1)}, u32[]{:S(2)}, u32[]{:S(2)}) collective-permute-start(bf16[128,1024]{0,1:T(8,128)(2,1)S(1)} %convert_bitcast_fusion), channel_id=1, source_target_pairs={{8,4},{12,8},{14,12},{10,14},{6,10},{2,6},{0,2},{4,0},{9,5},{13,9}... | collective-permute-start | bytes 786440 | tf_op jit(solution)/shard_map/ppermute | solution.py:151
  82.5 21.5 %collective-permute-start.3 = (bf16[128,1024]{0,1:T(8,128)(2,1)S(1)}, bf16[128,1024]{0,1:T(8,128)(2,1)}, u32[]{:S(2)}, u32[]{:S(2)}) collective-permute-start(bf16[128,1024]{0,1:T(8,128)(2,1)S(1)} %convert_bitcast_fusion), channel_id=1, source_target_pairs={{4,8},{8,12},{12,14},{14,10},{10,6},{6,2},{2,0},{0,4},{5,9},{9,13}... | collective-permute-start | bytes 786440 | tf_op jit(solution)/shard_map/ppermute | solution.py:148
  84.7 6.7 %collective-permute-start.12 = (f32[128,128]{1,0:T(8,128)S(1)}, f32[128,128]{1,0:T(8,128)}, u32[]{:S(2)}, u32[]{:S(2)}) collective-permute-start(f32[128,128]{1,0:T(8,128)S(1)} %add.198), channel_id=1, source_target_pairs={{0,4},{2,6},{4,0},{6,2},{8,12},{10,14},{12,8},{14,10},{1,5},{3,7},... | collective-permute-start | bytes 196616 | tf_op jit(solution)/shard_map/ppermute | solution.py:98
  92.2 5.2 %collective-permute-start.13 = (f32[128,128]{1,0:T(8,128)S(1)}, f32[128,128]{1,0:T(8,128)S(1)}, u32[]{:S(2)}, u32[]{:S(2)}) collective-permute-start(f32[128,128]{1,0:T(8,128)S(1)} %add.199), channel_id=1, source_target_pairs={{0,8},{2,10},{4,12},{6,14},{8,0},{10,2},{12,4},{14,6},{1,9},{3,11}... | collective-permute-start | bytes 196616 | tf_op jit(solution)/shard_map/ppermute | solution.py:98
  92.7 10.8 %copy-start.3 = (bf16[128,8192]{1,0:T(8,128)(2,1)}, bf16[128,8192]{1,0:T(8,128)(2,1)S(1)}, u32[]{:S(2)}) copy-start(bf16[128,8192]{1,0:T(8,128)(2,1)S(1)} %constant_dynamic-update-slice_fusion.7) | copy-start | bytes 6291460
  98.9 6.9 %copy-start.7 = (f32[1024]{0:T(1024)S(1)}, f32[1024]{0:T(1024)}, u32[]{:S(2)}) copy-start(f32[1024]{0:T(1024)} %get-tuple-element.28) | copy-start | bytes 12292
  98.9 6.9 %copy-start.8 = (f32[1024]{0:T(1024)S(1)}, f32[1024]{0:T(1024)}, u32[]{:S(2)}) copy-start(f32[1024]{0:T(1024)} %get-tuple-element.29) | copy-start | bytes 12292
  104.0 8.1 %collective-permute-start.5 = (bf16[128,1024]{0,1:T(8,128)(2,1)}, bf16[128,1024]{0,1:T(8,128)(2,1)}, u32[]{:S(2)}, u32[]{:S(2)}) collective-permute-start(bf16[128,1024]{0,1:T(8,128)(2,1)} %collective-permute-done.3), channel_id=1, source_target_pairs={{4,8},{8,12},{12,14},{14,10},{10,6},{6,2},{2,0},{0,4},{5,9},{9,13}... | collective-permute-start | bytes 786440 | tf_op jit(solution)/shard_map/ppermute | solution.py:148
  110.3 7.2 %collective-permute-start.6 = (bf16[128,1024]{0,1:T(8,128)(2,1)}, bf16[128,1024]{0,1:T(8,128)(2,1)S(1)}, u32[]{:S(2)}, u32[]{:S(2)}) collective-permute-start(bf16[128,1024]{0,1:T(8,128)(2,1)} %collective-permute-done.4), channel_id=1, source_target_pairs={{8,4},{12,8},{14,12},{10,14},{6,10},{2,6},{0,2},{4,0},{9,5},{13,9}... | collective-permute-start | bytes 786440 | tf_op jit(solution)/shard_map/ppermute | solution.py:151
  112.1 7.6 %collective-permute-start.7 = (bf16[128,1024]{0,1:T(8,128)(2,1)}, bf16[128,1024]{0,1:T(8,128)(2,1)S(1)}, u32[]{:S(2)}, u32[]{:S(2)}) collective-permute-start(bf16[128,1024]{0,1:T(8,128)(2,1)} %collective-permute-done.5), channel_id=1, source_target_pairs={{4,8},{8,12},{12,14},{14,10},{10,6},{6,2},{2,0},{0,4},{5,9},{9,13}... | collective-permute-start | bytes 786440 | tf_op jit(solution)/shard_map/ppermute | solution.py:148
  118.2 6.4 %collective-permute-start.8 = (bf16[128,1024]{0,1:T(8,128)(2,1)S(1)}, bf16[128,1024]{0,1:T(8,128)(2,1)S(1)}, u32[]{:S(2)}, u32[]{:S(2)}) collective-permute-start(bf16[128,1024]{0,1:T(8,128)(2,1)S(1)} %collective-permute-done.6), channel_id=1, source_target_pairs={{8,4},{12,8},{14,12},{10,14},{6,10},{2,6},{0,2},{4,0},{9,5},{13,9}... | collective-permute-start | bytes 786440 | tf_op jit(solution)/shard_map/ppermute | solution.py:151
  119.7 7.0 %collective-permute-start.9 = (bf16[128,1024]{0,1:T(8,128)(2,1)S(1)}, bf16[128,1024]{0,1:T(8,128)(2,1)}, u32[]{:S(2)}, u32[]{:S(2)}) collective-permute-start(bf16[128,1024]{0,1:T(8,128)(2,1)S(1)} %collective-permute-done.7), channel_id=1, source_target_pairs={{4,8},{8,12},{12,14},{14,10},{10,6},{6,2},{2,0},{0,4},{5,9},{9,13}... | collective-permute-start | bytes 786440 | tf_op jit(solution)/shard_map/ppermute | solution.py:148

commit v4 on v3

--- a/solution.py
+++ b/solution.py
@@ -73,19 +73,15 @@
     return order
 
 
-def gather_rows(block, axis):
+def gather_blocks(block, axis):
     n = lax.axis_size(axis)
-    if n & (n - 1):
-        return lax.all_gather(block, axis, axis=0, tiled=True)
     me = lax.axis_index(axis)
-    bit = 1
-    while bit < n:
-        pairs = [(i, i ^ bit) for i in range(n)]
-        other = lax.ppermute(block, axis, pairs)
-        low = (me & bit) == 0
-        block = jnp.where(low, jnp.concatenate([block, other]), jnp.concatenate([other, block]))
-        bit *= 2
-    return block
+    received = [block]
+    for shift in range(1, n):
+        pairs = [(i, (i + shift) % n) for i in range(n)]
+        received.append(lax.ppermute(block, axis, pairs))
+    stacked = jnp.stack(received)
+    return jnp.take(stacked, (me - jnp.arange(n)) % n, axis=0)
 
 
 def butterfly_sum(value, axis):
@@ -105,7 +101,7 @@
     width = design.shape[1]
     span = expression.shape[1] // n
     identity = jnp.eye(width, dtype=jnp.float32)
-    design_all = gather_rows(design, "cell")
+    design_all = gather_blocks(design, "cell").reshape(-1, width)
     sent = expression + (design_all[0, 0] * 0).astype(expression.dtype)
     expression_genes = lax.all_to_all(sent, "cell", 1, 0, tiled=True)
     gram_total = lax.dot_general(
@@ -119,7 +115,8 @@
     local_moment = lax.dot_general(
         coef, coef, (((0,), (0,)), ((), ())), precision=lax.Precision.HIGHEST
     )
-    moment = butterfly_sum(butterfly_sum(local_moment, "gene"), "cell")
+    chip_moment = butterfly_sum(local_moment, "gene")
+    moment = jnp.sum(gather_blocks(chip_moment, "cell"), axis=0)
     root_inv = newton(moment)
     low_rank_coef = coef - shrink_rate / math.sqrt(width) * matmul(coef, root_inv)
     coef_low_t = coef.astype(jnp.bfloat16).T

time: 130 us -> 165 us (1.27)
  waiting for transfers between devices: 32.2 us -> 49.3 us
  local copies, waits for them, and re-layouts: 15.9 us -> 30.2 us
  starting transfers between devices: 25.2 us -> 27.7 us
    ppermute x3 -> x14, waiting for transfers between devices: 4.35 us -> 29 us  [gather_blocks(): received.append(lax.ppermute(block, axis, pairs))]
    ppermute x4 -> x1, waiting for transfers between devices: 12.2 us -> 0.87 us  [butterfly_sum(): value = value + lax.ppermute(value, axis, pairs)]
    ppermute x3 -> x14, starting transfers between devices: 8.3 us -> 16.8 us  [gather_blocks(): received.append(lax.ppermute(block, axis, pairs))]
    ppermute x4, waiting for transfers between devices: 0.01 us -> 7.9 us  [per_device(): ahead = lax.ppermute(ahead, 'cell', forward)]
    ppermute x4, starting transfers between devices: 6.82 us -> 1.28 us  [per_device(): ahead = lax.ppermute(ahead, 'cell', forward)]
    all_to_all x1 -> x2, local copies, waits for them, and re-layouts: 2.85 us -> 7.81 us  [per_device(): expression_genes = lax.all_to_all(sent, 'cell', 1, 0, tiled=True)]
    unnamed x21 -> x32, local copies, waits for them, and re-layouts: 4.6 us -> 8.62 us
    ppermute x3, starting transfers between devices: 1.19 us -> 5.07 us  [per_device(): behind = lax.ppermute(behind, 'cell', backward)]
  transfers between devices with their start and end apart: 15 -> 23, of which waited for: 9 -> 15; matrix products, arithmetic and copies ran while one was open for 38% -> 36% of each run, Pallas kernels for 0% -> 0%
where the time goes in v4:
time: 165 us; the launch traced here: 164 us
  waiting for transfers between devices  49.3 us (30%)
  local copies, waits for them, and re-layouts  30.2 us (18%)
  other arithmetic  27.9 us (17%)
  starting transfers between devices  27.7 us (17%)
  matrix products  16.9 us (10%)
  between operations  11.7 us (7%)
    ppermute x14, waiting for transfers between devices, gather_blocks(): received.append(lax.ppermute(block, axis, pairs))  29 us
    ppermute x14, starting transfers between devices, gather_blocks(): received.append(lax.ppermute(block, axis, pairs))  16.8 us
    another operation x3, other arithmetic, invert(): factor = jnp.linalg.cholesky(matrix)  12.4 us
    another operation x2, other arithmetic, invert(): lax.linalg.triangular_solve(factor, identity, left_side=True, lower=True)  10.5 us
    all_to_all x1, waiting for transfers between devices, per_device(): expression_genes = lax.all_to_all(sent, 'cell', 1, 0, tiled=True)  9.38 us
    unnamed x32, local copies, waits for them, and re-layouts  8.62 us
    dot_general x26, matrix products, matmul(): return jnp.dot(left, right, precision=lax.Precision.HIGHEST)  8.15 us
    ppermute x4, waiting for transfers between devices, per_device(): ahead = lax.ppermute(ahead, 'cell', forward)  7.9 us
  transfers between devices with their start and end apart: 23, of which 15 were waited for; matrix products, arithmetic and copies ran while one was open for 36% of the time, Pallas kernels for 0%

profile of v4, /device:TPU:0, one launch (start us, length us, event | category | flops | bytes accessed | tf_op | source)
XLA Modules:
  0.0 163.7 jit_solution(11076976861056799472)
XLA Ops:
  0.6 6.1 %collective-permute-start.6 = (bf16[128,128]{1,0:T(8,128)(2,1)}, bf16[128,128]{1,0:T(8,128)(2,1)S(1)}, u32[]{:S(2)}, u32[]{:S(2)}) collective-permute-start(bf16[128,128]{1,0:T(8,128)(2,1)} %param.6), channel_id=1, source_target_pairs={{0,14},{2,0},{4,2},{6,4},{8,6},{10,8},{12,10},{14,12},{1,15},{3,1}... | collective-permute-start | bytes 98312 | tf_op jit(solution)/shard_map/ppermute | solution.py:82
  7.1 3.0 %collective-permute-start.3 = (bf16[128,128]{1,0:T(8,128)(2,1)}, bf16[128,128]{1,0:T(8,128)(2,1)S(1)}, u32[]{:S(2)}, u32[]{:S(2)}) collective-permute-start(bf16[128,128]{1,0:T(8,128)(2,1)} %param.6), channel_id=1, source_target_pairs={{0,8},{2,10},{4,12},{6,14},{8,0},{10,2},{12,4},{14,6},{1,9},{3,11}... | collective-permute-start | bytes 98312 | tf_op jit(solution)/shard_map/ppermute | solution.py:82
  10.1 1.5 collective-permute-start
  11.7 0.8 constant_dynamic-update-slice_fusion.7
  13.1 3.2 %copy.43 = bf16[128,8192]{0,1:T(8,128)(2,1)S(1)} copy(bf16[128,8192]{1,0:T(8,128)(2,1)} %param.5) | data formatting | bytes 4194304 | tf_op args[0]
  16.3 0.7 collective-permute-done
  17.0 5.7 %collective-permute-done.1 = bf16[128,128]{1,0:T(8,128)(2,1)S(1)} collective-permute-done((bf16[128,128]{1,0:T(8,128)(2,1)S(1)}, bf16[128,128]{1,0:T(8,128)(2,1)S(1)}, u32[]{:S(2)}, u32[]{:S(2)}) %collective-permute-start.1) | collective-permute-done | bytes 32800 | tf_op jit(solution)/shard_map/ppermute | solution.py:82
  22.7 5.7 %collective-permute-done.2 = bf16[128,128]{1,0:T(8,128)(2,1)S(1)} collective-permute-done((bf16[128,128]{1,0:T(8,128)(2,1)S(1)}, bf16[128,128]{1,0:T(8,128)(2,1)S(1)}, u32[]{:S(2)}, u32[]{:S(2)}) %collective-permute-start.2) | collective-permute-done | bytes 32800 | tf_op jit(solution)/shard_map/ppermute | solution.py:82
  30.9 1.5 broadcast_add_fusion
  32.4 3.9 %copy.45 = bf16[128,8,1024]{2,0,1:T(8,128)(2,1)} copy(bf16[128,8,1024]{0,2,1:T(8,128)(2,1)} %bitcast.190) | data formatting | bytes 4194304 | tf_op jit(solution)/shard_map/all_to_all | solution.py:106
  36.3 4.5 %all-to-all-start = ((bf16[128,8,1024]{2,0,1:T(8,128)(2,1)}), bf16[128,8,1024]{2,0,1:T(8,128)(2,1)}, u32[]{:S(2)}, u32[]{:S(2)}) async-start(bf16[128,8,1024]{2,0,1:T(8,128)(2,1)} %copy.45), calls=%async_computation | async-start | bytes 4194304 | tf_op jit(solution)/shard_map/all_to_all | solution.py:106
  46.1 0.7 fusion.35
  51.3 0.6 broadcast_add_fusion.1
  52.4 11.7 %cholesky.29 = f32[128,128]{1,0:T(8,128)S(1)} custom-call(f32[128,128]{1,0:T(8,128)S(1)} %fusion.27), custom_call_target="Cholesky" | custom-call | tf_op jit(solution)/shard_map/jit(cholesky)/cholesky | solution.py:21
  64.2 0.6 compare_reduce_fusion
  64.8 0.7 fusion.23
  65.5 9.8 %custom-call.6 = f32[1,128,128]{1,2,0:T(8,128)S(1)} custom-call(f32[1,128,128]{2,1,0:T(8,128)S(1)} %fusion.23), custom_call_target="InvertDiagBlocksLowerTriangular" | custom-call | tf_op jit(solution)/shard_map/triangular_solve | solution.py:22
  75.8 9.4 %all-to-all-done = bf16[128,8,1024]{2,0,1:T(8,128)(2,1)} async-done(((bf16[128,8,1024]{2,0,1:T(8,128)(2,1)}), bf16[128,8,1024]{2,0,1:T(8,128)(2,1)}, u32[]{:S(2)}, u32[]{:S(2)}) %all-to-all-start) | async-done | bytes 2097184 | tf_op jit(solution)/shard_map/all_to_all | solution.py:106
  85.2 3.9 %copy.46 = bf16[128,8,1024]{0,2,1:T(8,128)(2,1)} copy(bf16[128,8,1024]{2,0,1:T(8,128)(2,1)} %all-to-all-done) | data formatting | bytes 4194304 | tf_op jit(solution)/shard_map/all_to_all | solution.py:106
  89.1 2.4 %fusion.2 = f32[1024,128]{1,0:T(8,128)S(1)} fusion(bf16[128,8,1024]{0,2,1:T(8,128)(2,1)} %copy.46, bf16[8,128,128]{2,1,0:T(8,128)(2,1)S(1)} %gather_fusion, pred[8]{0:T(512)(128)(4,1)S(1)} %compare_and_fusion), kind=kOutput, calls=%fused_computation.4 | convolution fusion | flops 268566528 | bytes 2883592 | tf_op jit(solution)/shard_map/dot_general | solution.py:111
  92.1 1.0 fusion.38
  93.1 1.3 collective-permute-start.8
  94.4 0.8 collective-permute-start.7
  95.7 0.9 collective-permute-done.14
  96.6 1.5 bitcast_dynamic-update-slice_fusion.7
  98.1 1.3 collective-permute-start.15
  99.3 1.5 broadcast_in_dim.41
  100.9 0.7 constant_dynamic-update-slice_fusion.15
  101.6 1.4 collective-permute-start.20
  103.6 1.4 collective-permute-done.15
  105.6 0.6 bitcast_dynamic-update-slice_fusion.6
  106.2 4.9 %collective-permute-done.16 = f32[128,128]{1,0:T(8,128)S(1)} collective-permute-done((f32[128,128]{1,0:T(8,128)S(1)}, f32[128,128]{1,0:T(8,128)S(1)}, u32[]{:S(2)}, u32[]{:S(2)}) %collective-permute-start.16) | collective-permute-done | bytes 65568 | tf_op jit(solution)/shard_map/ppermute | solution.py:82
  111.1 0.7 collective-permute-start.17
  112.4 4.8 %collective-permute-done.17 = f32[128,128]{1,0:T(8,128)S(1)} collective-permute-done((f32[128,128]{1,0:T(8,128)S(1)}, f32[128,128]{1,0:T(8,128)S(1)}, u32[]{:S(2)}, u32[]{:S(2)}) %collective-permute-start.17) | collective-permute-done | bytes 65568 | tf_op jit(solution)/shard_map/ppermute | solution.py:82
  117.2 1.2 collective-permute-start.18
  118.4 0.6 bitcast_dynamic-update-slice_fusion.4
  119.0 3.5 %collective-permute-done.18 = f32[128,128]{1,0:T(8,128)S(1)} collective-permute-done((f32[128,128]{1,0:T(8,128)S(1)}, f32[128,128]{1,0:T(8,128)S(1)}, u32[]{:S(2)}, u32[]{:S(2)}) %collective-permute-start.18) | collective-permute-done | bytes 65568 | tf_op jit(solution)/shard_map/ppermute | solution.py:82
  122.6 0.6 bitcast_dynamic-update-slice_fusion.3
  123.2 0.6 bitcast_dynamic-update-slice_fusion.2
  123.9 0.6 bitcast_dynamic-update-slice_fusion.1
  124.5 2.3 %collective-permute-done.21 = f32[128,128]{1,0:T(8,128)S(1)} collective-permute-done((f32[128,128]{1,0:T(8,128)S(1)}, f32[128,128]{1,0:T(8,128)S(1)}, u32[]{:S(2)}, u32[]{:S(2)}) %collective-permute-start.21) | collective-permute-done | bytes 65568 | tf_op jit(solution)/shard_map/ppermute | solution.py:82
  126.8 0.6 bitcast_dynamic-update-slice_fusion
  127.5 1.6 gather_fusion.1
  129.1 0.8 select_reduce_fusion
  130.5 0.8 fusion.21
  131.3 0.8 fusion.29
  136.6 1.4 fusion.13
  138.4 1.3 subtract_convert_fusion.6
  139.7 1.3 subtract_convert_fusion.5
  141.3 1.8 %collective-permute-start.10 = (bf16[128,1024]{0,1:T(8,128)(2,1)}, bf16[128,1024]{0,1:T(8,128)(2,1)S(1)}, u32[]{:S(2)}, u32[]{:S(2)}) collective-permute-start(bf16[128,1024]{0,1:T(8,128)(2,1)} %collective-permute-done.8), channel_id=1, source_target_pairs={{8,4},{12,8},{14,12},{10,14},{6,10},{2,6},{0,2},{4,0},{9,5},{13,9}... | collective-permute-start | bytes 786440 | tf_op jit(solution)/shard_map/ppermute | solution.py:148
  143.2 0.7 constant_dynamic-update-slice_fusion.14
  143.9 0.7 constant_dynamic-update-slice_fusion.13
  144.6 2.3 %collective-permute-done.9 = bf16[128,1024]{0,1:T(8,128)(2,1)S(1)} collective-permute-done((bf16[128,1024]{0,1:T(8,128)(2,1)}, bf16[128,1024]{0,1:T(8,128)(2,1)S(1)}, u32[]{:S(2)}, u32[]{:S(2)}) %collective-permute-start.9) | collective-permute-done | bytes 262176 | tf_op jit(solution)/shard_map/ppermute | solution.py:145
  147.5 1.5 collective-permute-done.10
  149.0 0.7 copy-done.7
  150.4 1.9 %collective-permute-start.12 = (bf16[128,1024]{0,1:T(8,128)(2,1)}, bf16[128,1024]{0,1:T(8,128)(2,1)S(1)}, u32[]{:S(2)}, u32[]{:S(2)}) collective-permute-start(bf16[128,1024]{0,1:T(8,128)(2,1)} %copy-done.7), channel_id=1, source_target_pairs={{8,4},{12,8},{14,12},{10,14},{6,10},{2,6},{0,2},{4,0},{9,5},{13,9}... | collective-permute-start | bytes 786440 | tf_op jit(solution)/shard_map/ppermute | solution.py:148
  152.3 0.7 constant_dynamic-update-slice_fusion.12
  153.0 0.7 constant_dynamic-update-slice_fusion.11
  153.7 2.4 %collective-permute-done.11 = bf16[128,1024]{0,1:T(8,128)(2,1)S(1)} collective-permute-done((bf16[128,1024]{0,1:T(8,128)(2,1)S(1)}, bf16[128,1024]{0,1:T(8,128)(2,1)S(1)}, u32[]{:S(2)}, u32[]{:S(2)}) %collective-permute-start.11) | collective-permute-done | bytes 262176 | tf_op jit(solution)/shard_map/ppermute | solution.py:145
  156.5 0.7 collective-permute-done.12
  157.8 0.7 constant_dynamic-update-slice_fusion.10
  158.6 0.7 constant_dynamic-update-slice_fusion.9
  159.3 3.2 %collective-permute-done.13 = bf16[128,1024]{0,1:T(8,128)(2,1)S(1)} collective-permute-done((bf16[128,1024]{0,1:T(8,128)(2,1)S(1)}, bf16[128,1024]{0,1:T(8,128)(2,1)S(1)}, u32[]{:S(2)}, u32[]{:S(2)}) %collective-permute-start.13) | collective-permute-done | bytes 262176 | tf_op jit(solution)/shard_map/ppermute | solution.py:145
  163.0 0.7 constant_dynamic-update-slice_fusion.8
  (96 shorter events, 15.1 us)
Async XLA Ops:
  0.6 27.9 %collective-permute-start.6 = (bf16[128,128]{1,0:T(8,128)(2,1)}, bf16[128,128]{1,0:T(8,128)(2,1)S(1)}, u32[]{:S(2)}, u32[]{:S(2)}) collective-permute-start(bf16[128,128]{1,0:T(8,128)(2,1)} %param.6), channel_id=1, source_target_pairs={{0,14},{2,0},{4,2},{6,4},{8,6},{10,8},{12,10},{14,12},{1,15},{3,1}... | collective-permute-start | bytes 98312 | tf_op jit(solution)/shard_map/ppermute | solution.py:82
  6.7 21.8 %collective-permute-start.5 = (bf16[128,128]{1,0:T(8,128)(2,1)}, bf16[128,128]{1,0:T(8,128)(2,1)S(1)}, u32[]{:S(2)}, u32[]{:S(2)}) collective-permute-start(bf16[128,128]{1,0:T(8,128)(2,1)} %param.6), channel_id=1, source_target_pairs={{0,12},{2,14},{4,0},{6,2},{8,4},{10,6},{12,8},{14,10},{1,13},{3,15... | collective-permute-start | bytes 98312 | tf_op jit(solution)/shard_map/ppermute | solution.py:82
  7.1 21.3 %collective-permute-start.4 = (bf16[128,128]{1,0:T(8,128)(2,1)}, bf16[128,128]{1,0:T(8,128)(2,1)S(1)}, u32[]{:S(2)}, u32[]{:S(2)}) collective-permute-start(bf16[128,128]{1,0:T(8,128)(2,1)} %param.6), channel_id=1, source_target_pairs={{0,10},{2,12},{4,14},{6,0},{8,2},{10,4},{12,6},{14,8},{1,11},{3,13... | collective-permute-start | bytes 98312 | tf_op jit(solution)/shard_map/ppermute | solution.py:82
  7.1 21.3 %collective-permute-start.3 = (bf16[128,128]{1,0:T(8,128)(2,1)}, bf16[128,128]{1,0:T(8,128)(2,1)S(1)}, u32[]{:S(2)}, u32[]{:S(2)}) collective-permute-start(bf16[128,128]{1,0:T(8,128)(2,1)} %param.6), channel_id=1, source_target_pairs={{0,8},{2,10},{4,12},{6,14},{8,0},{10,2},{12,4},{14,6},{1,9},{3,11}... | collective-permute-start | bytes 98312 | tf_op jit(solution)/shard_map/ppermute | solution.py:82
  10.1 6.8 %collective-permute-start = (bf16[128,128]{1,0:T(8,128)(2,1)}, bf16[128,128]{1,0:T(8,128)(2,1)S(1)}, u32[]{:S(2)}, u32[]{:S(2)}) collective-permute-start(bf16[128,128]{1,0:T(8,128)(2,1)} %param.6), channel_id=1, source_target_pairs={{0,2},{2,4},{4,6},{6,8},{8,10},{10,12},{12,14},{14,0},{1,3},{3,5},... | collective-permute-start | bytes 98312 | tf_op jit(solution)/shard_map/ppermute | solution.py:82
  11.7 77.5 %copy-start.6 = (pred[8]{0:T(512)(128)(4,1)}, pred[8]{0:T(512)(128)(4,1)S(1)}, u32[]{:S(2)}) copy-start(pred[8]{0:T(512)(128)(4,1)S(1)} %compare_and_fusion) | copy-start | bytes 28
  13.1 3.9 %copy-start = (bf16[128,128]{1,0:T(8,128)(2,1)S(1)}, bf16[128,128]{1,0:T(8,128)(2,1)}, u32[]{:S(2)}) copy-start(bf16[128,128]{1,0:T(8,128)(2,1)} %param.6) | copy-start | bytes 98308
  17.0 5.7 %collective-permute-start.1 = (bf16[128,128]{1,0:T(8,128)(2,1)S(1)}, bf16[128,128]{1,0:T(8,128)(2,1)S(1)}, u32[]{:S(2)}, u32[]{:S(2)}) collective-permute-start(bf16[128,128]{1,0:T(8,128)(2,1)S(1)} %copy-done), channel_id=1, source_target_pairs={{0,4},{2,6},{4,8},{6,10},{8,12},{10,14},{12,0},{14,2},{1,5},{3,7},... | collective-permute-start | bytes 98312 | tf_op jit(solution)/shard_map/ppermute | solution.py:82
  22.7 5.7 %collective-permute-start.2 = (bf16[128,128]{1,0:T(8,128)(2,1)S(1)}, bf16[128,128]{1,0:T(8,128)(2,1)S(1)}, u32[]{:S(2)}, u32[]{:S(2)}) collective-permute-start(bf16[128,128]{1,0:T(8,128)(2,1)S(1)} %copy-done), channel_id=1, source_target_pairs={{0,6},{2,8},{4,10},{6,12},{8,14},{10,0},{12,2},{14,4},{1,7},{3,9},... | collective-permute-start | bytes 98312 | tf_op jit(solution)/shard_map/ppermute | solution.py:82
  36.3 4.5 %copy-start.8 = (s32[8]{0:T(128)S(1)}, s32[8]{0:T(128)}, u32[]{:S(2)}) copy-start(s32[8]{0:T(128)} %constant.188.clone) | copy-start | bytes 100
  36.3 9.8 %copy-start.2 = (s32[8]{0:T(128)S(1)}, s32[8]{0:T(128)}, u32[]{:S(2)}) copy-start(s32[8]{0:T(128)} %constant.187.clone) | copy-start | bytes 100
  36.3 15.0 %copy-start.1 = (f32[8192]{0:T(1024)S(1)}, f32[8192]{0:T(1024)}, u32[]{:S(2)}) copy-start(f32[8192]{0:T(1024)} %param.7) | copy-start | bytes 98308
  36.3 48.9 %all-to-all-start = ((bf16[128,8,1024]{2,0,1:T(8,128)(2,1)}), bf16[128,8,1024]{2,0,1:T(8,128)(2,1)}, u32[]{:S(2)}, u32[]{:S(2)}) async-start(bf16[128,8,1024]{2,0,1:T(8,128)(2,1)} %copy.45), calls=%async_computation | async-start | bytes 4194304 | tf_op jit(solution)/shard_map/all_to_all | solution.py:106
  93.1 46.6 %collective-permute-start.8 = (bf16[128,1024]{0,1:T(8,128)(2,1)S(1)}, bf16[128,1024]{0,1:T(8,128)(2,1)}, u32[]{:S(2)}, u32[]{:S(2)}) collective-permute-start(bf16[128,1024]{0,1:T(8,128)(2,1)S(1)} %convert_bitcast_fusion), channel_id=1, source_target_pairs={{8,4},{12,8},{14,12},{10,14},{6,10},{2,6},{0,2},{4,0},{9,5},{13,9}... | collective-permute-start | bytes 786440 | tf_op jit(solution)/shard_map/ppermute | solution.py:148
  94.4 43.6 %collective-permute-start.7 = (bf16[128,1024]{0,1:T(8,128)(2,1)S(1)}, bf16[128,1024]{0,1:T(8,128)(2,1)}, u32[]{:S(2)}, u32[]{:S(2)}) collective-permute-start(bf16[128,1024]{0,1:T(8,128)(2,1)S(1)} %convert_bitcast_fusion), channel_id=1, source_target_pairs={{4,8},{8,12},{12,14},{14,10},{10,6},{6,2},{2,0},{0,4},{5,9},{9,13}... | collective-permute-start | bytes 786440 | tf_op jit(solution)/shard_map/ppermute | solution.py:145
  95.2 1.4 collective-permute-start.14
  98.1 7.0 %collective-permute-start.15 = (f32[128,128]{1,0:T(8,128)S(1)}, f32[128,128]{1,0:T(8,128)S(1)}, u32[]{:S(2)}, u32[]{:S(2)}) collective-permute-start(f32[128,128]{1,0:T(8,128)S(1)} %get-tuple-element.3), channel_id=1, source_target_pairs={{0,2},{2,4},{4,6},{6,8},{8,10},{10,12},{12,14},{14,0},{1,3},{3,5},... | collective-permute-start | bytes 196616 | tf_op jit(solution)/shard_map/ppermute | solution.py:82
  101.6 22.3 %collective-permute-start.20 = (f32[128,128]{1,0:T(8,128)S(1)}, f32[128,128]{1,0:T(8,128)S(1)}, u32[]{:S(2)}, u32[]{:S(2)}) collective-permute-start(f32[128,128]{1,0:T(8,128)S(1)} %get-tuple-element.3), channel_id=1, source_target_pairs={{0,12},{2,14},{4,0},{6,2},{8,4},{10,6},{12,8},{14,10},{1,13},{3,15... | collective-permute-start | bytes 196616 | tf_op jit(solution)/shard_map/ppermute | solution.py:82
  103.0 20.2 %collective-permute-start.19 = (f32[128,128]{1,0:T(8,128)S(1)}, f32[128,128]{1,0:T(8,128)S(1)}, u32[]{:S(2)}, u32[]{:S(2)}) collective-permute-start(f32[128,128]{1,0:T(8,128)S(1)} %get-tuple-element.3), channel_id=1, source_target_pairs={{0,10},{2,12},{4,14},{6,0},{8,2},{10,4},{12,6},{14,8},{1,11},{3,13... | collective-permute-start | bytes 196616 | tf_op jit(solution)/shard_map/ppermute | solution.py:82
  105.0 6.1 %collective-permute-start.16 = (f32[128,128]{1,0:T(8,128)S(1)}, f32[128,128]{1,0:T(8,128)S(1)}, u32[]{:S(2)}, u32[]{:S(2)}) collective-permute-start(f32[128,128]{1,0:T(8,128)S(1)} %get-tuple-element.3), channel_id=1, source_target_pairs={{0,4},{2,6},{4,8},{6,10},{8,12},{10,14},{12,0},{14,2},{1,5},{3,7},... | collective-permute-start | bytes 196616 | tf_op jit(solution)/shard_map/ppermute | solution.py:82
  111.1 6.1 %collective-permute-start.17 = (f32[128,128]{1,0:T(8,128)S(1)}, f32[128,128]{1,0:T(8,128)S(1)}, u32[]{:S(2)}, u32[]{:S(2)}) collective-permute-start(f32[128,128]{1,0:T(8,128)S(1)} %get-tuple-element.3), channel_id=1, source_target_pairs={{0,6},{2,8},{4,10},{6,12},{8,14},{10,0},{12,2},{14,4},{1,7},{3,9},... | collective-permute-start | bytes 196616 | tf_op jit(solution)/shard_map/ppermute | solution.py:82
  117.2 5.4 %collective-permute-start.18 = (f32[128,128]{1,0:T(8,128)S(1)}, f32[128,128]{1,0:T(8,128)S(1)}, u32[]{:S(2)}, u32[]{:S(2)}) collective-permute-start(f32[128,128]{1,0:T(8,128)S(1)} %get-tuple-element.3), channel_id=1, source_target_pairs={{0,8},{2,10},{4,12},{6,14},{8,0},{10,2},{12,4},{14,6},{1,9},{3,11}... | collective-permute-start | bytes 196616 | tf_op jit(solution)/shard_map/ppermute | solution.py:82
  122.6 4.3 %collective-permute-start.21 = (f32[128,128]{1,0:T(8,128)S(1)}, f32[128,128]{1,0:T(8,128)S(1)}, u32[]{:S(2)}, u32[]{:S(2)}) collective-permute-start(f32[128,128]{1,0:T(8,128)S(1)} %get-tuple-element.3), channel_id=1, source_target_pairs={{0,14},{2,0},{4,2},{6,4},{8,6},{10,8},{12,10},{14,12},{1,15},{3,1}... | collective-permute-start | bytes 196616 | tf_op jit(solution)/shard_map/ppermute | solution.py:82
  133.2 5.1 %copy-start.4 = (f32[1024]{0:T(1024)S(1)}, f32[1024]{0:T(1024)}, u32[]{:S(2)}) copy-start(f32[1024]{0:T(1024)} %get-tuple-element.28) | copy-start | bytes 12292
  133.2 5.1 %copy-start.5 = (f32[1024]{0:T(1024)S(1)}, f32[1024]{0:T(1024)}, u32[]{:S(2)}) copy-start(f32[1024]{0:T(1024)} %get-tuple-element.29) | copy-start | bytes 12292
  134.3 5.4 %copy-start.3 = (f32[1024]{0:T(1024)S(1)}, f32[1024]{0:T(1024)}, u32[]{:S(2)}) copy-start(f32[1024]{0:T(1024)} %get-tuple-element.27) | copy-start | bytes 12292
  138.0 8.9 %collective-permute-start.9 = (bf16[128,1024]{0,1:T(8,128)(2,1)}, bf16[128,1024]{0,1:T(8,128)(2,1)S(1)}, u32[]{:S(2)}, u32[]{:S(2)}) collective-permute-start(bf16[128,1024]{0,1:T(8,128)(2,1)} %collective-permute-done.7), channel_id=1, source_target_pairs={{4,8},{8,12},{12,14},{14,10},{10,6},{6,2},{2,0},{0,4},{5,9},{9,13}... | collective-permute-start | bytes 786440 | tf_op jit(solution)/shard_map/ppermute | solution.py:145
  141.3 7.7 %collective-permute-start.10 = (bf16[128,1024]{0,1:T(8,128)(2,1)}, bf16[128,1024]{0,1:T(8,128)(2,1)S(1)}, u32[]{:S(2)}, u32[]{:S(2)}) collective-permute-start(bf16[128,1024]{0,1:T(8,128)(2,1)} %collective-permute-done.8), channel_id=1, source_target_pairs={{8,4},{12,8},{14,12},{10,14},{6,10},{2,6},{0,2},{4,0},{9,5},{13,9}... | collective-permute-start | bytes 786440 | tf_op jit(solution)/shard_map/ppermute | solution.py:148
  146.9 9.2 %collective-permute-start.11 = (bf16[128,1024]{0,1:T(8,128)(2,1)S(1)}, bf16[128,1024]{0,1:T(8,128)(2,1)S(1)}, u32[]{:S(2)}, u32[]{:S(2)}) collective-permute-start(bf16[128,1024]{0,1:T(8,128)(2,1)S(1)} %collective-permute-done.9), channel_id=1, source_target_pairs={{4,8},{8,12},{12,14},{14,10},{10,6},{6,2},{2,0},{0,4},{5,9},{9,13}... | collective-permute-start | bytes 786440 | tf_op jit(solution)/shard_map/ppermute | solution.py:145
  149.0 0.7 copy-start.7
  150.4 6.8 %collective-permute-start.12 = (bf16[128,1024]{0,1:T(8,128)(2,1)}, bf16[128,1024]{0,1:T(8,128)(2,1)S(1)}, u32[]{:S(2)}, u32[]{:S(2)}) collective-permute-start(bf16[128,1024]{0,1:T(8,128)(2,1)} %copy-done.7), channel_id=1, source_target_pairs={{8,4},{12,8},{14,12},{10,14},{6,10},{2,6},{0,2},{4,0},{9,5},{13,9}... | collective-permute-start | bytes 786440 | tf_op jit(solution)/shard_map/ppermute | solution.py:148
  156.1 6.4 %collective-permute-start.13 = (bf16[128,1024]{0,1:T(8,128)(2,1)S(1)}, bf16[128,1024]{0,1:T(8,128)(2,1)S(1)}, u32[]{:S(2)}, u32[]{:S(2)}) collective-permute-start(bf16[128,1024]{0,1:T(8,128)(2,1)S(1)} %collective-permute-done.11), channel_id=1, source_target_pairs={{4,8},{8,12},{12,14},{14,10},{10,6},{6,2},{2,0},{0,4},{5,9},{9,13}... | collective-permute-start | bytes 786440 | tf_op jit(solution)/shard_map/ppermute | solution.py:145

commit v5 on v3

--- a/solution.py
+++ b/solution.py
@@ -5,6 +5,8 @@
 import jax.numpy as jnp
 from jax import lax
 from jax.sharding import PartitionSpec as P
+from jax.experimental import pallas as pl
+from jax.experimental.pallas import tpu as pltpu
 
 NS_STEPS = 8
 
@@ -100,6 +102,43 @@
     return value
 
 
+def place_kernel(owner_ref, design_ref, level_ref, expression_ref, *rest):
+    block_refs, out_ref = rest[:-1], rest[-1]
+    span = block_refs[0].shape[1]
+    design = design_ref[...]
+    for slot, block_ref in enumerate(block_refs):
+        start = pl.multiple_of(owner_ref[slot] * span, span)
+        columns = pl.ds(start, span)
+        fitted = jnp.dot(design, block_ref[...], preferred_element_type=jnp.float32)
+        slack = expression_ref[:, columns].astype(jnp.float32) - fitted
+        level = level_ref[:, columns]
+        out_ref[:, columns] = (slack - jnp.clip(slack, level - 1.0, level)).astype(out_ref.dtype)
+
+
+def place_blocks(design, blocks, owners, expression, quantile_level):
+    span = blocks[0].shape[1]
+    level = quantile_level.reshape(1, -1)
+    if span % 128:
+        out = jnp.zeros(expression.shape, jnp.bfloat16)
+        for slot, block in enumerate(blocks):
+            start = owners[slot] * span
+            fitted = jnp.dot(design, block, preferred_element_type=jnp.float32)
+            local = lax.dynamic_slice_in_dim(expression, start, span, axis=1).astype(jnp.float32)
+            part = lax.dynamic_slice_in_dim(level, start, span, axis=1)
+            slack = local - fitted
+            piece = (slack - jnp.clip(slack, part - 1.0, part)).astype(jnp.bfloat16)
+            out = lax.dynamic_update_slice_in_dim(out, piece, start, axis=1)
+        return out
+    vmem = pl.BlockSpec(memory_space=pltpu.VMEM)
+    return pl.pallas_call(
+        place_kernel,
+        out_shape=jax.ShapeDtypeStruct(expression.shape, jnp.bfloat16),
+        in_specs=[pl.BlockSpec(memory_space=pltpu.SMEM)] + [vmem] * (3 + len(blocks)),
+        out_specs=vmem,
+        compiler_params=pltpu.CompilerParams(vmem_limit_bytes=48 * 1024 * 1024),
+    )(owners, design, level, expression, *blocks)
+
+
 def per_device(ring, expression, design, quantile_level):
     n = len(ring)
     width = design.shape[1]
@@ -131,25 +170,18 @@
     forward = [(ring[q], ring[(q + 1) % n]) for q in range(n)]
     backward = [(ring[(q + 1) % n], ring[q]) for q in range(n)]
 
-    out = jnp.zeros(expression.shape, jnp.bfloat16)
-
-    def place(out, block, owner):
-        start = owner * span
-        fitted = jnp.dot(design, block, preferred_element_type=jnp.float32)
-        local = lax.dynamic_slice_in_dim(expression, start, span, axis=1).astype(jnp.float32)
-        level = lax.dynamic_slice_in_dim(quantile_level, start, span)[None, :]
-        slack = local - fitted
-        piece = (slack - jnp.clip(slack, level - 1.0, level)).astype(jnp.bfloat16)
-        return lax.dynamic_update_slice_in_dim(out, piece, start, axis=1)
-
-    out = place(out, coef_low_t, me)
+    blocks = [coef_low_t]
+    owners = [me]
     ahead, behind = coef_low_t, coef_low_t
     for step in range(1, n // 2 + 1):
         ahead = lax.ppermute(ahead, "cell", forward)
-        out = place(out, ahead, ring_arr[(pos - step) % n])
+        blocks.append(ahead)
+        owners.append(ring_arr[(pos - step) % n])
         if step <= (n - 1) // 2:
             behind = lax.ppermute(behind, "cell", backward)
-            out = place(out, behind, ring_arr[(pos + step) % n])
+            blocks.append(behind)
+            owners.append(ring_arr[(pos + step) % n])
+    out = place_blocks(design, blocks, jnp.stack(owners).astype(jnp.int32), expression, quantile_level)
     return (out, low_rank_coef)
 
 

time: 130 us -> 135 us (1.038)
  waiting for transfers between devices: 32.2 us -> 50.2 us
  matrix products: 17.1 us -> 10.4 us
  between operations: 11 us -> 6.38 us
  Pallas kernels: 0 us -> 3.01 us
  local copies, waits for them, and re-layouts: 15.9 us -> 13.9 us
  other arithmetic: 27.5 us -> 26 us
    ppermute x4, waiting for transfers between devices: 0.01 us -> 16.2 us  [per_device(): ahead = lax.ppermute(ahead, 'cell', forward)]
    all_to_all x1, waiting for transfers between devices: 10.8 us -> 21.2 us  [per_device(): expression_genes = lax.all_to_all(sent, 'cell', 1, 0, tiled=True)]
    dot_general x8 -> x0, matrix products: 6.72 us -> none  [place(): fitted = jnp.dot(design, block, preferred_element_type=jnp.float32)]
    dynamic_update_slice x8 -> x0, local copies, waits for them, and re-layouts: 5.08 us -> none  [place(): return lax.dynamic_update_slice_in_dim(out, piece, start, axis=1)]
    ppermute x3, waiting for transfers between devices: 4.83 us -> 0.01 us  [per_device(): behind = lax.ppermute(behind, 'cell', backward)]
    another operation x0 -> x1, local copies, waits for them, and re-layouts: none -> 4.46 us  [per_device(): jnp.stack(owners).astype(jnp.int32)]
    ppermute x4, waiting for transfers between devices: 12.2 us -> 8.49 us  [butterfly_sum(): value = value + lax.ppermute(value, axis, pairs)]
    pallas_call x0 -> x1, Pallas kernels: none -> 3.01 us  [place_blocks(): pl.pallas_call(place_kernel, out_shape=jax.ShapeDtypeStruct(expression.sh...]
  transfers between devices with their start and end apart: 15 -> 15, of which waited for: 9 -> 9; matrix products, arithmetic and copies ran while one was open for 38% -> 30% of each run, Pallas kernels for 0% -> 0%
where the time goes in v5:
time: 135 us; the launch traced here: 134 us
  waiting for transfers between devices  50.2 us (37%)
  other arithmetic  26 us (19%)
  starting transfers between devices  24.5 us (18%)
  local copies, waits for them, and re-layouts  13.9 us (10%)
  matrix products  10.4 us (8%)
  between operations  6.38 us (5%)
  Pallas kernels  3.01 us (2%)
    all_to_all x1, waiting for transfers between devices, per_device(): expression_genes = lax.all_to_all(sent, 'cell', 1, 0, tiled=True)  21.2 us
    ppermute x4, waiting for transfers between devices, per_device(): ahead = lax.ppermute(ahead, 'cell', forward)  16.2 us
    another operation x3, other arithmetic, invert(): factor = jnp.linalg.cholesky(matrix)  12.4 us
    another operation x2, other arithmetic, invert(): lax.linalg.triangular_solve(factor, identity, left_side=True, lower=True)  10.4 us
    ppermute x4, waiting for transfers between devices, butterfly_sum(): value = value + lax.ppermute(value, axis, pairs)  8.49 us
    ppermute x3, starting transfers between devices, gather_rows(): other = lax.ppermute(block, axis, pairs)  8.3 us
    dot_general x26, matrix products, matmul(): return jnp.dot(left, right, precision=lax.Precision.HIGHEST)  8.13 us
    all_to_all x1, starting transfers between devices, per_device(): expression_genes = lax.all_to_all(sent, 'cell', 1, 0, tiled=True)  7.13 us
  transfers between devices with their start and end apart: 15, of which 9 were waited for; matrix products, arithmetic and copies ran while one was open for 30% of the time, Pallas kernels for 0%

profile of v5, /device:TPU:0, one launch (start us, length us, event | category | flops | bytes accessed | tf_op | source)
XLA Modules:
  0.0 134.4 jit_solution(1928834280937506917)
XLA Ops:
  0.6 3.0 %collective-permute-start = (bf16[128,128]{1,0:T(8,128)(2,1)}, bf16[128,128]{1,0:T(8,128)(2,1)S(1)}, u32[]{:S(2)}, u32[]{:S(2)}) collective-permute-start(bf16[128,128]{1,0:T(8,128)(2,1)} %design_ref.1), channel_id=1, source_target_pairs={{0,2},{2,0},{4,6},{6,4},{8,10},{10,8},{12,14},{14,12},{1,3},{3,1},... | collective-permute-start | bytes 98312 | tf_op jit(solution)/shard_map/ppermute | solution.py:86
  3.7 2.1 %collective-permute-done = bf16[128,128]{1,0:T(8,128)(2,1)S(1)} collective-permute-done((bf16[128,128]{1,0:T(8,128)(2,1)}, bf16[128,128]{1,0:T(8,128)(2,1)S(1)}, u32[]{:S(2)}, u32[]{:S(2)}) %collective-permute-start) | collective-permute-done | bytes 32800 | tf_op jit(solution)/shard_map/ppermute | solution.py:86
  5.8 0.9 maximum_select_fusion.2
  6.6 2.2 %collective-permute-start.1 = (bf16[256,128]{1,0:T(8,128)(2,1)S(1)}, bf16[256,128]{1,0:T(8,128)(2,1)S(1)}, u32[]{:S(2)}, u32[]{:S(2)}) collective-permute-start(bf16[256,128]{1,0:T(8,128)(2,1)S(1)} %maximum_select_fusion.2), channel_id=1, source_target_pairs={{0,4},{2,6},{4,0},{6,2},{8,12},{10,14},{12,8},{14,10},{1,5},{3,7},... | collective-permute-start | bytes 196616 | tf_op jit(solution)/shard_map/ppermute | solution.py:86
  8.8 2.2 %collective-permute-done.1 = bf16[256,128]{1,0:T(8,128)(2,1)S(1)} collective-permute-done((bf16[256,128]{1,0:T(8,128)(2,1)S(1)}, bf16[256,128]{1,0:T(8,128)(2,1)S(1)}, u32[]{:S(2)}, u32[]{:S(2)}) %collective-permute-start.1) | collective-permute-done | bytes 65568 | tf_op jit(solution)/shard_map/ppermute | solution.py:86
  11.1 3.1 %collective-permute-start.2 = (bf16[512,128]{1,0:T(8,128)(2,1)S(1)}, bf16[512,128]{1,0:T(8,128)(2,1)S(1)}, u32[]{:S(2)}, u32[]{:S(2)}) collective-permute-start(bf16[512,128]{1,0:T(8,128)(2,1)S(1)} %maximum_select_fusion.1), channel_id=1, source_target_pairs={{0,8},{2,10},{4,12},{6,14},{8,0},{10,2},{12,4},{14,6},{1,9},{3,11}... | collective-permute-start | bytes 393224 | tf_op jit(solution)/shard_map/ppermute | solution.py:86
  14.2 3.2 %copy.11 = bf16[128,8192]{0,1:T(8,128)(2,1)S(1)} copy(bf16[128,8192]{1,0:T(8,128)(2,1)} %expression_ref.1) | data formatting | bytes 4194304 | tf_op args[0]
  17.5 0.5 slice.14
  18.7 1.5 %broadcast_add_fusion = bf16[128,8192]{0,1:T(8,128)(2,1)} fusion(bf16[128,8192]{0,1:T(8,128)(2,1)S(1)} %copy.11, bf16[]{:T(256)} %bitcast.9), kind=kLoop, calls=%fused_computation.18 | loop fusion | flops 1048576 | bytes 4194306 | tf_op jit(solution)/shard_map/add | solution.py:148
  20.1 7.1 %all-to-all-start = ((bf16[128,8,1024]{0,2,1:T(8,128)(2,1)}), bf16[128,8,1024]{0,2,1:T(8,128)(2,1)S(1)}, u32[]{:S(2)}, u32[]{:S(2)}) async-start(bf16[128,8,1024]{0,2,1:T(8,128)(2,1)} %bitcast.87), calls=%async_computation | async-start | bytes 4194304 | tf_op jit(solution)/shard_map/all_to_all | solution.py:149
  27.3 0.3 fusion.18
  27.7 11.7 %cholesky.29 = f32[128,128]{1,0:T(8,128)S(1)} custom-call(f32[128,128]{1,0:T(8,128)S(1)} %fusion.13), custom_call_target="Cholesky" | custom-call | tf_op jit(solution)/shard_map/jit(cholesky)/cholesky | solution.py:23
  39.4 0.7 compare_reduce_fusion
  40.1 0.6 fusion.9
  40.8 9.8 %custom-call.6 = f32[1,128,128]{1,2,0:T(8,128)S(1)} custom-call(f32[1,128,128]{2,1,0:T(8,128)S(1)} %fusion.9), custom_call_target="InvertDiagBlocksLowerTriangular" | custom-call | tf_op jit(solution)/shard_map/triangular_solve | solution.py:24
  50.6 0.2 fusion.10
  50.8 0.3 fusion.19
  51.1 21.2 %all-to-all-done = bf16[128,8,1024]{0,2,1:T(8,128)(2,1)S(1)} async-done(((bf16[128,8,1024]{0,2,1:T(8,128)(2,1)}), bf16[128,8,1024]{0,2,1:T(8,128)(2,1)S(1)}, u32[]{:S(2)}, u32[]{:S(2)}) %all-to-all-start) | async-done | bytes 2097184 | tf_op jit(solution)/shard_map/all_to_all | solution.py:149
  72.3 1.3 copy-done.3
  73.6 2.9 %copy.12 = bf16[8,128,1024]{2,1,0:T(8,128)(2,1)S(1)} copy(bf16[8,128,1024]{1,2,0:T(8,128)(2,1)} %bitcast.86) | data formatting | bytes 4194304 | tf_op jit(solution)/shard_map/all_to_all | solution.py:149
  76.5 0.7 fusion.17
  77.2 0.6 fusion.20
  77.8 1.0 fusion.21
  78.9 1.2 collective-permute-done.10
  80.1 1.3 collective-permute-start.11
  81.5 3.0 %collective-permute-done.11 = f32[128,128]{1,0:T(8,128)S(1)} collective-permute-done((f32[128,128]{1,0:T(8,128)S(1)}, f32[128,128]{1,0:T(8,128)S(1)}, u32[]{:S(2)}, u32[]{:S(2)}) %collective-permute-start.11) | collective-permute-done | bytes 65568 | tf_op jit(solution)/shard_map/ppermute | solution.py:100
  84.6 4.3 %collective-permute-done.12 = f32[128,128]{1,0:T(8,128)S(1)} collective-permute-done((f32[128,128]{1,0:T(8,128)S(1)}, f32[128,128]{1,0:T(8,128)S(1)}, u32[]{:S(2)}, u32[]{:S(2)}) %collective-permute-start.12) | collective-permute-done | bytes 65568 | tf_op jit(solution)/shard_map/ppermute | solution.py:100
  88.9 0.6 dynamic_slice.24
  94.2 0.7 fusion.16
  94.9 4.5 %stack.7.owner_ref = s32[8]{0:T(128)S(1)} concatenate(s32[1]{0:T(128)} %bitcast, s32[1]{0:T(128)} %get-tuple-element.9, s32[1]{0:T(128)} %get-tuple-element.8, s32[1]{0:T(128)} %get-tuple-element.7, s32[1]{0:T(128)} %get-tuple-element.6, s32[1]{0:T(128)} %get-tuple-element.5, s32[1]{0:T(128)} %get-tuple-element.10, s32[1]{0:T(128)} %get-tuple-element.4), dimensions={0} | concatenate | bytes 64 | tf_op jit(solution)/shard_map/stack | solution.py:184
  99.5 1.3 collective-permute-start.4
  100.8 0.8 collective-permute-start.3
  101.6 0.6 select_reduce_fusion
  102.2 0.8 fusion.8
  103.1 0.8 fusion.15
  104.1 0.2 fusion.7
  104.3 0.2 fusion.23
  104.5 0.2 fusion.22
  104.7 0.2 fusion.6
  105.0 0.2 fusion.25
  105.2 0.2 fusion.24
  105.4 0.2 fusion.5
  105.6 0.2 fusion.27
  105.8 0.2 fusion.26
  106.0 0.2 fusion.4
  106.3 0.2 fusion.29
  106.5 0.2 fusion.28
  106.7 0.2 fusion.3
  106.9 0.2 fusion.31
  107.1 0.2 fusion.30
  107.3 1.8 %collective-permute-start.5 = (bf16[128,1024]{1,0:T(8,128)(2,1)S(1)}, bf16[128,1024]{1,0:T(8,128)(2,1)S(1)}, u32[]{:S(2)}, u32[]{:S(2)}) collective-permute-start(bf16[128,1024]{1,0:T(8,128)(2,1)S(1)} %collective-permute-done.3.rest_1_), channel_id=1, source_target_pairs={{4,8},{8,12},{12,14},{14,10},{10,6},{6,2},{2,0},{0,4},{5,9},{9,13}... | collective-permute-start | bytes 786440 | tf_op jit(solution)/shard_map/ppermute | solution.py:177
  109.2 0.2 fusion.2
  109.4 0.7 collective-permute-start.6
  110.1 0.2 fusion.32
  110.3 5.4 %collective-permute-done.5.rest_3_ = bf16[128,1024]{1,0:T(8,128)(2,1)S(1)} collective-permute-done((bf16[128,1024]{1,0:T(8,128)(2,1)S(1)}, bf16[128,1024]{1,0:T(8,128)(2,1)S(1)}, u32[]{:S(2)}, u32[]{:S(2)}) %collective-permute-start.5) | collective-permute-done | bytes 262176 | tf_op jit(solution)/shard_map/ppermute | solution.py:177
  115.7 1.3 collective-permute-start.7
  116.9 0.2 fusion.33
  117.1 0.2 fusion.1
  117.3 1.1 collective-permute-start.8
  118.4 6.5 %collective-permute-done.7.rest_5_ = bf16[128,1024]{1,0:T(8,128)(2,1)S(1)} collective-permute-done((bf16[128,1024]{1,0:T(8,128)(2,1)S(1)}, bf16[128,1024]{1,0:T(8,128)(2,1)S(1)}, u32[]{:S(2)}, u32[]{:S(2)}) %collective-permute-start.7) | collective-permute-done | bytes 262176 | tf_op jit(solution)/shard_map/ppermute | solution.py:177
  124.9 0.6 collective-permute-start.9
  125.7 1.4 %fusion = f32[1024,128]{1,0:T(8,128)} fusion(f32[1024,128]{1,0:T(8,128)S(1)} %fusion.20, f32[128,128]{1,0:T(8,128)S(1)} %fusion.34), kind=kOutput, calls=%fused_computation.1 | convolution fusion | flops 201588736 | bytes 1114112 | tf_op jit(solution)/shard_map/dot_general | solution.py:18
  127.1 4.3 %collective-permute-done.9.rest_7_ = bf16[128,1024]{1,0:T(8,128)(2,1)S(1)} collective-permute-done((bf16[128,1024]{1,0:T(8,128)(2,1)S(1)}, bf16[128,1024]{1,0:T(8,128)(2,1)S(1)}, u32[]{:S(2)}, u32[]{:S(2)}) %collective-permute-start.9) | collective-permute-done | bytes 262176 | tf_op jit(solution)/shard_map/ppermute | solution.py:177
  131.4 3.0 %shard_map.68 = bf16[128,8192]{1,0:T(8,128)(2,1)} custom-call(s32[8]{0:T(128)S(1)} %stack.7.owner_ref, bf16[128,128]{1,0:T(8,128)(2,1)S(1)} %copy-done.1, f32[1,8192]{1,0:T(1,128)S(1)} %bitcast.84, bf16[128,8192]{1,0:T(8,128)(2,1)S(1)} %copy-done, bf16[128,1024]{1,0:T(8,128)(2,1)S(1)} %bitcast.83, bf16[128,1024]{1,0:T(8,128)(2,1)S(1)} %collective-permute-done.3.rest_1_, ...), custom_call_target="tpu_custom_call" | custom-call | tf_op jit(solution)/shard_map/pallas_call | solution.py:133
  (31 shorter events, 1.1 us)
Async XLA Ops:
  0.6 5.1 %collective-permute-start = (bf16[128,128]{1,0:T(8,128)(2,1)}, bf16[128,128]{1,0:T(8,128)(2,1)S(1)}, u32[]{:S(2)}, u32[]{:S(2)}) collective-permute-start(bf16[128,128]{1,0:T(8,128)(2,1)} %design_ref.1), channel_id=1, source_target_pairs={{0,2},{2,0},{4,6},{6,4},{8,10},{10,8},{12,14},{14,12},{1,3},{3,1},... | collective-permute-start | bytes 98312 | tf_op jit(solution)/shard_map/ppermute | solution.py:86
  6.6 4.4 %collective-permute-start.1 = (bf16[256,128]{1,0:T(8,128)(2,1)S(1)}, bf16[256,128]{1,0:T(8,128)(2,1)S(1)}, u32[]{:S(2)}, u32[]{:S(2)}) collective-permute-start(bf16[256,128]{1,0:T(8,128)(2,1)S(1)} %maximum_select_fusion.2), channel_id=1, source_target_pairs={{0,4},{2,6},{4,0},{6,2},{8,12},{10,14},{12,8},{14,10},{1,5},{3,7},... | collective-permute-start | bytes 196616 | tf_op jit(solution)/shard_map/ppermute | solution.py:86
  11.1 6.3 %collective-permute-start.2 = (bf16[512,128]{1,0:T(8,128)(2,1)S(1)}, bf16[512,128]{1,0:T(8,128)(2,1)S(1)}, u32[]{:S(2)}, u32[]{:S(2)}) collective-permute-start(bf16[512,128]{1,0:T(8,128)(2,1)S(1)} %maximum_select_fusion.1), channel_id=1, source_target_pairs={{0,8},{2,10},{4,12},{6,14},{8,0},{10,2},{12,4},{14,6},{1,9},{3,11}... | collective-permute-start | bytes 393224 | tf_op jit(solution)/shard_map/ppermute | solution.py:86
  20.1 52.1 %all-to-all-start = ((bf16[128,8,1024]{0,2,1:T(8,128)(2,1)}), bf16[128,8,1024]{0,2,1:T(8,128)(2,1)S(1)}, u32[]{:S(2)}, u32[]{:S(2)}) async-start(bf16[128,8,1024]{0,2,1:T(8,128)(2,1)} %bitcast.87), calls=%async_computation | async-start | bytes 4194304 | tf_op jit(solution)/shard_map/all_to_all | solution.py:149
  72.3 1.3 copy-start.3
  77.2 11.7 %copy-start.5 = (s32[8]{0:T(128)S(1)}, s32[8]{0:T(128)}, u32[]{:S(2)}) copy-start(s32[8]{0:T(128)} %constant.128.clone) | copy-start | bytes 100
  77.2 17.0 %copy-start.4 = (s32[8]{0:T(128)S(1)}, s32[8]{0:T(128)}, u32[]{:S(2)}) copy-start(s32[8]{0:T(128)} %constant.127.clone) | copy-start | bytes 100
  78.8 1.3 collective-permute-start.10
  80.1 4.3 %collective-permute-start.11 = (f32[128,128]{1,0:T(8,128)S(1)}, f32[128,128]{1,0:T(8,128)S(1)}, u32[]{:S(2)}, u32[]{:S(2)}) collective-permute-start(f32[128,128]{1,0:T(8,128)S(1)} %add.133), channel_id=1, source_target_pairs={{0,2},{2,0},{4,6},{6,4},{8,10},{10,8},{12,14},{14,12},{1,3},{3,1},... | collective-permute-start | bytes 196616 | tf_op jit(solution)/shard_map/ppermute | solution.py:100
  84.5 4.3 %collective-permute-start.12 = (f32[128,128]{1,0:T(8,128)S(1)}, f32[128,128]{1,0:T(8,128)S(1)}, u32[]{:S(2)}, u32[]{:S(2)}) collective-permute-start(f32[128,128]{1,0:T(8,128)S(1)} %add.134), channel_id=1, source_target_pairs={{0,4},{2,6},{4,0},{6,2},{8,12},{10,14},{12,8},{14,10},{1,5},{3,7},... | collective-permute-start | bytes 196616 | tf_op jit(solution)/shard_map/ppermute | solution.py:100
  88.8 12.8 %collective-permute-start.13 = (f32[128,128]{1,0:T(8,128)S(1)}, f32[128,128]{1,0:T(8,128)S(1)}, u32[]{:S(2)}, u32[]{:S(2)}) collective-permute-start(f32[128,128]{1,0:T(8,128)S(1)} %add.135), channel_id=1, source_target_pairs={{0,8},{2,10},{4,12},{6,14},{8,0},{10,2},{12,4},{14,6},{1,9},{3,11}... | collective-permute-start | bytes 196616 | tf_op jit(solution)/shard_map/ppermute | solution.py:100
  99.5 9.9 %collective-permute-start.4 = (bf16[128,1024]{1,0:T(8,128)(2,1)S(1)}, bf16[128,1024]{1,0:T(8,128)(2,1)S(1)}, u32[]{:S(2)}, u32[]{:S(2)}) collective-permute-start(bf16[128,1024]{1,0:T(8,128)(2,1)S(1)} %bitcast.81), channel_id=1, source_target_pairs={{8,4},{12,8},{14,12},{10,14},{6,10},{2,6},{0,2},{4,0},{9,5},{13,9}... | collective-permute-start | bytes 786440 | tf_op jit(solution)/shard_map/ppermute | solution.py:181
  100.8 6.5 %collective-permute-start.3 = (bf16[128,1024]{1,0:T(8,128)(2,1)S(1)}, bf16[128,1024]{1,0:T(8,128)(2,1)S(1)}, u32[]{:S(2)}, u32[]{:S(2)}) collective-permute-start(bf16[128,1024]{1,0:T(8,128)(2,1)S(1)} %bitcast.82), channel_id=1, source_target_pairs={{4,8},{8,12},{12,14},{14,10},{10,6},{6,2},{2,0},{0,4},{5,9},{9,13}... | collective-permute-start | bytes 786440 | tf_op jit(solution)/shard_map/ppermute | solution.py:177
  105.0 26.4 %copy-start = (bf16[128,8192]{1,0:T(8,128)(2,1)S(1)}, bf16[128,8192]{1,0:T(8,128)(2,1)}, u32[]{:S(2)}) copy-start(bf16[128,8192]{1,0:T(8,128)(2,1)} %expression_ref.1) | copy-start | bytes 6291460
  105.0 26.4 %copy-start.1 = (bf16[128,128]{1,0:T(8,128)(2,1)S(1)}, bf16[128,128]{1,0:T(8,128)(2,1)}, u32[]{:S(2)}) copy-start(bf16[128,128]{1,0:T(8,128)(2,1)} %design_ref.1) | copy-start | bytes 98308
  105.0 26.4 %copy-start.2 = (f32[8192]{0:T(1024)S(1)}, f32[8192]{0:T(1024)}, u32[]{:S(2)}) copy-start(f32[8192]{0:T(1024)} %param.7) | copy-start | bytes 98308
  107.3 8.3 %collective-permute-start.5 = (bf16[128,1024]{1,0:T(8,128)(2,1)S(1)}, bf16[128,1024]{1,0:T(8,128)(2,1)S(1)}, u32[]{:S(2)}, u32[]{:S(2)}) collective-permute-start(bf16[128,1024]{1,0:T(8,128)(2,1)S(1)} %collective-permute-done.3.rest_1_), channel_id=1, source_target_pairs={{4,8},{8,12},{12,14},{14,10},{10,6},{6,2},{2,0},{0,4},{5,9},{9,13}... | collective-permute-start | bytes 786440 | tf_op jit(solution)/shard_map/ppermute | solution.py:177
  109.4 8.0 %collective-permute-start.6 = (bf16[128,1024]{1,0:T(8,128)(2,1)S(1)}, bf16[128,1024]{1,0:T(8,128)(2,1)S(1)}, u32[]{:S(2)}, u32[]{:S(2)}) collective-permute-start(bf16[128,1024]{1,0:T(8,128)(2,1)S(1)} %collective-permute-done.4.rest_2_), channel_id=1, source_target_pairs={{8,4},{12,8},{14,12},{10,14},{6,10},{2,6},{0,2},{4,0},{9,5},{13,9}... | collective-permute-start | bytes 786440 | tf_op jit(solution)/shard_map/ppermute | solution.py:181
  115.7 9.3 %collective-permute-start.7 = (bf16[128,1024]{1,0:T(8,128)(2,1)S(1)}, bf16[128,1024]{1,0:T(8,128)(2,1)S(1)}, u32[]{:S(2)}, u32[]{:S(2)}) collective-permute-start(bf16[128,1024]{1,0:T(8,128)(2,1)S(1)} %collective-permute-done.5.rest_3_), channel_id=1, source_target_pairs={{4,8},{8,12},{12,14},{14,10},{10,6},{6,2},{2,0},{0,4},{5,9},{9,13}... | collective-permute-start | bytes 786440 | tf_op jit(solution)/shard_map/ppermute | solution.py:177
  117.3 9.7 %collective-permute-start.8 = (bf16[128,1024]{1,0:T(8,128)(2,1)S(1)}, bf16[128,1024]{1,0:T(8,128)(2,1)S(1)}, u32[]{:S(2)}, u32[]{:S(2)}) collective-permute-start(bf16[128,1024]{1,0:T(8,128)(2,1)S(1)} %collective-permute-done.6.rest_4_), channel_id=1, source_target_pairs={{8,4},{12,8},{14,12},{10,14},{6,10},{2,6},{0,2},{4,0},{9,5},{13,9}... | collective-permute-start | bytes 786440 | tf_op jit(solution)/shard_map/ppermute | solution.py:181
  124.9 6.4 %collective-permute-start.9 = (bf16[128,1024]{1,0:T(8,128)(2,1)S(1)}, bf16[128,1024]{1,0:T(8,128)(2,1)S(1)}, u32[]{:S(2)}, u32[]{:S(2)}) collective-permute-start(bf16[128,1024]{1,0:T(8,128)(2,1)S(1)} %collective-permute-done.7.rest_5_), channel_id=1, source_target_pairs={{4,8},{8,12},{12,14},{14,10},{10,6},{6,2},{2,0},{0,4},{5,9},{9,13}... | collective-permute-start | bytes 786440 | tf_op jit(solution)/shard_map/ppermute | solution.py:177

commit v6 on v5

--- a/solution.py
+++ b/solution.py
@@ -158,9 +158,7 @@
     local_moment = lax.dot_general(
         coef, coef, (((0,), (0,)), ((), ())), precision=lax.Precision.HIGHEST
     )
-    moment = butterfly_sum(butterfly_sum(local_moment, "gene"), "cell")
-    root_inv = newton(moment)
-    low_rank_coef = coef - shrink_rate / math.sqrt(width) * matmul(coef, root_inv)
+    chip_moment = butterfly_sum(local_moment, "gene")
     coef_low_t = coef.astype(jnp.bfloat16).T
 
     ring_arr = jnp.array(ring, dtype=jnp.int32)
@@ -170,18 +168,25 @@
     forward = [(ring[q], ring[(q + 1) % n]) for q in range(n)]
     backward = [(ring[(q + 1) % n], ring[q]) for q in range(n)]
 
-    blocks = [coef_low_t]
+    blocks, moments = [coef_low_t], [chip_moment]
     owners = [me]
-    ahead, behind = coef_low_t, coef_low_t
+    ahead = behind = (coef_low_t, chip_moment)
     for step in range(1, n // 2 + 1):
         ahead = lax.ppermute(ahead, "cell", forward)
-        blocks.append(ahead)
+        blocks.append(ahead[0])
+        moments.append(ahead[1])
         owners.append(ring_arr[(pos - step) % n])
         if step <= (n - 1) // 2:
             behind = lax.ppermute(behind, "cell", backward)
-            blocks.append(behind)
+            blocks.append(behind[0])
+            moments.append(behind[1])
             owners.append(ring_arr[(pos + step) % n])
-    out = place_blocks(design, blocks, jnp.stack(owners).astype(jnp.int32), expression, quantile_level)
+    owners = jnp.stack(owners).astype(jnp.int32)
+    slots = jnp.zeros((n,), jnp.int32).at[owners].set(jnp.arange(n, dtype=jnp.int32))
+    moment = jnp.sum(jnp.take(jnp.stack(moments), slots, axis=0), axis=0)
+    root_inv = newton(moment)
+    low_rank_coef = coef - shrink_rate / math.sqrt(width) * matmul(coef, root_inv)
+    out = place_blocks(design, blocks, owners, expression, quantile_level)
     return (out, low_rank_coef)
 
 

time: 135 us -> 131 us (0.970)
  waiting for transfers between devices: 50.2 us -> 35.7 us
  local copies, waits for them, and re-layouts: 13.9 us -> 19.6 us
  starting transfers between devices: 24.5 us -> 28.8 us
    all_to_all x1, waiting for transfers between devices: 21.2 us -> 10.2 us  [per_device(): expression_genes = lax.all_to_all(sent, 'cell', 1, 0, tiled=True)]
    ppermute x4 -> x1, waiting for transfers between devices: 8.49 us -> 0.01 us  [butterfly_sum(): value = value + lax.ppermute(value, axis, pairs)]
    ppermute x3 -> x6, waiting for transfers between devices: 0.01 us -> 8.01 us  [per_device(): behind = lax.ppermute(behind, 'cell', backward)]
    ppermute x3 -> x6, starting transfers between devices: 3.12 us -> 9.2 us  [per_device(): behind = lax.ppermute(behind, 'cell', backward)]
    another operation x1 -> x3, local copies, waits for them, and re-layouts: 4.46 us -> 8.91 us  [the longest x2 8.9 us: per_device(): owners = jnp.stack(owners).astype(jnp.int32)]
    ppermute x4 -> x8, waiting for transfers between devices: 16.2 us -> 13.1 us  [per_device(): ahead = lax.ppermute(ahead, 'cell', forward)]
    ppermute x4 -> x1, starting transfers between devices: 1.55 us -> 0.07 us  [butterfly_sum(): value = value + lax.ppermute(value, axis, pairs)]
    ppermute x4 -> x8, starting transfers between devices: 4.43 us -> 4 us  [per_device(): ahead = lax.ppermute(ahead, 'cell', forward)]
  transfers between devices with their start and end apart: 15 -> 19, of which waited for: 9 -> 11; matrix products, arithmetic and copies ran while one was open for 30% -> 36% of each run, Pallas kernels for 0% -> 0%
where the time goes in v6:
time: 131 us; the launch traced here: 130 us
  waiting for transfers between devices  35.7 us (27%)
  starting transfers between devices  28.8 us (22%)
  other arithmetic  26.1 us (20%)
  local copies, waits for them, and re-layouts  19.6 us (15%)
  matrix products  10.4 us (8%)
  between operations  6.27 us (5%)
  Pallas kernels  3.02 us (2%)
    ppermute x8, waiting for transfers between devices, per_device(): ahead = lax.ppermute(ahead, 'cell', forward)  13.1 us
    another operation x3, other arithmetic, invert(): factor = jnp.linalg.cholesky(matrix)  12.4 us
    another operation x2, other arithmetic, invert(): lax.linalg.triangular_solve(factor, identity, left_side=True, lower=True)  10.4 us
    all_to_all x1, waiting for transfers between devices, per_device(): expression_genes = lax.all_to_all(sent, 'cell', 1, 0, tiled=True)  10.2 us
    ppermute x6, starting transfers between devices, per_device(): behind = lax.ppermute(behind, 'cell', backward)  9.2 us
    another operation x2, local copies, waits for them, and re-layouts, per_device(): owners = jnp.stack(owners).astype(jnp.int32)  8.9 us
    ppermute x3, starting transfers between devices, gather_rows(): other = lax.ppermute(block, axis, pairs)  8.3 us
    dot_general x26, matrix products, matmul(): return jnp.dot(left, right, precision=lax.Precision.HIGHEST)  8.15 us
  transfers between devices with their start and end apart: 19, of which 11 were waited for; matrix products, arithmetic and copies ran while one was open for 36% of the time, Pallas kernels for 0%

profile of v6, /device:TPU:0, one launch (start us, length us, event | category | flops | bytes accessed | tf_op | source)
XLA Modules:
  0.0 129.9 jit_solution(14915632351617271334)
XLA Ops:
  0.6 3.0 %collective-permute-start = (bf16[128,128]{1,0:T(8,128)(2,1)}, bf16[128,128]{1,0:T(8,128)(2,1)S(1)}, u32[]{:S(2)}, u32[]{:S(2)}) collective-permute-start(bf16[128,128]{1,0:T(8,128)(2,1)} %design_ref.1), channel_id=1, source_target_pairs={{0,2},{2,0},{4,6},{6,4},{8,10},{10,8},{12,14},{14,12},{1,3},{3,1},... | collective-permute-start | bytes 98312 | tf_op jit(solution)/shard_map/ppermute | solution.py:86
  3.7 2.1 %collective-permute-done = bf16[128,128]{1,0:T(8,128)(2,1)S(1)} collective-permute-done((bf16[128,128]{1,0:T(8,128)(2,1)}, bf16[128,128]{1,0:T(8,128)(2,1)S(1)}, u32[]{:S(2)}, u32[]{:S(2)}) %collective-permute-start) | collective-permute-done | bytes 32800 | tf_op jit(solution)/shard_map/ppermute | solution.py:86
  5.8 0.9 maximum_select_fusion.2
  6.6 2.2 %collective-permute-start.1 = (bf16[256,128]{1,0:T(8,128)(2,1)S(1)}, bf16[256,128]{1,0:T(8,128)(2,1)S(1)}, u32[]{:S(2)}, u32[]{:S(2)}) collective-permute-start(bf16[256,128]{1,0:T(8,128)(2,1)S(1)} %maximum_select_fusion.2), channel_id=1, source_target_pairs={{0,4},{2,6},{4,0},{6,2},{8,12},{10,14},{12,8},{14,10},{1,5},{3,7},... | collective-permute-start | bytes 196616 | tf_op jit(solution)/shard_map/ppermute | solution.py:86
  8.8 2.2 %collective-permute-done.1 = bf16[256,128]{1,0:T(8,128)(2,1)S(1)} collective-permute-done((bf16[256,128]{1,0:T(8,128)(2,1)S(1)}, bf16[256,128]{1,0:T(8,128)(2,1)S(1)}, u32[]{:S(2)}, u32[]{:S(2)}) %collective-permute-start.1) | collective-permute-done | bytes 65568 | tf_op jit(solution)/shard_map/ppermute | solution.py:86
  11.1 3.1 %collective-permute-start.2 = (bf16[512,128]{1,0:T(8,128)(2,1)S(1)}, bf16[512,128]{1,0:T(8,128)(2,1)S(1)}, u32[]{:S(2)}, u32[]{:S(2)}) collective-permute-start(bf16[512,128]{1,0:T(8,128)(2,1)S(1)} %maximum_select_fusion.1), channel_id=1, source_target_pairs={{0,8},{2,10},{4,12},{6,14},{8,0},{10,2},{12,4},{14,6},{1,9},{3,11}... | collective-permute-start | bytes 393224 | tf_op jit(solution)/shard_map/ppermute | solution.py:86
  14.2 3.2 %copy.11 = bf16[128,8192]{0,1:T(8,128)(2,1)S(1)} copy(bf16[128,8192]{1,0:T(8,128)(2,1)} %expression_ref.1) | data formatting | bytes 4194304 | tf_op args[0]
  17.5 0.5 slice.16
  18.7 1.5 %broadcast_add_fusion = bf16[128,8192]{0,1:T(8,128)(2,1)} fusion(bf16[128,8192]{0,1:T(8,128)(2,1)S(1)} %copy.11, bf16[]{:T(256)} %bitcast.9), kind=kLoop, calls=%fused_computation.20 | loop fusion | flops 1048576 | bytes 4194306 | tf_op jit(solution)/shard_map/add | solution.py:148
  20.1 7.3 %all-to-all-start = ((bf16[128,8,1024]{0,2,1:T(8,128)(2,1)}), bf16[128,8,1024]{0,2,1:T(8,128)(2,1)S(1)}, u32[]{:S(2)}, u32[]{:S(2)}) async-start(bf16[128,8,1024]{0,2,1:T(8,128)(2,1)} %bitcast.113), calls=%async_computation | async-start | bytes 4194304 | tf_op jit(solution)/shard_map/all_to_all | solution.py:149
  27.4 0.6 dynamic_slice.24
  32.6 0.7 fusion.19
  33.3 4.5 %stack.61 = s32[8,1]{0,1:T(1,128)S(1)} concatenate(s32[1,1]{0,1:T(1,128)} %bitcast.17, s32[1,1]{0,1:T(1,128)} %bitcast.18, s32[1,1]{0,1:T(1,128)} %bitcast.19, s32[1,1]{0,1:T(1,128)} %bitcast.20, s32[1,1]{0,1:T(1,128)} %bitcast.21, s32[1,1]{0,1:T(1,128)} %bitcast.22, s32[1,1]{0,1:T(1,128)} %bitcast.23, s32[1,1]{0,1:T(1,128)} %bitcast.24), dimensions={0} | concatenate | bytes 64 | tf_op jit(solution)/shard_map/stack | solution.py:184
  37.8 0.6 scatter_custom_fusion
  38.4 0.3 fusion.21
  38.8 11.7 %cholesky.29 = f32[128,128]{1,0:T(8,128)S(1)} custom-call(f32[128,128]{1,0:T(8,128)S(1)} %fusion.13), custom_call_target="Cholesky" | custom-call | tf_op jit(solution)/shard_map/jit(cholesky)/cholesky | solution.py:23
  50.5 0.7 compare_reduce_fusion
  51.2 0.6 fusion.9
  51.8 9.8 %custom-call.6 = f32[1,128,128]{1,2,0:T(8,128)S(1)} custom-call(f32[1,128,128]{2,1,0:T(8,128)S(1)} %fusion.9), custom_call_target="InvertDiagBlocksLowerTriangular" | custom-call | tf_op jit(solution)/shard_map/triangular_solve | solution.py:24
  61.6 0.2 fusion.10
  61.9 0.3 fusion.22
  62.2 10.2 %all-to-all-done = bf16[128,8,1024]{0,2,1:T(8,128)(2,1)S(1)} async-done(((bf16[128,8,1024]{0,2,1:T(8,128)(2,1)}), bf16[128,8,1024]{0,2,1:T(8,128)(2,1)S(1)}, u32[]{:S(2)}, u32[]{:S(2)}) %all-to-all-start) | async-done | bytes 2097184 | tf_op jit(solution)/shard_map/all_to_all | solution.py:149
  72.4 1.3 %copy-done.3 = bf16[128,8,1024]{0,2,1:T(8,128)(2,1)} copy-done((bf16[128,8,1024]{0,2,1:T(8,128)(2,1)}, bf16[128,8,1024]{0,2,1:T(8,128)(2,1)S(1)}, u32[]{:S(2)}) %copy-start.3) | copy-done | bytes 2097176
  73.7 2.9 %copy.12 = bf16[8,128,1024]{2,1,0:T(8,128)(2,1)S(1)} copy(bf16[8,128,1024]{1,2,0:T(8,128)(2,1)} %bitcast.112) | data formatting | bytes 4194304 | tf_op jit(solution)/shard_map/all_to_all | solution.py:149
  76.6 0.7 fusion.20
  77.3 0.6 fusion.23
  77.9 1.0 fusion.24
  79.0 4.4 %stack.52.owner_ref = s32[8]{0:T(128)S(1)} concatenate(s32[1]{0:T(128)} %bitcast, s32[1]{0:T(128)} %get-tuple-element.9, s32[1]{0:T(128)} %get-tuple-element.8, s32[1]{0:T(128)} %get-tuple-element.7, s32[1]{0:T(128)} %get-tuple-element.6, s32[1]{0:T(128)} %get-tuple-element.5, s32[1]{0:T(128)} %get-tuple-element.10, s32[1]{0:T(128)} %get-tuple-element.4), dimensions={0} | concatenate | bytes 64 | tf_op jit(solution)/shard_map/stack | solution.py:184
  83.7 0.2 collective-permute-start.3
  83.9 1.9 %collective-permute-start.4 = (bf16[128,1024]{1,0:T(8,128)(2,1)S(1)}, bf16[128,1024]{1,0:T(8,128)(2,1)S(1)}, u32[]{:S(2)}, u32[]{:S(2)}) collective-permute-start(bf16[128,1024]{1,0:T(8,128)(2,1)S(1)} %bitcast.108), channel_id=1, source_target_pairs={{8,4},{12,8},{14,12},{10,14},{6,10},{2,6},{0,2},{4,0},{9,5},{13,9}... | collective-permute-start | bytes 786440 | tf_op jit(solution)/shard_map/ppermute | solution.py:180
  85.8 2.0 %collective-permute-start.12 = (f32[128,128]{1,0:T(8,128)S(1)}, f32[128,128]{1,0:T(8,128)S(1)}, u32[]{:S(2)}, u32[]{:S(2)}) collective-permute-start(f32[128,128]{1,0:T(8,128)S(1)} %get-tuple-element.3), channel_id=1, source_target_pairs={{8,4},{12,8},{14,12},{10,14},{6,10},{2,6},{0,2},{4,0},{9,5},{13,9}... | collective-permute-start | bytes 196616 | tf_op jit(solution)/shard_map/ppermute | solution.py:180
  87.8 0.7 collective-permute-done.11
  88.5 5.4 %collective-permute-done.12 = f32[128,128]{1,0:T(8,128)S(1)} collective-permute-done((f32[128,128]{1,0:T(8,128)S(1)}, f32[128,128]{1,0:T(8,128)S(1)}, u32[]{:S(2)}, u32[]{:S(2)}) %collective-permute-start.12) | collective-permute-done | bytes 65568 | tf_op jit(solution)/shard_map/ppermute | solution.py:180
  93.9 1.7 %collective-permute-start.14 = (f32[128,128]{1,0:T(8,128)S(1)}, f32[128,128]{1,0:T(8,128)S(1)}, u32[]{:S(2)}, u32[]{:S(2)}) collective-permute-start(f32[128,128]{1,0:T(8,128)S(1)} %collective-permute-done.12), channel_id=1, source_target_pairs={{8,4},{12,8},{14,12},{10,14},{6,10},{2,6},{0,2},{4,0},{9,5},{13,9}... | collective-permute-start | bytes 196616 | tf_op jit(solution)/shard_map/ppermute | solution.py:180
  95.7 0.4 collective-permute-start.15
  96.0 2.2 %collective-permute-done.14 = f32[128,128]{1,0:T(8,128)S(1)} collective-permute-done((f32[128,128]{1,0:T(8,128)S(1)}, f32[128,128]{1,0:T(8,128)S(1)}, u32[]{:S(2)}, u32[]{:S(2)}) %collective-permute-start.14) | collective-permute-done | bytes 65568 | tf_op jit(solution)/shard_map/ppermute | solution.py:180
  98.2 1.7 %collective-permute-start.16 = (f32[128,128]{1,0:T(8,128)S(1)}, f32[128,128]{1,0:T(8,128)S(1)}, u32[]{:S(2)}, u32[]{:S(2)}) collective-permute-start(f32[128,128]{1,0:T(8,128)S(1)} %collective-permute-done.14), channel_id=1, source_target_pairs={{8,4},{12,8},{14,12},{10,14},{6,10},{2,6},{0,2},{4,0},{9,5},{13,9}... | collective-permute-start | bytes 196616 | tf_op jit(solution)/shard_map/ppermute | solution.py:180
  100.0 0.5 collective-permute-start.17
  100.5 1.8 %collective-permute-start.5 = (bf16[128,1024]{1,0:T(8,128)(2,1)S(1)}, bf16[128,1024]{1,0:T(8,128)(2,1)S(1)}, u32[]{:S(2)}, u32[]{:S(2)}) collective-permute-start(bf16[128,1024]{1,0:T(8,128)(2,1)S(1)} %collective-permute-done.3.rest_1_), channel_id=1, source_target_pairs={{4,8},{8,12},{12,14},{14,10},{10,6},{6,2},{2,0},{0,4},{5,9},{9,13}... | collective-permute-start | bytes 786440 | tf_op jit(solution)/shard_map/ppermute | solution.py:175
  102.3 0.3 collective-permute-start.6
  102.6 0.4 collective-permute-done.16
  103.0 2.0 %collective-permute-done.17 = f32[128,128]{1,0:T(8,128)S(1)} collective-permute-done((f32[128,128]{1,0:T(8,128)S(1)}, f32[128,128]{1,0:T(8,128)S(1)}, u32[]{:S(2)}, u32[]{:S(2)}) %collective-permute-start.17) | collective-permute-done | bytes 65568 | tf_op jit(solution)/shard_map/ppermute | solution.py:175
  105.0 0.6 gather_fusion
  105.7 0.6 select_reduce_fusion.1
  106.3 0.8 fusion.8
  107.2 0.8 fusion.15
  108.2 0.2 fusion.7
  108.4 0.2 fusion.26
  108.6 0.2 fusion.25
  108.8 0.2 fusion.6
  109.5 0.2 fusion.5
  110.2 0.2 fusion.4
  110.8 0.2 fusion.3
  111.0 0.2 fusion.34
  111.2 0.2 fusion.33
  111.4 0.2 fusion.2
  111.9 0.5 collective-permute-start.7
  112.5 0.2 fusion.1
  112.8 1.7 %collective-permute-start.8 = (bf16[128,1024]{1,0:T(8,128)(2,1)S(1)}, bf16[128,1024]{1,0:T(8,128)(2,1)S(1)}, u32[]{:S(2)}, u32[]{:S(2)}) collective-permute-start(bf16[128,1024]{1,0:T(8,128)(2,1)S(1)} %collective-permute-done.6.rest_4_), channel_id=1, source_target_pairs={{8,4},{12,8},{14,12},{10,14},{6,10},{2,6},{0,2},{4,0},{9,5},{13,9}... | collective-permute-start | bytes 786440 | tf_op jit(solution)/shard_map/ppermute | solution.py:180
  114.4 6.1 %collective-permute-done.7.rest_5_ = bf16[128,1024]{1,0:T(8,128)(2,1)S(1)} collective-permute-done((bf16[128,1024]{1,0:T(8,128)(2,1)S(1)}, bf16[128,1024]{1,0:T(8,128)(2,1)S(1)}, u32[]{:S(2)}, u32[]{:S(2)}) %collective-permute-start.7) | collective-permute-done | bytes 262176 | tf_op jit(solution)/shard_map/ppermute | solution.py:175
  120.5 0.6 collective-permute-start.9
  121.3 1.4 %fusion = f32[1024,128]{1,0:T(8,128)} fusion(f32[1024,128]{1,0:T(8,128)S(1)} %fusion.23, f32[128,128]{1,0:T(8,128)S(1)} %fusion.37), kind=kOutput, calls=%fused_computation.3 | convolution fusion | flops 201588736 | bytes 1114112 | tf_op jit(solution)/shard_map/dot_general | solution.py:18
  122.7 4.2 %collective-permute-done.9.rest_7_ = bf16[128,1024]{1,0:T(8,128)(2,1)S(1)} collective-permute-done((bf16[128,1024]{1,0:T(8,128)(2,1)S(1)}, bf16[128,1024]{1,0:T(8,128)(2,1)S(1)}, u32[]{:S(2)}, u32[]{:S(2)}) %collective-permute-start.9) | collective-permute-done | bytes 262176 | tf_op jit(solution)/shard_map/ppermute | solution.py:175
  126.9 3.0 %shard_map.68 = bf16[128,8192]{1,0:T(8,128)(2,1)} custom-call(s32[8]{0:T(128)S(1)} %stack.52.owner_ref, bf16[128,128]{1,0:T(8,128)(2,1)S(1)} %copy-done.1, f32[1,8192]{1,0:T(1,128)S(1)} %bitcast.110, bf16[128,8192]{1,0:T(8,128)(2,1)S(1)} %copy-done, bf16[128,1024]{1,0:T(8,128)(2,1)S(1)} %bitcast.109, bf16[128,1024]{1,0:T(8,128)(2,1)S(1)} %collective-permute-done.3.rest_1_, ...), custom_call_target="tpu_custom_call" | custom-call | tf_op jit(solution)/shard_map/pallas_call | solution.py:133
  (53 shorter events, 2.8 us)
Async XLA Ops:
  0.6 5.1 %collective-permute-start = (bf16[128,128]{1,0:T(8,128)(2,1)}, bf16[128,128]{1,0:T(8,128)(2,1)S(1)}, u32[]{:S(2)}, u32[]{:S(2)}) collective-permute-start(bf16[128,128]{1,0:T(8,128)(2,1)} %design_ref.1), channel_id=1, source_target_pairs={{0,2},{2,0},{4,6},{6,4},{8,10},{10,8},{12,14},{14,12},{1,3},{3,1},... | collective-permute-start | bytes 98312 | tf_op jit(solution)/shard_map/ppermute | solution.py:86
  6.6 4.4 %collective-permute-start.1 = (bf16[256,128]{1,0:T(8,128)(2,1)S(1)}, bf16[256,128]{1,0:T(8,128)(2,1)S(1)}, u32[]{:S(2)}, u32[]{:S(2)}) collective-permute-start(bf16[256,128]{1,0:T(8,128)(2,1)S(1)} %maximum_select_fusion.2), channel_id=1, source_target_pairs={{0,4},{2,6},{4,0},{6,2},{8,12},{10,14},{12,8},{14,10},{1,5},{3,7},... | collective-permute-start | bytes 196616 | tf_op jit(solution)/shard_map/ppermute | solution.py:86
  11.1 6.3 %collective-permute-start.2 = (bf16[512,128]{1,0:T(8,128)(2,1)S(1)}, bf16[512,128]{1,0:T(8,128)(2,1)S(1)}, u32[]{:S(2)}, u32[]{:S(2)}) collective-permute-start(bf16[512,128]{1,0:T(8,128)(2,1)S(1)} %maximum_select_fusion.1), channel_id=1, source_target_pairs={{0,8},{2,10},{4,12},{6,14},{8,0},{10,2},{12,4},{14,6},{1,9},{3,11}... | collective-permute-start | bytes 393224 | tf_op jit(solution)/shard_map/ppermute | solution.py:86
  20.1 7.3 %copy-start.5 = (s32[8]{0:T(128)S(1)}, s32[8]{0:T(128)}, u32[]{:S(2)}) copy-start(s32[8]{0:T(128)} %constant.143.clone) | copy-start | bytes 100
  20.1 12.4 %copy-start.4 = (s32[8]{0:T(128)S(1)}, s32[8]{0:T(128)}, u32[]{:S(2)}) copy-start(s32[8]{0:T(128)} %constant.142.clone) | copy-start | bytes 100
  20.1 52.3 %all-to-all-start = ((bf16[128,8,1024]{0,2,1:T(8,128)(2,1)}), bf16[128,8,1024]{0,2,1:T(8,128)(2,1)S(1)}, u32[]{:S(2)}, u32[]{:S(2)}) async-start(bf16[128,8,1024]{0,2,1:T(8,128)(2,1)} %bitcast.113), calls=%async_computation | async-start | bytes 4194304 | tf_op jit(solution)/shard_map/all_to_all | solution.py:149
  72.4 1.3 %copy-start.3 = (bf16[128,8,1024]{0,2,1:T(8,128)(2,1)}, bf16[128,8,1024]{0,2,1:T(8,128)(2,1)S(1)}, u32[]{:S(2)}) copy-start(bf16[128,8,1024]{0,2,1:T(8,128)(2,1)S(1)} %all-to-all-done) | copy-start | bytes 6291460
  78.9 4.5 %collective-permute-start.10 = (f32[128,128]{1,0:T(8,128)S(1)}, f32[128,128]{1,0:T(8,128)S(1)}, u32[]{:S(2)}, u32[]{:S(2)}) collective-permute-start(f32[128,128]{1,0:T(8,128)S(1)} %fusion.24), channel_id=1, source_target_pairs={{0,1},{1,0},{2,3},{3,2},{4,5},{5,4},{6,7},{7,6},{8,9},{9,8},{10,11... | collective-permute-start | bytes 196616 | tf_op jit(solution)/shard_map/ppermute | solution.py:100
  83.5 5.0 %collective-permute-start.11 = (f32[128,128]{1,0:T(8,128)S(1)}, f32[128,128]{1,0:T(8,128)S(1)}, u32[]{:S(2)}, u32[]{:S(2)}) collective-permute-start(f32[128,128]{1,0:T(8,128)S(1)} %get-tuple-element.3), channel_id=1, source_target_pairs={{4,8},{8,12},{12,14},{14,10},{10,6},{6,2},{2,0},{0,4},{5,9},{9,13}... | collective-permute-start | bytes 196616 | tf_op jit(solution)/shard_map/ppermute | solution.py:175
  83.7 16.8 %collective-permute-start.3 = (bf16[128,1024]{1,0:T(8,128)(2,1)S(1)}, bf16[128,1024]{1,0:T(8,128)(2,1)S(1)}, u32[]{:S(2)}, u32[]{:S(2)}) collective-permute-start(bf16[128,1024]{1,0:T(8,128)(2,1)S(1)} %bitcast.107), channel_id=1, source_target_pairs={{4,8},{8,12},{12,14},{14,10},{10,6},{6,2},{2,0},{0,4},{5,9},{9,13}... | collective-permute-start | bytes 786440 | tf_op jit(solution)/shard_map/ppermute | solution.py:175
  83.9 18.3 %collective-permute-start.4 = (bf16[128,1024]{1,0:T(8,128)(2,1)S(1)}, bf16[128,1024]{1,0:T(8,128)(2,1)S(1)}, u32[]{:S(2)}, u32[]{:S(2)}) collective-permute-start(bf16[128,1024]{1,0:T(8,128)(2,1)S(1)} %bitcast.108), channel_id=1, source_target_pairs={{8,4},{12,8},{14,12},{10,14},{6,10},{2,6},{0,2},{4,0},{9,5},{13,9}... | collective-permute-start | bytes 786440 | tf_op jit(solution)/shard_map/ppermute | solution.py:180
  85.8 8.1 %collective-permute-start.12 = (f32[128,128]{1,0:T(8,128)S(1)}, f32[128,128]{1,0:T(8,128)S(1)}, u32[]{:S(2)}, u32[]{:S(2)}) collective-permute-start(f32[128,128]{1,0:T(8,128)S(1)} %get-tuple-element.3), channel_id=1, source_target_pairs={{8,4},{12,8},{14,12},{10,14},{6,10},{2,6},{0,2},{4,0},{9,5},{13,9}... | collective-permute-start | bytes 196616 | tf_op jit(solution)/shard_map/ppermute | solution.py:180
  88.5 7.2 %collective-permute-start.13 = (f32[128,128]{1,0:T(8,128)S(1)}, f32[128,128]{1,0:T(8,128)S(1)}, u32[]{:S(2)}, u32[]{:S(2)}) collective-permute-start(f32[128,128]{1,0:T(8,128)S(1)} %collective-permute-done.11), channel_id=1, source_target_pairs={{4,8},{8,12},{12,14},{14,10},{10,6},{6,2},{2,0},{0,4},{5,9},{9,13}... | collective-permute-start | bytes 196616 | tf_op jit(solution)/shard_map/ppermute | solution.py:175
  93.9 4.3 %collective-permute-start.14 = (f32[128,128]{1,0:T(8,128)S(1)}, f32[128,128]{1,0:T(8,128)S(1)}, u32[]{:S(2)}, u32[]{:S(2)}) collective-permute-start(f32[128,128]{1,0:T(8,128)S(1)} %collective-permute-done.12), channel_id=1, source_target_pairs={{8,4},{12,8},{14,12},{10,14},{6,10},{2,6},{0,2},{4,0},{9,5},{13,9}... | collective-permute-start | bytes 196616 | tf_op jit(solution)/shard_map/ppermute | solution.py:180
  95.7 4.3 %collective-permute-start.15 = (f32[128,128]{1,0:T(8,128)S(1)}, f32[128,128]{1,0:T(8,128)S(1)}, u32[]{:S(2)}, u32[]{:S(2)}) collective-permute-start(f32[128,128]{1,0:T(8,128)S(1)} %collective-permute-done.13), channel_id=1, source_target_pairs={{4,8},{8,12},{12,14},{14,10},{10,6},{6,2},{2,0},{0,4},{5,9},{9,13}... | collective-permute-start | bytes 196616 | tf_op jit(solution)/shard_map/ppermute | solution.py:175
  98.2 4.8 %collective-permute-start.16 = (f32[128,128]{1,0:T(8,128)S(1)}, f32[128,128]{1,0:T(8,128)S(1)}, u32[]{:S(2)}, u32[]{:S(2)}) collective-permute-start(f32[128,128]{1,0:T(8,128)S(1)} %collective-permute-done.14), channel_id=1, source_target_pairs={{8,4},{12,8},{14,12},{10,14},{6,10},{2,6},{0,2},{4,0},{9,5},{13,9}... | collective-permute-start | bytes 196616 | tf_op jit(solution)/shard_map/ppermute | solution.py:180
  100.0 5.0 %collective-permute-start.17 = (f32[128,128]{1,0:T(8,128)S(1)}, f32[128,128]{1,0:T(8,128)S(1)}, u32[]{:S(2)}, u32[]{:S(2)}) collective-permute-start(f32[128,128]{1,0:T(8,128)S(1)} %collective-permute-done.15), channel_id=1, source_target_pairs={{4,8},{8,12},{12,14},{14,10},{10,6},{6,2},{2,0},{0,4},{5,9},{9,13}... | collective-permute-start | bytes 196616 | tf_op jit(solution)/shard_map/ppermute | solution.py:175
  100.5 11.4 %collective-permute-start.5 = (bf16[128,1024]{1,0:T(8,128)(2,1)S(1)}, bf16[128,1024]{1,0:T(8,128)(2,1)S(1)}, u32[]{:S(2)}, u32[]{:S(2)}) collective-permute-start(bf16[128,1024]{1,0:T(8,128)(2,1)S(1)} %collective-permute-done.3.rest_1_), channel_id=1, source_target_pairs={{4,8},{8,12},{12,14},{14,10},{10,6},{6,2},{2,0},{0,4},{5,9},{9,13}... | collective-permute-start | bytes 786440 | tf_op jit(solution)/shard_map/ppermute | solution.py:175
  102.3 10.5 %collective-permute-start.6 = (bf16[128,1024]{1,0:T(8,128)(2,1)S(1)}, bf16[128,1024]{1,0:T(8,128)(2,1)S(1)}, u32[]{:S(2)}, u32[]{:S(2)}) collective-permute-start(bf16[128,1024]{1,0:T(8,128)(2,1)S(1)} %collective-permute-done.4.rest_2_), channel_id=1, source_target_pairs={{8,4},{12,8},{14,12},{10,14},{6,10},{2,6},{0,2},{4,0},{9,5},{13,9}... | collective-permute-start | bytes 786440 | tf_op jit(solution)/shard_map/ppermute | solution.py:180
  109.1 17.8 %copy-start = (bf16[128,8192]{1,0:T(8,128)(2,1)S(1)}, bf16[128,8192]{1,0:T(8,128)(2,1)}, u32[]{:S(2)}) copy-start(bf16[128,8192]{1,0:T(8,128)(2,1)} %expression_ref.1) | copy-start | bytes 6291460
  109.1 17.8 %copy-start.1 = (bf16[128,128]{1,0:T(8,128)(2,1)S(1)}, bf16[128,128]{1,0:T(8,128)(2,1)}, u32[]{:S(2)}) copy-start(bf16[128,128]{1,0:T(8,128)(2,1)} %design_ref.1) | copy-start | bytes 98308
  109.1 17.8 %copy-start.2 = (f32[8192]{0:T(1024)S(1)}, f32[8192]{0:T(1024)}, u32[]{:S(2)}) copy-start(f32[8192]{0:T(1024)} %param.7) | copy-start | bytes 98308
  111.9 8.7 %collective-permute-start.7 = (bf16[128,1024]{1,0:T(8,128)(2,1)S(1)}, bf16[128,1024]{1,0:T(8,128)(2,1)S(1)}, u32[]{:S(2)}, u32[]{:S(2)}) collective-permute-start(bf16[128,1024]{1,0:T(8,128)(2,1)S(1)} %collective-permute-done.5.rest_3_), channel_id=1, source_target_pairs={{4,8},{8,12},{12,14},{14,10},{10,6},{6,2},{2,0},{0,4},{5,9},{9,13}... | collective-permute-start | bytes 786440 | tf_op jit(solution)/shard_map/ppermute | solution.py:175
  112.8 9.9 %collective-permute-start.8 = (bf16[128,1024]{1,0:T(8,128)(2,1)S(1)}, bf16[128,1024]{1,0:T(8,128)(2,1)S(1)}, u32[]{:S(2)}, u32[]{:S(2)}) collective-permute-start(bf16[128,1024]{1,0:T(8,128)(2,1)S(1)} %collective-permute-done.6.rest_4_), channel_id=1, source_target_pairs={{8,4},{12,8},{14,12},{10,14},{6,10},{2,6},{0,2},{4,0},{9,5},{13,9}... | collective-permute-start | bytes 786440 | tf_op jit(solution)/shard_map/ppermute | solution.py:180
  120.5 6.4 %collective-permute-start.9 = (bf16[128,1024]{1,0:T(8,128)(2,1)S(1)}, bf16[128,1024]{1,0:T(8,128)(2,1)S(1)}, u32[]{:S(2)}, u32[]{:S(2)}) collective-permute-start(bf16[128,1024]{1,0:T(8,128)(2,1)S(1)} %collective-permute-done.7.rest_5_), channel_id=1, source_target_pairs={{4,8},{8,12},{12,14},{14,10},{10,6},{6,2},{2,0},{0,4},{5,9},{9,13}... | collective-permute-start | bytes 786440 | tf_op jit(solution)/shard_map/ppermute | solution.py:175

commit v7 on v6

--- a/solution.py
+++ b/solution.py
@@ -102,12 +102,22 @@
     return value
 
 
-def place_kernel(owner_ref, design_ref, level_ref, expression_ref, *rest):
+def lookup(table, index):
+    value = jnp.int32(table[0])
+    for entry, item in enumerate(table[1:], 1):
+        value = jnp.where(index == entry, jnp.int32(item), value)
+    return value
+
+
+def place_kernel(ring, shifts, design_ref, level_ref, expression_ref, *rest):
     block_refs, out_ref = rest[:-1], rest[-1]
+    n = len(ring)
     span = block_refs[0].shape[1]
+    pos = lookup([ring.index(i) for i in range(n)], lax.axis_index("cell"))
     design = design_ref[...]
-    for slot, block_ref in enumerate(block_refs):
-        start = pl.multiple_of(owner_ref[slot] * span, span)
+    for shift, block_ref in zip(shifts, block_refs):
+        owner = lookup(ring, (pos + shift + n) % n)
+        start = pl.multiple_of(owner * span, span)
         columns = pl.ds(start, span)
         fitted = jnp.dot(design, block_ref[...], preferred_element_type=jnp.float32)
         slack = expression_ref[:, columns].astype(jnp.float32) - fitted
@@ -115,7 +125,7 @@
         out_ref[:, columns] = (slack - jnp.clip(slack, level - 1.0, level)).astype(out_ref.dtype)
 
 
-def place_blocks(design, blocks, owners, expression, quantile_level):
+def place_blocks(ring, shifts, design, blocks, owners, expression, quantile_level):
     span = blocks[0].shape[1]
     level = quantile_level.reshape(1, -1)
     if span % 128:
@@ -131,12 +141,12 @@
         return out
     vmem = pl.BlockSpec(memory_space=pltpu.VMEM)
     return pl.pallas_call(
-        place_kernel,
+        functools.partial(place_kernel, ring, shifts),
         out_shape=jax.ShapeDtypeStruct(expression.shape, jnp.bfloat16),
-        in_specs=[pl.BlockSpec(memory_space=pltpu.SMEM)] + [vmem] * (3 + len(blocks)),
+        in_specs=[vmem] * (3 + len(blocks)),
         out_specs=vmem,
         compiler_params=pltpu.CompilerParams(vmem_limit_bytes=48 * 1024 * 1024),
-    )(owners, design, level, expression, *blocks)
+    )(design, level, expression, *blocks)
 
 
 def per_device(ring, expression, design, quantile_level):
@@ -169,24 +179,32 @@
     backward = [(ring[(q + 1) % n], ring[q]) for q in range(n)]
 
     blocks, moments = [coef_low_t], [chip_moment]
-    owners = [me]
+    owners, shifts = [me], [0]
+
+    def tie(block, moment):
+        block = block + (moment[0, 0] * 0).astype(block.dtype)
+        moment = moment + (block[0, 0] * 0).astype(moment.dtype)
+        return block, moment
+
     ahead = behind = (coef_low_t, chip_moment)
     for step in range(1, n // 2 + 1):
-        ahead = lax.ppermute(ahead, "cell", forward)
+        ahead = tuple(lax.ppermute(tie(*ahead), "cell", forward))
         blocks.append(ahead[0])
         moments.append(ahead[1])
         owners.append(ring_arr[(pos - step) % n])
+        shifts.append(-step)
         if step <= (n - 1) // 2:
-            behind = lax.ppermute(behind, "cell", backward)
+            behind = tuple(lax.ppermute(tie(*behind), "cell", backward))
             blocks.append(behind[0])
             moments.append(behind[1])
             owners.append(ring_arr[(pos + step) % n])
+            shifts.append(step)
     owners = jnp.stack(owners).astype(jnp.int32)
     slots = jnp.zeros((n,), jnp.int32).at[owners].set(jnp.arange(n, dtype=jnp.int32))
     moment = jnp.sum(jnp.take(jnp.stack(moments), slots, axis=0), axis=0)
     root_inv = newton(moment)
     low_rank_coef = coef - shrink_rate / math.sqrt(width) * matmul(coef, root_inv)
-    out = place_blocks(design, blocks, owners, expression, quantile_level)
+    out = place_blocks(ring, shifts, design, blocks, owners, expression, quantile_level)
     return (out, low_rank_coef)
 
 

time: 131 us -> 141 us (1.076)
  waiting for transfers between devices: 35.7 us -> 27.7 us
  local copies, waits for them, and re-layouts: 19.6 us -> 27.6 us
  between operations: 6.27 us -> 14.2 us
  other arithmetic: 26.1 us -> 27.6 us
    ppermute x14, waiting for transfers between devices: 21.1 us -> 12 us  [the longest x8 9.9 us: per_device(): ahead = tuple(lax.ppermute(tie(*ahead), 'cell', forward))]
    slice x0 -> x12, local copies, waits for them, and re-layouts: none -> 6.98 us  [the longest x6 3.91 us: tie(): moment = moment + (block[0, 0] * 0).astype(moment.dtype)]
    another operation x2 -> x1, local copies, waits for them, and re-layouts: 8.9 us -> 4.46 us  [per_device(): owners = jnp.stack(owners).astype(jnp.int32)]
    unnamed x19, local copies, waits for them, and re-layouts: 4.59 us -> 8.37 us
  transfers between devices with their start and end apart: 19 -> 19, of which waited for: 11 -> 9; matrix products, arithmetic and copies ran while one was open for 36% -> 39% of each run, Pallas kernels for 0% -> 0%
where the time goes in v7:
time: 141 us; the launch traced here: 140 us
  starting transfers between devices  30.2 us (21%)
  waiting for transfers between devices  27.7 us (20%)
  other arithmetic  27.6 us (20%)
  local copies, waits for them, and re-layouts  27.6 us (20%)
  between operations  14.2 us (10%)
  matrix products  10.4 us (7%)
  Pallas kernels  2.47 us (2%)
    another operation x3, other arithmetic, invert(): factor = jnp.linalg.cholesky(matrix)  12.4 us
    another operation x2, other arithmetic, invert(): lax.linalg.triangular_solve(factor, identity, left_side=True, lower=True)  10.5 us
    all_to_all x1, waiting for transfers between devices, per_device(): expression_genes = lax.all_to_all(sent, 'cell', 1, 0, tiled=True)  10.2 us
    ppermute x8, waiting for transfers between devices, per_device(): ahead = tuple(lax.ppermute(tie(*ahead), 'cell', forward))  9.9 us
    ppermute x6, starting transfers between devices, per_device(): behind = tuple(lax.ppermute(tie(*behind), 'cell', backward))  9.28 us
    unnamed x19, local copies, waits for them, and re-layouts  8.37 us
    ppermute x3, starting transfers between devices, gather_rows(): other = lax.ppermute(block, axis, pairs)  8.3 us
    dot_general x26, matrix products, matmul(): return jnp.dot(left, right, precision=lax.Precision.HIGHEST)  8.15 us
  transfers between devices with their start and end apart: 19, of which 9 were waited for; matrix products, arithmetic and copies ran while one was open for 39% of the time, Pallas kernels for 0%

profile of v7, /device:TPU:0, one launch (start us, length us, event | category | flops | bytes accessed | tf_op | source)
XLA Modules:
  0.0 140.1 jit_solution(6632458945394737594)
XLA Ops:
  0.6 3.0 %collective-permute-start = (bf16[128,128]{1,0:T(8,128)(2,1)}, bf16[128,128]{1,0:T(8,128)(2,1)S(1)}, u32[]{:S(2)}, u32[]{:S(2)}) collective-permute-start(bf16[128,128]{1,0:T(8,128)(2,1)} %design_ref.1), channel_id=1, source_target_pairs={{0,2},{2,0},{4,6},{6,4},{8,10},{10,8},{12,14},{14,12},{1,3},{3,1},... | collective-permute-start | bytes 98312 | tf_op jit(solution)/shard_map/ppermute | solution.py:86
  3.7 2.1 %collective-permute-done = bf16[128,128]{1,0:T(8,128)(2,1)S(1)} collective-permute-done((bf16[128,128]{1,0:T(8,128)(2,1)}, bf16[128,128]{1,0:T(8,128)(2,1)S(1)}, u32[]{:S(2)}, u32[]{:S(2)}) %collective-permute-start) | collective-permute-done | bytes 32800 | tf_op jit(solution)/shard_map/ppermute | solution.py:86
  5.8 0.9 maximum_select_fusion.2
  6.6 2.2 %collective-permute-start.1 = (bf16[256,128]{1,0:T(8,128)(2,1)S(1)}, bf16[256,128]{1,0:T(8,128)(2,1)S(1)}, u32[]{:S(2)}, u32[]{:S(2)}) collective-permute-start(bf16[256,128]{1,0:T(8,128)(2,1)S(1)} %maximum_select_fusion.2), channel_id=1, source_target_pairs={{0,4},{2,6},{4,0},{6,2},{8,12},{10,14},{12,8},{14,10},{1,5},{3,7},... | collective-permute-start | bytes 196616 | tf_op jit(solution)/shard_map/ppermute | solution.py:86
  8.8 2.2 %collective-permute-done.1 = bf16[256,128]{1,0:T(8,128)(2,1)S(1)} collective-permute-done((bf16[256,128]{1,0:T(8,128)(2,1)S(1)}, bf16[256,128]{1,0:T(8,128)(2,1)S(1)}, u32[]{:S(2)}, u32[]{:S(2)}) %collective-permute-start.1) | collective-permute-done | bytes 65568 | tf_op jit(solution)/shard_map/ppermute | solution.py:86
  11.1 3.1 %collective-permute-start.2 = (bf16[512,128]{1,0:T(8,128)(2,1)S(1)}, bf16[512,128]{1,0:T(8,128)(2,1)S(1)}, u32[]{:S(2)}, u32[]{:S(2)}) collective-permute-start(bf16[512,128]{1,0:T(8,128)(2,1)S(1)} %maximum_select_fusion.1), channel_id=1, source_target_pairs={{0,8},{2,10},{4,12},{6,14},{8,0},{10,2},{12,4},{14,6},{1,9},{3,11}... | collective-permute-start | bytes 393224 | tf_op jit(solution)/shard_map/ppermute | solution.py:86
  14.2 3.2 %copy.11 = bf16[128,8192]{0,1:T(8,128)(2,1)S(1)} copy(bf16[128,8192]{1,0:T(8,128)(2,1)} %expression_ref.1) | data formatting | bytes 4194304 | tf_op args[0]
  17.5 0.5 slice.66
  18.7 1.5 %broadcast_add_fusion = bf16[128,8192]{0,1:T(8,128)(2,1)} fusion(bf16[128,8192]{0,1:T(8,128)(2,1)S(1)} %copy.11, bf16[]{:T(256)} %bitcast.1), kind=kLoop, calls=%fused_computation.20 | loop fusion | flops 1048576 | bytes 4194306 | tf_op jit(solution)/shard_map/add | solution.py:158
  20.1 7.3 %all-to-all-start = ((bf16[128,8,1024]{0,2,1:T(8,128)(2,1)}), bf16[128,8,1024]{0,2,1:T(8,128)(2,1)S(1)}, u32[]{:S(2)}, u32[]{:S(2)}) async-start(bf16[128,8,1024]{0,2,1:T(8,128)(2,1)} %bitcast.130), calls=%async_computation | async-start | bytes 4194304 | tf_op jit(solution)/shard_map/all_to_all | solution.py:159
  27.4 0.6 dynamic_slice.24
  32.6 0.7 fusion.19
  33.3 4.5 %stack.55 = s32[8,1]{0,1:T(1,128)S(1)} concatenate(s32[1,1]{0,1:T(1,128)} %bitcast.19, s32[1,1]{0,1:T(1,128)} %bitcast.21, s32[1,1]{0,1:T(1,128)} %bitcast.23, s32[1,1]{0,1:T(1,128)} %bitcast.25, s32[1,1]{0,1:T(1,128)} %bitcast.27, s32[1,1]{0,1:T(1,128)} %bitcast.29, s32[1,1]{0,1:T(1,128)} %bitcast.31, s32[1,1]{0,1:T(1,128)} %bitcast.33), dimensions={0} | concatenate | bytes 64 | tf_op jit(solution)/shard_map/stack | solution.py:202
  37.8 0.6 scatter_custom_fusion
  38.8 11.7 %cholesky.29 = f32[128,128]{1,0:T(8,128)S(1)} custom-call(f32[128,128]{1,0:T(8,128)S(1)} %fusion.13), custom_call_target="Cholesky" | custom-call | tf_op jit(solution)/shard_map/jit(cholesky)/cholesky | solution.py:23
  50.5 0.6 compare_reduce_fusion
  51.2 0.7 fusion.9
  51.8 9.8 %custom-call.6 = f32[1,128,128]{1,2,0:T(8,128)S(1)} custom-call(f32[1,128,128]{2,1,0:T(8,128)S(1)} %fusion.9), custom_call_target="InvertDiagBlocksLowerTriangular" | custom-call | tf_op jit(solution)/shard_map/triangular_solve | solution.py:24
  62.2 10.2 %all-to-all-done = bf16[128,8,1024]{0,2,1:T(8,128)(2,1)S(1)} async-done(((bf16[128,8,1024]{0,2,1:T(8,128)(2,1)}), bf16[128,8,1024]{0,2,1:T(8,128)(2,1)S(1)}, u32[]{:S(2)}, u32[]{:S(2)}) %all-to-all-start) | async-done | bytes 2097184 | tf_op jit(solution)/shard_map/all_to_all | solution.py:159
  72.4 1.3 copy-done.3
  73.7 2.9 %copy.12 = bf16[8,128,1024]{2,1,0:T(8,128)(2,1)S(1)} copy(bf16[8,128,1024]{1,2,0:T(8,128)(2,1)} %bitcast.129) | data formatting | bytes 4194304 | tf_op jit(solution)/shard_map/all_to_all | solution.py:159
  76.6 0.7 fusion.20
  77.3 0.6 fusion.23
  77.9 1.0 fusion.24
  79.2 1.1 collective-permute-done.3
  80.2 0.6 bitcast_dynamic-update-slice_fusion.7
  82.1 0.5 slice.68
  83.4 2.0 %collective-permute-start.8 = (f32[128,128]{1,0:T(8,128)S(1)}, f32[128,128]{1,0:T(8,128)S(1)}, u32[]{:S(2)}, u32[]{:S(2)}) collective-permute-start(f32[128,128]{1,0:T(8,128)S(1)} %broadcast_add_fusion.12), channel_id=1, source_target_pairs={{8,4},{12,8},{14,12},{10,14},{6,10},{2,6},{0,2},{4,0},{9,5},{13,9}... | collective-permute-start | bytes 196616 | tf_op jit(solution)/shard_map/ppermute | solution.py:197
  85.4 1.3 collective-permute-start.5
  86.6 0.8 collective-permute-start.4
  87.6 0.6 bitcast_dynamic-update-slice_fusion.6
  88.2 0.6 bitcast_dynamic-update-slice_fusion.5
  88.9 0.5 slice.70
  90.0 0.5 slice.69
  91.2 2.1 %collective-permute-done.5.rest_2_ = bf16[128,1024]{1,0:T(8,128)(2,1)S(1)} collective-permute-done((bf16[128,1024]{1,0:T(8,128)(2,1)S(1)}, bf16[128,1024]{1,0:T(8,128)(2,1)S(1)}, u32[]{:S(2)}, u32[]{:S(2)}) %collective-permute-start.5) | collective-permute-done | bytes 262176 | tf_op jit(solution)/shard_map/ppermute | solution.py:197
  93.3 0.6 slice.73
  93.9 1.9 %collective-permute-start.9 = (bf16[128,1024]{1,0:T(8,128)(2,1)S(1)}, bf16[128,1024]{1,0:T(8,128)(2,1)S(1)}, u32[]{:S(2)}, u32[]{:S(2)}) collective-permute-start(bf16[128,1024]{1,0:T(8,128)(2,1)S(1)} %broadcast_add_fusion.4), channel_id=1, source_target_pairs={{8,4},{12,8},{14,12},{10,14},{6,10},{2,6},{0,2},{4,0},{9,5},{13,9}... | collective-permute-start | bytes 786440 | tf_op jit(solution)/shard_map/ppermute | solution.py:197
  95.8 0.5 slice.71
  97.8 0.5 collective-permute-start.10
  98.3 1.7 %collective-permute-start.12 = (f32[128,128]{1,0:T(8,128)S(1)}, f32[128,128]{1,0:T(8,128)S(1)}, u32[]{:S(2)}, u32[]{:S(2)}) collective-permute-start(f32[128,128]{1,0:T(8,128)S(1)} %broadcast_add_fusion.10), channel_id=1, source_target_pairs={{8,4},{12,8},{14,12},{10,14},{6,10},{2,6},{0,2},{4,0},{9,5},{13,9}... | collective-permute-start | bytes 196616 | tf_op jit(solution)/shard_map/ppermute | solution.py:197
  100.0 4.9 %collective-permute-done.10 = f32[128,128]{1,0:T(8,128)S(1)} collective-permute-done((f32[128,128]{1,0:T(8,128)S(1)}, f32[128,128]{1,0:T(8,128)S(1)}, u32[]{:S(2)}, u32[]{:S(2)}) %collective-permute-start.10) | collective-permute-done | bytes 65568 | tf_op jit(solution)/shard_map/ppermute | solution.py:191
  104.9 0.6 bitcast_dynamic-update-slice_fusion.4
  105.6 0.6 bitcast_dynamic-update-slice_fusion.3
  107.4 0.5 slice.72
  108.6 0.6 slice.77
  109.2 0.7 collective-permute-start.13
  109.9 0.5 slice.75
  110.4 1.3 collective-permute-start.11
  113.4 1.7 %collective-permute-start.16 = (f32[128,128]{1,0:T(8,128)S(1)}, f32[128,128]{1,0:T(8,128)S(1)}, u32[]{:S(2)}, u32[]{:S(2)}) collective-permute-start(f32[128,128]{1,0:T(8,128)S(1)} %broadcast_add_fusion.8), channel_id=1, source_target_pairs={{8,4},{12,8},{14,12},{10,14},{6,10},{2,6},{0,2},{4,0},{9,5},{13,9}... | collective-permute-start | bytes 196616 | tf_op jit(solution)/shard_map/ppermute | solution.py:197
  115.1 2.5 %collective-permute-done.14 = f32[128,128]{1,0:T(8,128)S(1)} collective-permute-done((f32[128,128]{1,0:T(8,128)S(1)}, f32[128,128]{1,0:T(8,128)S(1)}, u32[]{:S(2)}, u32[]{:S(2)}) %collective-permute-start.14) | collective-permute-done | bytes 65568 | tf_op jit(solution)/shard_map/ppermute | solution.py:191
  117.6 0.5 slice.76
  118.8 0.6 bitcast_dynamic-update-slice_fusion.2
  119.4 0.7 broadcast_add_fusion.1
  120.1 1.2 slice.78
  122.0 1.7 %collective-permute-start.17 = (f32[128,128]{1,0:T(8,128)S(1)}, f32[128,128]{1,0:T(8,128)S(1)}, u32[]{:S(2)}, u32[]{:S(2)}) collective-permute-start(f32[128,128]{1,0:T(8,128)S(1)} %broadcast_add_fusion.7), channel_id=1, source_target_pairs={{4,8},{8,12},{12,14},{14,10},{10,6},{6,2},{2,0},{0,4},{5,9},{9,13}... | collective-permute-start | bytes 196616 | tf_op jit(solution)/shard_map/ppermute | solution.py:191
  123.7 0.6 bitcast_dynamic-update-slice_fusion.1
  124.7 2.3 %collective-permute-done.17 = f32[128,128]{1,0:T(8,128)S(1)} collective-permute-done((f32[128,128]{1,0:T(8,128)S(1)}, f32[128,128]{1,0:T(8,128)S(1)}, u32[]{:S(2)}, u32[]{:S(2)}) %collective-permute-start.17) | collective-permute-done | bytes 65568 | tf_op jit(solution)/shard_map/ppermute | solution.py:191
  127.0 0.6 bitcast_dynamic-update-slice_fusion
  127.7 1.6 %gather_fusion = f32[8,128,128]{2,1,0:T(8,128)S(1)} fusion(f32[8,128,128]{2,1,0:T(8,128)} %bitcast_dynamic-update-slice_fusion, s32[1024]{0:T(1024)S(1)} %pad_clamp_fusion), kind=kCustom, calls=%fused_computation | custom fusion | bytes 1048608 | tf_op jit(solution)/shard_map/jit(_take)/gather | solution.py:204
  129.4 0.6 select_reduce_fusion.1
  130.0 0.8 fusion.8
  130.9 0.8 fusion.15
  136.2 1.4 fusion
  137.6 2.5 %shard_map.68 = bf16[128,8192]{1,0:T(8,128)(2,1)} custom-call(bf16[128,128]{1,0:T(8,128)(2,1)S(1)} %copy-done.1, f32[1,8192]{1,0:T(1,128)S(1)} %bitcast.127, bf16[128,8192]{1,0:T(8,128)(2,1)S(1)} %copy-done, bf16[128,1024]{1,0:T(8,128)(2,1)S(1)} %bitcast.126, bf16[128,1024]{1,0:T(8,128)(2,1)S(1)} %collective-permute-done.4.rest_1_, ...), custom_call_target="tpu_custom_call" | custom-call | tf_op jit(solution)/shard_map/pallas_call | solution.py:143
  (76 shorter events, 8.1 us)
Async XLA Ops:
  0.6 5.1 %collective-permute-start = (bf16[128,128]{1,0:T(8,128)(2,1)}, bf16[128,128]{1,0:T(8,128)(2,1)S(1)}, u32[]{:S(2)}, u32[]{:S(2)}) collective-permute-start(bf16[128,128]{1,0:T(8,128)(2,1)} %design_ref.1), channel_id=1, source_target_pairs={{0,2},{2,0},{4,6},{6,4},{8,10},{10,8},{12,14},{14,12},{1,3},{3,1},... | collective-permute-start | bytes 98312 | tf_op jit(solution)/shard_map/ppermute | solution.py:86
  6.6 4.4 %collective-permute-start.1 = (bf16[256,128]{1,0:T(8,128)(2,1)S(1)}, bf16[256,128]{1,0:T(8,128)(2,1)S(1)}, u32[]{:S(2)}, u32[]{:S(2)}) collective-permute-start(bf16[256,128]{1,0:T(8,128)(2,1)S(1)} %maximum_select_fusion.2), channel_id=1, source_target_pairs={{0,4},{2,6},{4,0},{6,2},{8,12},{10,14},{12,8},{14,10},{1,5},{3,7},... | collective-permute-start | bytes 196616 | tf_op jit(solution)/shard_map/ppermute | solution.py:86
  11.1 6.3 %collective-permute-start.2 = (bf16[512,128]{1,0:T(8,128)(2,1)S(1)}, bf16[512,128]{1,0:T(8,128)(2,1)S(1)}, u32[]{:S(2)}, u32[]{:S(2)}) collective-permute-start(bf16[512,128]{1,0:T(8,128)(2,1)S(1)} %maximum_select_fusion.1), channel_id=1, source_target_pairs={{0,8},{2,10},{4,12},{6,14},{8,0},{10,2},{12,4},{14,6},{1,9},{3,11}... | collective-permute-start | bytes 393224 | tf_op jit(solution)/shard_map/ppermute | solution.py:86
  20.1 7.3 %copy-start.5 = (s32[8]{0:T(128)S(1)}, s32[8]{0:T(128)}, u32[]{:S(2)}) copy-start(s32[8]{0:T(128)} %constant.156.clone) | copy-start | bytes 100
  20.1 12.4 %copy-start.4 = (s32[8]{0:T(128)S(1)}, s32[8]{0:T(128)}, u32[]{:S(2)}) copy-start(s32[8]{0:T(128)} %constant.155.clone) | copy-start | bytes 100
  20.1 52.3 %all-to-all-start = ((bf16[128,8,1024]{0,2,1:T(8,128)(2,1)}), bf16[128,8,1024]{0,2,1:T(8,128)(2,1)S(1)}, u32[]{:S(2)}, u32[]{:S(2)}) async-start(bf16[128,8,1024]{0,2,1:T(8,128)(2,1)} %bitcast.130), calls=%async_computation | async-start | bytes 4194304 | tf_op jit(solution)/shard_map/all_to_all | solution.py:159
  72.4 1.3 copy-start.3
  78.9 1.3 collective-permute-start.3
  83.3 4.3 %collective-permute-start.6 = (f32[128,128]{1,0:T(8,128)S(1)}, f32[128,128]{1,0:T(8,128)S(1)}, u32[]{:S(2)}, u32[]{:S(2)}) collective-permute-start(f32[128,128]{1,0:T(8,128)S(1)} %broadcast_add_fusion.12), channel_id=1, source_target_pairs={{4,8},{8,12},{12,14},{14,10},{10,6},{6,2},{2,0},{0,4},{5,9},{9,13}... | collective-permute-start | bytes 196616 | tf_op jit(solution)/shard_map/ppermute | solution.py:191
  83.4 4.9 %collective-permute-start.8 = (f32[128,128]{1,0:T(8,128)S(1)}, f32[128,128]{1,0:T(8,128)S(1)}, u32[]{:S(2)}, u32[]{:S(2)}) collective-permute-start(f32[128,128]{1,0:T(8,128)S(1)} %broadcast_add_fusion.12), channel_id=1, source_target_pairs={{8,4},{12,8},{14,12},{10,14},{6,10},{2,6},{0,2},{4,0},{9,5},{13,9}... | collective-permute-start | bytes 196616 | tf_op jit(solution)/shard_map/ppermute | solution.py:197
  85.4 7.9 %collective-permute-start.5 = (bf16[128,1024]{1,0:T(8,128)(2,1)S(1)}, bf16[128,1024]{1,0:T(8,128)(2,1)S(1)}, u32[]{:S(2)}, u32[]{:S(2)}) collective-permute-start(bf16[128,1024]{1,0:T(8,128)(2,1)S(1)} %broadcast_add_fusion.6), channel_id=1, source_target_pairs={{8,4},{12,8},{14,12},{10,14},{6,10},{2,6},{0,2},{4,0},{9,5},{13,9}... | collective-permute-start | bytes 786440 | tf_op jit(solution)/shard_map/ppermute | solution.py:197
  86.6 9.1 %collective-permute-start.4 = (bf16[128,1024]{1,0:T(8,128)(2,1)S(1)}, bf16[128,1024]{1,0:T(8,128)(2,1)S(1)}, u32[]{:S(2)}, u32[]{:S(2)}) collective-permute-start(bf16[128,1024]{1,0:T(8,128)(2,1)S(1)} %broadcast_add_fusion.6), channel_id=1, source_target_pairs={{4,8},{8,12},{12,14},{14,10},{10,6},{6,2},{2,0},{0,4},{5,9},{9,13}... | collective-permute-start | bytes 786440 | tf_op jit(solution)/shard_map/ppermute | solution.py:191
  93.9 14.7 %collective-permute-start.9 = (bf16[128,1024]{1,0:T(8,128)(2,1)S(1)}, bf16[128,1024]{1,0:T(8,128)(2,1)S(1)}, u32[]{:S(2)}, u32[]{:S(2)}) collective-permute-start(bf16[128,1024]{1,0:T(8,128)(2,1)S(1)} %broadcast_add_fusion.4), channel_id=1, source_target_pairs={{8,4},{12,8},{14,12},{10,14},{6,10},{2,6},{0,2},{4,0},{9,5},{13,9}... | collective-permute-start | bytes 786440 | tf_op jit(solution)/shard_map/ppermute | solution.py:197
  96.3 13.6 %collective-permute-start.7 = (bf16[128,1024]{1,0:T(8,128)(2,1)S(1)}, bf16[128,1024]{1,0:T(8,128)(2,1)S(1)}, u32[]{:S(2)}, u32[]{:S(2)}) collective-permute-start(bf16[128,1024]{1,0:T(8,128)(2,1)S(1)} %broadcast_add_fusion.5), channel_id=1, source_target_pairs={{4,8},{8,12},{12,14},{14,10},{10,6},{6,2},{2,0},{0,4},{5,9},{9,13}... | collective-permute-start | bytes 786440 | tf_op jit(solution)/shard_map/ppermute | solution.py:191
  97.8 7.2 %collective-permute-start.10 = (f32[128,128]{1,0:T(8,128)S(1)}, f32[128,128]{1,0:T(8,128)S(1)}, u32[]{:S(2)}, u32[]{:S(2)}) collective-permute-start(f32[128,128]{1,0:T(8,128)S(1)} %broadcast_add_fusion.11), channel_id=1, source_target_pairs={{4,8},{8,12},{12,14},{14,10},{10,6},{6,2},{2,0},{0,4},{5,9},{9,13}... | collective-permute-start | bytes 196616 | tf_op jit(solution)/shard_map/ppermute | solution.py:191
  98.3 7.2 %collective-permute-start.12 = (f32[128,128]{1,0:T(8,128)S(1)}, f32[128,128]{1,0:T(8,128)S(1)}, u32[]{:S(2)}, u32[]{:S(2)}) collective-permute-start(f32[128,128]{1,0:T(8,128)S(1)} %broadcast_add_fusion.10), channel_id=1, source_target_pairs={{8,4},{12,8},{14,12},{10,14},{6,10},{2,6},{0,2},{4,0},{9,5},{13,9}... | collective-permute-start | bytes 196616 | tf_op jit(solution)/shard_map/ppermute | solution.py:197
  109.2 28.4 %collective-permute-start.13 = (bf16[128,1024]{1,0:T(8,128)(2,1)S(1)}, bf16[128,1024]{1,0:T(8,128)(2,1)S(1)}, u32[]{:S(2)}, u32[]{:S(2)}) collective-permute-start(bf16[128,1024]{1,0:T(8,128)(2,1)S(1)} %broadcast_add_fusion.2), channel_id=1, source_target_pairs={{8,4},{12,8},{14,12},{10,14},{6,10},{2,6},{0,2},{4,0},{9,5},{13,9}... | collective-permute-start | bytes 786440 | tf_op jit(solution)/shard_map/ppermute | solution.py:197
  110.4 9.0 %collective-permute-start.11 = (bf16[128,1024]{1,0:T(8,128)(2,1)S(1)}, bf16[128,1024]{1,0:T(8,128)(2,1)S(1)}, u32[]{:S(2)}, u32[]{:S(2)}) collective-permute-start(bf16[128,1024]{1,0:T(8,128)(2,1)S(1)} %broadcast_add_fusion.3), channel_id=1, source_target_pairs={{4,8},{8,12},{12,14},{14,10},{10,6},{6,2},{2,0},{0,4},{5,9},{9,13}... | collective-permute-start | bytes 786440 | tf_op jit(solution)/shard_map/ppermute | solution.py:191
  113.0 4.6 %collective-permute-start.14 = (f32[128,128]{1,0:T(8,128)S(1)}, f32[128,128]{1,0:T(8,128)S(1)}, u32[]{:S(2)}, u32[]{:S(2)}) collective-permute-start(f32[128,128]{1,0:T(8,128)S(1)} %broadcast_add_fusion.9), channel_id=1, source_target_pairs={{4,8},{8,12},{12,14},{14,10},{10,6},{6,2},{2,0},{0,4},{5,9},{9,13}... | collective-permute-start | bytes 196616 | tf_op jit(solution)/shard_map/ppermute | solution.py:191
  113.4 10.3 %collective-permute-start.16 = (f32[128,128]{1,0:T(8,128)S(1)}, f32[128,128]{1,0:T(8,128)S(1)}, u32[]{:S(2)}, u32[]{:S(2)}) collective-permute-start(f32[128,128]{1,0:T(8,128)S(1)} %broadcast_add_fusion.8), channel_id=1, source_target_pairs={{8,4},{12,8},{14,12},{10,14},{6,10},{2,6},{0,2},{4,0},{9,5},{13,9}... | collective-permute-start | bytes 196616 | tf_op jit(solution)/shard_map/ppermute | solution.py:197
  122.0 5.0 %collective-permute-start.17 = (f32[128,128]{1,0:T(8,128)S(1)}, f32[128,128]{1,0:T(8,128)S(1)}, u32[]{:S(2)}, u32[]{:S(2)}) collective-permute-start(f32[128,128]{1,0:T(8,128)S(1)} %broadcast_add_fusion.7), channel_id=1, source_target_pairs={{4,8},{8,12},{12,14},{14,10},{10,6},{6,2},{2,0},{0,4},{5,9},{9,13}... | collective-permute-start | bytes 196616 | tf_op jit(solution)/shard_map/ppermute | solution.py:191
  124.3 13.2 %collective-permute-start.15 = (bf16[128,1024]{1,0:T(8,128)(2,1)}, bf16[128,1024]{1,0:T(8,128)(2,1)S(1)}, u32[]{:S(2)}, u32[]{:S(2)}) collective-permute-start(bf16[128,1024]{1,0:T(8,128)(2,1)} %broadcast_add_fusion.1), channel_id=1, source_target_pairs={{4,8},{8,12},{12,14},{14,10},{10,6},{6,2},{2,0},{0,4},{5,9},{9,13}... | collective-permute-start | bytes 786440 | tf_op jit(solution)/shard_map/ppermute | solution.py:191
  132.8 4.8 %copy-start = (bf16[128,8192]{1,0:T(8,128)(2,1)S(1)}, bf16[128,8192]{1,0:T(8,128)(2,1)}, u32[]{:S(2)}) copy-start(bf16[128,8192]{1,0:T(8,128)(2,1)} %expression_ref.1) | copy-start | bytes 6291460
  132.8 4.8 %copy-start.1 = (bf16[128,128]{1,0:T(8,128)(2,1)S(1)}, bf16[128,128]{1,0:T(8,128)(2,1)}, u32[]{:S(2)}) copy-start(bf16[128,128]{1,0:T(8,128)(2,1)} %design_ref.1) | copy-start | bytes 98308
  132.8 4.8 %copy-start.2 = (f32[8192]{0:T(1024)S(1)}, f32[8192]{0:T(1024)}, u32[]{:S(2)}) copy-start(f32[8192]{0:T(1024)} %param.7) | copy-start | bytes 98308
